TPU v7x, 32 devices: a whole 2x2x4 slice. The times are simulated.
32 devices in a mesh: seq: 8 (over z, y), mp: 4 (over x, core).
Axes of the slice: x: 2, y: 2, z: 4, core: 2. Of those that a mesh axis runs over, the one named last changes fastest.
Arguments:
- query: bfloat16 [3840, 5120], P('seq', 'mp'), may hold values from -32 to 32
- query_gain: float32 [5120], P('mp'), may hold values from 0.25 to 1.75
- cond: bfloat16 [8, 2, 128, 5120], P('seq', None, None, 'mp'), may hold values from -32 to 32
- key_gain: float32 [5120], P('mp'), may hold values from 0.25 to 1.75
- grad_out: bfloat16 [3840, 5120], P('seq', 'mp'), may hold values from -15 to 15
- clip_len: int32 [3], replicated, may hold values from 1 to 1920, 3840 in all
- clip_owner: int32 [3], replicated, may hold values from 0 to 7, as said below
Outputs:
- grad_query: bfloat16 [3840, 5120], P('seq', 'mp')
- grad_cond: bfloat16 [8, 2, 128, 5120], P('seq', None, None, 'mp')
Inputs may be any that keep to these rules, and one draw needn't show every extreme that they name: `clip_len`: the clip lengths sum to 3840, and the longest is exactly 1920. `clip_owner`: the owners of the 3 clips are distinct slots.
All inputs are finite; a program needn't handle non-finite values.
Results may differ from a plain program's by a relative error of at most 0.011.
Values may be sent and summed in bfloat16 or wider, within the bound.
No kernel may reach another device: no remote copies, remote signals or barrier semaphores. Data moves between devices by JAX's collectives and lax.ppermute only.
A program may use at most 128 MiB of HBM per device.

v0:
```python
import math

import jax
import jax.numpy as jnp
from jax import lax
from jax.sharding import PartitionSpec as P

D = 5120
HEAD_DIM = 128


EPS = 1e-06
MASKED = -1e30


def broadcast(value, axis, root):
    mine = lax.axis_index(axis) == root
    return lax.psum(jnp.where(mine, value, jnp.zeros_like(value)), axis)


def attend(query_heads, key_heads, value_heads, grad_heads, allowed, score_scale):
    scores = (
        jnp.einsum("thd,khd->htk", query_heads, key_heads, preferred_element_type=jnp.float32)
        * score_scale
    )
    scores = jnp.where(allowed[None, :, :], scores, MASKED)
    row_max = jnp.max(scores, axis=2, keepdims=True)
    weights = jnp.exp(scores - row_max)
    normed_weights = weights / jnp.sum(weights, axis=2, keepdims=True)
    weights_low = normed_weights.astype(jnp.bfloat16)
    attended = jnp.einsum(
        "htk,khd->thd", weights_low, value_heads, preferred_element_type=jnp.float32
    ).astype(jnp.bfloat16)
    delta = jnp.sum(grad_heads.astype(jnp.float32) * attended.astype(jnp.float32), axis=2)
    grad_weights = jnp.einsum(
        "thd,khd->htk", grad_heads, value_heads, preferred_element_type=jnp.float32
    )
    grad_scores = (
        normed_weights * (grad_weights - jnp.transpose(delta)[:, :, None]) * score_scale
    ).astype(jnp.bfloat16)
    grad_q = jnp.einsum("htk,khd->thd", grad_scores, key_heads, preferred_element_type=jnp.float32)
    grad_k = jnp.einsum(
        "htk,thd->khd", grad_scores, query_heads, preferred_element_type=jnp.float32
    )
    grad_v = jnp.einsum("htk,thd->khd", weights_low, grad_heads, preferred_element_type=jnp.float32)
    return (grad_q, grad_k, grad_v)


def local(query, query_gain, cond, key_gain, grad_out, clip_len, clip_owner):
    tok_rows = query.shape[0]
    feat_width = query.shape[1]
    head_count = feat_width // HEAD_DIM
    clip_count = clip_len.shape[0]
    cond_depth = cond.shape[2]
    my_index = lax.axis_index("seq")
    first_pos = my_index * tok_rows
    position = first_pos + jnp.arange(tok_rows, dtype=jnp.int32)
    starts = jnp.cumsum(clip_len) - clip_len
    clip_of = jnp.sum((position[:, None] >= starts[None, :]).astype(jnp.int32), axis=1) - 1
    query_wide = query.astype(jnp.float32)
    query_sumsq = lax.psum(jnp.sum(query_wide * query_wide, axis=1), "mp")
    query_scale = lax.rsqrt(query_sumsq / D + EPS)
    query_normed = (query_wide * query_scale[:, None] * query_gain).astype(jnp.bfloat16)
    slab_stack = jnp.stack(
        [broadcast(cond[0], "seq", clip_owner[clip_index]) for clip_index in range(clip_count)]
    )
    key_raw = slab_stack[:, 0].astype(jnp.float32)
    key_sumsq = lax.psum(jnp.sum(key_raw * key_raw, axis=2), "mp")
    key_scale = lax.rsqrt(key_sumsq / D + EPS)
    key_normed = (key_raw * key_scale[:, :, None] * key_gain).astype(jnp.bfloat16)
    key_heads = key_normed.reshape(clip_count, cond_depth, head_count, HEAD_DIM)
    value_heads = slab_stack[:, 1].reshape(clip_count, cond_depth, head_count, HEAD_DIM)
    query_heads = query_normed.reshape(tok_rows, head_count, HEAD_DIM)
    grad_heads = grad_out.reshape(tok_rows, head_count, HEAD_DIM)
    score_scale = 1.0 / math.sqrt(HEAD_DIM)
    key_clip = jnp.arange(clip_count * cond_depth, dtype=jnp.int32) // cond_depth
    allowed = clip_of[:, None] == key_clip[None, :]
    grad_query_wide, grad_keys_flat, grad_values_flat = attend(
        query_heads,
        key_heads.reshape(clip_count * cond_depth, head_count, HEAD_DIM),
        value_heads.reshape(clip_count * cond_depth, head_count, HEAD_DIM),
        grad_heads,
        allowed,
        score_scale,
    )
    key_grad = grad_keys_flat.reshape(clip_count, cond_depth, feat_width)
    value_grad = grad_values_flat.reshape(clip_count, cond_depth, feat_width)
    grad_query = grad_query_wide.reshape(tok_rows, feat_width).astype(jnp.bfloat16)
    partial_grads = jnp.stack([key_grad, value_grad], axis=1)
    owner_mask = (clip_owner == my_index).astype(jnp.float32)
    summed = lax.psum(partial_grads, "seq")
    owned_grads = jnp.sum(summed * owner_mask[:, None, None, None], axis=0).astype(jnp.bfloat16)
    return (grad_query, owned_grads[None])


def solution(mesh):
    return jax.shard_map(
        local,
        mesh=mesh,
        in_specs=(
            P("seq", "mp"),
            P("mp"),
            P("seq", None, None, "mp"),
            P("mp"),
            P("seq", "mp"),
            P(),
            P(),
        ),
        out_specs=(P("seq", "mp"), P("seq", None, None, "mp")),
        check_vma=False,
    )
```

profile of v0, /device:TPU:0, one launch (start us, length us, event | category | flops | bytes accessed | tf_op | source)
XLA Modules:
  0.0 390.9 jit_solution(13383794463649991475)
XLA Ops:
  7.2 1.4 fusion.21
  10.6 2.4 broadcast_select_fusion
  13.2 1.7 copy.50
  14.8 1.5 copy.53
  17.1 98.0 %all-reduce.7.cloned.1.call-done = (bf16[1,2,128,1280]{3,2,1,0:T(8,128)(2,1)}, bf16[1,2,128,1280]{3,2,1,0:T(8,128)(2,1)}, bf16[1,2,128,1280]{3,2,1,0:T(8,128)(2,1)}) async-done(((bf16[1,2,128,1280]{3,2,1,0:T(8,128)(2,1)}, bf16[1,2,128,1280]{3,2,1,0:T(8,128)(2,1)}, bf16[1,2,128,1280]{3,2,1,0:T(8,128)(2,1)}), (bf16[1,2,128,1280]{3,2,1,0:T(8,128)(2,1)}, bf16[1,2,128,1280]{3,2,1,0:T(8,128)(2,1)}, ...) | async-done | bytes 1966096 | tf_op jit(solution)/shard_map/psum | solution.py:18
  115.1 1.2 constant_dynamic-update-slice_fusion.2
  116.3 1.1 constant_dynamic-update-slice_fusion.1
  117.7 1.2 fusion.20
  118.9 6.8 %all-reduce = (f32[3,128]{1,0:T(4,128)S(1)}, f32[480]{0:T(512)S(1)}) all-reduce(f32[3,128]{1,0:T(4,128)S(1)} %multiply_reduce_fusion.1, f32[480]{0:T(512)S(1)} %fusion.8), channel_id=1, replica_groups=mesh['seq'=8,'mp'=4] {'mp'}, use_global_device_ids=true, to_apply=%region_4.5 | all-reduce | flops 864 | bytes 6912 | tf_op jit(solution)/shard_map/psum | solution.py:68
  125.7 3.4 copy.49
  129.1 3.7 reshape_reshape_squeeze.3
  132.8 2.7 fusion.10
  135.5 2.4 copy.46
  137.9 2.6 copy.45
  140.6 3.1 reshape.127
  143.7 7.8 %fusion.22 = (f32[10,480]{1,0:T(8,128)S(1)}, f32[10,480,384]{2,1,0:T(8,128)}) fusion(pred[480,384]{1,0:T(8,128)(4,1)S(1)} %broadcast_compare_fusion, bf16[480,10,128]{0,2,1:T(8,128)(2,1)} %bitcast.55, f32[384,10,128]{0,2,1:T(8,128)S(1)} %reshape.127, f32[10,128]{1,0:T(8,128)S(1)} %bitcast.58, f32[384]{0:T(512)S(1)} %rsqrt_bitcast_fusion), kind=kOutput, calls=%fused_computation.56 | convolution fusion | flops 480706944 | bytes 10777856 | tf_op jit(solution)/shard_map/sub | solution.py:28
  151.5 3.6 fusion.7
  155.1 1.9 copy-done.1
  157.0 1.4 convolution_bitcast_fusion
  158.4 1.8 copy.59
  160.2 4.0 %fusion.11 = f32[480,10]{0,1:T(8,128)S(1)} fusion(bf16[480,10,128]{2,0,1:T(8,128)(2,1)} %copy.53, bf16[384,10,128]{0,2,1:T(8,128)(2,1)} %reshape_reshape_squeeze.3, bf16[10,480,384]{2,1,0:T(8,128)(2,1)} %copy-done.1), kind=kOutput, calls=%fused_computation.20 | convolution fusion | flops 474926400 | bytes 5917440 | tf_op jit(solution)/shard_map/htk,khd->thd/dot_general | solution.py:31
  164.2 4.4 %fusion.2 = bf16[10,480,384]{2,1,0:T(8,128)(2,1)S(1)} fusion(f32[10,480]{1,0:T(8,128)S(1)} %bitcast.61, f32[10,480,384]{2,1,0:T(8,128)} %get-tuple-element.22, f32[10,480]{1,0:T(8,128)S(1)} %get-tuple-element.21, bf16[384,10,128]{0,2,1:T(8,128)(2,1)S(1)} %copy-done.6, bf16[480,10,128]{0,2,1:T(8,128)(2,1)S(1)} %bitcast.53), kind=kOutput, calls=%fused_computation.3 | convolution fusion | flops 481075200 | bytes 13309440 | tf_op jit(solution)/shard_map/thd,khd->htk/dot_general | solution.py:35
  168.6 1.9 copy-done
  170.5 2.1 convolution_bitcast_fusion.1
  172.7 2.7 stack_reshape.6
  175.4 4.0 %stack_reshape.7 = f32[3,1,128,1280]{2,0,3,1:T(4,128)} reshape(f32[384,10,128]{0,2,1:T(8,128)} %copy.59) | data formatting | bytes 3932160 | tf_op jit(solution)/shard_map/stack;reshape | solution.py:89
  179.4 5.0 %pad_maximum_fusion = f32[3,2,128,1280]{2,0,3,1:T(4,128)} fusion(f32[3,1,128,1280]{2,0,3,1:T(4,128)} %stack_reshape.7, f32[3,1,128,1280]{2,0,3,1:T(4,128)S(1)} %stack_reshape.6), kind=kLoop, calls=%fused_computation.7 | loop fusion | flops 983040 | bytes 7864320 | tf_op jit(solution)/shard_map/stack | solution.py:89
  186.0 3.2 fusion.12
  189.9 1.5 copy.60
  191.4 176.1 %all-reduce.5.cloned.1.call-done = f32[3,2,128,1280]{2,0,3,1:T(4,128)} async-done(((f32[3,2,128,1280]{2,0,3,1:T(4,128)}), f32[3,2,128,1280]{2,0,3,1:T(4,128)}) %all-reduce.5.cloned.1.call-update) | async-done | bytes 3932176 | tf_op jit(solution)/shard_map/psum | solution.py:91
  367.5 15.5 %multiply_reduce_fusion = bf16[2,128,1280]{1,2,0:T(8,128)(2,1)S(1)} fusion(f32[3,2,128,1280]{2,0,3,1:T(4,128)} %all-reduce.5.cloned.1.call-done, f32[3]{0:T(128)S(1)} %compare_convert_fusion), kind=kLoop, calls=%fused_computation.8 | loop fusion | flops 1638400 | bytes 4587532 | tf_op jit(solution)/shard_map/reduce_sum | solution.py:92
  383.0 1.1 copy.61
  (40 shorter events, 3.4 us)
Async XLA Ops:
  7.2 107.9 %all-reduce.7.cloned.1.call-start = ((), (), s32[]{:S(2)}) async-start(), calls=%async_computation.1 | async-start | bytes 3932160 | tf_op jit(solution)/shard_map/psum | solution.py:18
  13.1 354.4 %all-reduce.5.cloned.1.call-start = ((), (), s32[]{:S(2)}) async-start(), calls=%async_computation | async-start | bytes 10485760 | tf_op jit(solution)/shard_map/psum | solution.py:91
  13.1 3.2 copy-start.11
  13.1 3.5 copy-start.5
  115.1 2.3 copy-start.7
  125.7 7.1 %copy-start.8 = (f32[1280]{0:T(1024)S(1)}, f32[1280]{0:T(1024)}, u32[]{:S(2)}) copy-start(f32[1280]{0:T(1024)} %param.8) | copy-start | bytes 15364
  140.6 3.1 copy-start.9
  143.6 7.9 %copy-start.2 = (f32[384,10,128]{0,2,1:T(8,128)}, f32[384,10,128]{0,2,1:T(8,128)S(1)}, u32[]{:S(2)}) copy-start(f32[384,10,128]{0,2,1:T(8,128)S(1)} %reshape.127) | copy-start | bytes 5898244
  155.1 1.9 copy-start.1
  160.2 4.0 %copy-start.6 = (bf16[384,10,128]{0,2,1:T(8,128)(2,1)S(1)}, bf16[384,10,128]{0,2,1:T(8,128)(2,1)}, u32[]{:S(2)}) copy-start(bf16[384,10,128]{0,2,1:T(8,128)(2,1)} %reshape_reshape_squeeze.3) | copy-start | bytes 2949124
  164.2 6.3 %copy-start.4 = (bf16[480,1280]{0,1:T(8,128)(2,1)S(1)}, bf16[480,1280]{0,1:T(8,128)(2,1)}, u32[]{:S(2)}) copy-start(bf16[480,1280]{0,1:T(8,128)(2,1)} %copy.46) | copy-start | bytes 3686404
  168.6 1.9 copy-start
  184.5 0.7 copy-start.10
  184.5 1.6 copy-start.3
Sparse Core Ops, SparseCore 0:
  13.2 101.8 all-reduce.6
  184.6 182.7 all-reduce.4
where the time goes:
time: 392 us; the launch traced here: 391 us
  waiting for transfers between devices  274 us (70%)
  local copies, waits for them, and re-layouts  39.3 us (10%)
  other arithmetic  31.4 us (8%)
  matrix products  23 us (6%)
  between operations  16.2 us (4%)
  blocking collectives  6.81 us (2%)
    psum x1, waiting for transfers between devices, local(): summed = lax.psum(partial_grads, 'seq')  176 us
    psum x1, waiting for transfers between devices, broadcast(): return lax.psum(jnp.where(mine, value, jnp.zeros_like(value)), axis)  98 us
    reduce_sum x1, other arithmetic, local(): jnp.sum(summed * owner_mask[:, None, None, None], axis=0)  15.5 us
    unnamed x29, local copies, waits for them, and re-layouts  12 us
    sub x1, matrix products, attend(): weights = jnp.exp(scores - row_max)  7.85 us
  transfers between devices with their start and end apart: 2, of which 2 were waited for; matrix products, arithmetic and copies ran while one was open for 2% of the time, Pallas kernels for 0%

commit v1 on v0

v1 whole, which is shorter than its diff:
```python
import math

import jax
import jax.numpy as jnp
from jax import lax
from jax.experimental import pallas as pl
from jax.experimental.pallas import tpu as pltpu
from jax.sharding import PartitionSpec as P

D = 5120
HEAD_DIM = 128


EPS = 1e-06
MASKED = -1e30


def attend_kernel(tok_clip_ref, key_clip_ref, q_ref, k_ref, v_ref, g_ref, dq_ref, dk_ref, dv_ref):
    score_scale = 1.0 / math.sqrt(HEAD_DIM)
    q = q_ref[...]
    k = k_ref[...]
    v = v_ref[...]
    g = g_ref[...]
    allowed = tok_clip_ref[...] == key_clip_ref[...]
    nt = (((1,), (1,)), ((), ()))
    tn = (((0,), (0,)), ((), ()))
    scores = lax.dot_general(q, k, nt, preferred_element_type=jnp.float32) * score_scale
    scores = jnp.where(allowed, scores, MASKED)
    row_max = jnp.max(scores, axis=1, keepdims=True)
    weights = jnp.exp(scores - row_max)
    normed = weights / jnp.sum(weights, axis=1, keepdims=True)
    weights_low = normed.astype(jnp.bfloat16)
    attended = jnp.dot(weights_low, v, preferred_element_type=jnp.float32).astype(jnp.bfloat16)
    delta = jnp.sum(g.astype(jnp.float32) * attended.astype(jnp.float32), axis=1, keepdims=True)
    grad_weights = lax.dot_general(g, v, nt, preferred_element_type=jnp.float32)
    grad_scores = (normed * (grad_weights - delta) * score_scale).astype(jnp.bfloat16)
    dq_ref[...] = jnp.dot(grad_scores, k, preferred_element_type=jnp.float32).astype(dq_ref.dtype)
    dk_ref[...] = lax.dot_general(grad_scores, q, tn, preferred_element_type=jnp.float32)
    dv_ref[...] = lax.dot_general(weights_low, g, tn, preferred_element_type=jnp.float32)


def attend(tok_clip, key_clip, query_normed, keys, values, grad_out):
    tok_rows, feat_width = query_normed.shape
    key_rows = keys.shape[0]
    head_count = feat_width // HEAD_DIM
    tok_spec = pl.BlockSpec((tok_rows, HEAD_DIM), lambda h: (0, h))
    key_spec = pl.BlockSpec((key_rows, HEAD_DIM), lambda h: (0, h))
    return pl.pallas_call(
        attend_kernel,
        grid=(head_count,),
        in_specs=[
            pl.BlockSpec((tok_rows, 1), lambda h: (0, 0)),
            pl.BlockSpec((1, key_rows), lambda h: (0, 0)),
            tok_spec,
            key_spec,
            key_spec,
            tok_spec,
        ],
        out_specs=[tok_spec, key_spec, key_spec],
        out_shape=[
            jax.ShapeDtypeStruct((tok_rows, feat_width), jnp.bfloat16),
            jax.ShapeDtypeStruct((key_rows, feat_width), jnp.float32),
            jax.ShapeDtypeStruct((key_rows, feat_width), jnp.float32),
        ],
        compiler_params=pltpu.CompilerParams(dimension_semantics=("arbitrary",)),
    )(tok_clip, key_clip, query_normed, keys, values, grad_out)


def local(query, query_gain, cond, key_gain, grad_out, clip_len, clip_owner):
    tok_rows = query.shape[0]
    clip_count = clip_len.shape[0]
    cond_depth = cond.shape[2]
    my_index = lax.axis_index("seq")
    first_pos = my_index * tok_rows
    position = first_pos + jnp.arange(tok_rows, dtype=jnp.int32)
    starts = jnp.cumsum(clip_len) - clip_len
    clip_of = jnp.sum((position[:, None] >= starts[None, :]).astype(jnp.int32), axis=1) - 1
    query_wide = query.astype(jnp.float32)
    own_key = cond[0, 0].astype(jnp.float32)
    sums = lax.psum(
        (jnp.sum(query_wide * query_wide, axis=1), jnp.sum(own_key * own_key, axis=1)), "mp"
    )
    query_scale = lax.rsqrt(sums[0] / D + EPS)
    query_normed = (query_wide * query_scale[:, None] * query_gain).astype(jnp.bfloat16)
    key_scale = lax.rsqrt(sums[1] / D + EPS)
    own_key_normed = (own_key * key_scale[:, None] * key_gain).astype(jnp.bfloat16)
    own_slab = jnp.stack([own_key_normed, cond[0, 1]])
    owned = clip_owner == my_index
    slabs = lax.psum(
        jnp.where(owned[:, None, None, None], own_slab[None], jnp.zeros_like(own_slab)[None]),
        "seq",
    )
    first_clip = clip_of[0]
    second_clip = first_clip + 1
    second_index = jnp.minimum(second_clip, clip_count - 1)
    slab_a = lax.dynamic_index_in_dim(slabs, first_clip, 0, keepdims=False)
    slab_b = lax.dynamic_index_in_dim(slabs, second_index, 0, keepdims=False)
    keys = jnp.concatenate([slab_a[0], slab_b[0]], axis=0)
    values = jnp.concatenate([slab_a[1], slab_b[1]], axis=0)
    key_clip = jnp.concatenate(
        [jnp.full((cond_depth,), first_clip, jnp.int32), jnp.full((cond_depth,), second_clip, jnp.int32)]
    )
    grad_query, key_grad, value_grad = attend(
        clip_of[:, None], key_clip[None, :], query_normed, keys, values, grad_out
    )
    part_a = jnp.stack([key_grad[:cond_depth], value_grad[:cond_depth]])
    part_b = jnp.stack([key_grad[cond_depth:], value_grad[cond_depth:]])
    clip_ids = jnp.arange(clip_count, dtype=jnp.int32)[:, None, None, None]
    partial_grads = jnp.where(clip_ids == first_clip, part_a[None], 0.0) + jnp.where(
        clip_ids == second_clip, part_b[None], 0.0
    )
    summed = lax.psum(partial_grads, "seq")
    my_clip = jnp.sum(jnp.where(owned, jnp.arange(clip_count, dtype=jnp.int32), 0))
    mine = lax.dynamic_index_in_dim(summed, my_clip, 0, keepdims=False)
    owned_grads = jnp.where(jnp.any(owned), mine, 0.0).astype(jnp.bfloat16)
    return (grad_query, owned_grads[None])


def solution(mesh):
    return jax.shard_map(
        local,
        mesh=mesh,
        in_specs=(
            P("seq", "mp"),
            P("mp"),
            P("seq", None, None, "mp"),
            P("mp"),
            P("seq", "mp"),
            P(),
            P(),
        ),
        out_specs=(P("seq", "mp"), P("seq", None, None, "mp")),
        check_vma=False,
    )
```

time: 392 us -> 308 us (0.79)
  waiting for transfers between devices: 274 us -> 88 us
  blocking collectives: 6.81 us -> 165 us
  local copies, waits for them, and re-layouts: 39.3 us -> 7.38 us
  matrix products: 23 us -> 0 us
  other arithmetic: 31.4 us -> 13.4 us
  Pallas kernels: 0 us -> 14.8 us
    psum x2 -> x1, waiting for transfers between devices: 274 us -> 88 us  [local(): lax.psum(jnp.where(owned[:, None, None, None], own_slab[None], jnp.zeros_...]
    psum x1 -> x2, blocking collectives: 6.81 us -> 165 us  [the longest x1 157 us: local(): summed = lax.psum(partial_grads, 'seq')]
    dot_general x5 -> x0, matrix products: 15.1 us -> none  [the longest x1 4.37 us: attend(): jnp.einsum('thd,khd->htk', grad_heads, value_heads, preferred_element_typ...]
    pallas_call x0 -> x1, Pallas kernels: none -> 14.8 us  [attend(): pl.pallas_call(attend_kernel, grid=(head_count,), in_specs=[pl.BlockSpec(...]
    reduce_sum x3, other arithmetic: 16.1 us -> 3.41 us  [the longest x1 1.6 us: local(): jnp.sum(query_wide * query_wide, axis=1)]
    unnamed x29 -> x14, local copies, waits for them, and re-layouts: 12 us -> 0.88 us
    convert_element_type x4 -> x0, local copies, waits for them, and re-layouts: 8.73 us -> none  [the longest x2 5.7 us: local(): key_raw = slab_stack[:, 0].astype(jnp.float32)]
    another operation x4 -> x3, local copies, waits for them, and re-layouts: 10.5 us -> 2.56 us  [the longest x2 1.56 us: local(): part_a = jnp.stack([key_grad[:cond_depth], value_grad[:cond_depth]])]
  transfers between devices with their start and end apart: 2 -> 1, of which waited for: 2 -> 1; matrix products, arithmetic and copies ran while one was open for 2% -> 2% of each run, Pallas kernels for 0% -> 0%
where the time goes in v1:
time: 308 us
  blocking collectives  165 us (54%)
  waiting for transfers between devices  88 us (29%)
  between operations  18.7 us (6%)
  Pallas kernels  14.8 us (5%)
  other arithmetic  13.4 us (4%)
  local copies, waits for them, and re-layouts  7.38 us (2%)
    psum x1, blocking collectives, local(): summed = lax.psum(partial_grads, 'seq')  157 us
    psum x1, waiting for transfers between devices, local(): lax.psum(jnp.where(owned[:, None, None, None], own_slab[None], jnp.zeros_...  88 us
    pallas_call x1, Pallas kernels, attend(): pl.pallas_call(attend_kernel, grid=(head_count,), in_specs=[pl.BlockSpec(...  14.8 us
    psum x1, blocking collectives, local(): lax.psum((jnp.sum(query_wide * query_wide, axis=1), jnp.sum(own_key * own...  8.34 us
  transfers between devices with their start and end apart: 1, of which 1 were waited for; matrix products, arithmetic and copies ran while one was open for 2% of the time, Pallas kernels for 0%

profile of v1, /device:TPU:0, one launch (start us, length us, event | category | flops | bytes accessed | tf_op | source)
XLA Modules:
  0.0 307.6 jit_solution(6678611969527583955)
XLA Ops:
  7.2 0.0 all-reduce.5.cloned.1.call-start
  7.2 1.2 fusion.6
  8.4 1.0 slice_bitcast_fusion.4
  9.4 1.6 fusion
  11.0 8.3 %all-reduce.1 = (f32[480]{0:T(512)S(1)}, f32[128]{0:T(128)S(1)}) all-reduce(f32[480]{0:T(512)S(1)} %fusion, f32[128]{0:T(128)S(1)} %fusion.6), channel_id=1, replica_groups=mesh['seq'=8,'mp'=4] {'mp'}, use_global_device_ids=true, to_apply=%region_3.4 | all-reduce | flops 608 | bytes 4864 | tf_op jit(solution)/shard_map/psum | solution.py:80
  19.4 0.7 fusion.7
  20.1 0.1 fusion.5
  20.2 0.1 pad_maximum_fusion.2
  20.3 1.5 broadcast_select_fusion
  21.8 0.0 all-reduce.5.cloned.1.call-update
  21.8 0.6 copy-done.6
  22.5 0.2 reduce-window.9
  22.6 0.6 select_reduce_fusion
  24.6 0.1 convert_reduce_fusion
  24.7 0.5 slice.37
  27.2 0.7 broadcast_in_dim.83
  27.8 0.6 concatenate.9
  28.4 0.8 copy.10.tok_clip_ref
  30.6 0.7 iota_compare_fusion
  31.2 1.4 fusion.2.q_ref
  32.6 88.0 %all-reduce.5.cloned.1.call-done = bf16[3,2,128,1280]{3,2,1,0:T(8,128)(2,1)} async-done(((bf16[3,2,128,1280]{3,2,1,0:T(8,128)(2,1)}), bf16[3,2,128,1280]{3,2,1,0:T(8,128)(2,1)}) %all-reduce.5.cloned.1.call-update) | async-done | bytes 1966096 | tf_op jit(solution)/shard_map/psum | solution.py:89
  120.6 1.4 dynamic-slice_bitcast_fusion.1
  122.0 1.1 pad_maximum_fusion.3
  123.1 14.8 %shard_map.86 = (bf16[480,1280]{1,0:T(8,128)(2,1)}, f32[256,1280]{1,0:T(8,128)}, f32[256,1280]{1,0:T(8,128)}) custom-call(s32[480,1]{1,0:T(8,128)} %copy.10.tok_clip_ref, s32[1,256]{1,0:T(1,128)} %bitcast.33, bf16[480,1280]{1,0:T(8,128)(2,1)} %fusion.2.q_ref, bf16[256,1280]{1,0:T(8,128)(2,1)} %get-tuple-element.20.k_ref, ...), custom_call_target="tpu_custom_call" | custom-call | tf_op jit(solution)/shard_map/pallas_call | solution.py:48
  137.9 1.5 slice_bitcast_fusion.3
  139.4 0.2 copy-done.2
  139.6 0.1 slice_bitcast_fusion.2
  139.7 0.1 pad_maximum_fusion
  139.8 0.1 pad_maximum_fusion.1
  139.9 2.3 select_add_fusion
  142.2 156.9 %all-reduce.6 = bf16[3,2,128,1280]{3,2,1,0:T(8,128)(2,1)S(1)} all-reduce(f32[3,2,128,1280]{3,2,1,0:T(8,128)} %select_add_fusion), channel_id=1, replica_groups=mesh['seq'=8,'mp'=4] {'seq'}, use_global_device_ids=true, to_apply=%region_8.9 | all-reduce | flops 983040 | bytes 5898240 | tf_op jit(solution)/shard_map/psum | solution.py:112
  299.2 1.6 select_convert_fusion
  (17 shorter events, 0.1 us)
Async XLA Ops:
  7.2 12.9 %copy-start.1 = (bf16[1,2,128,1280]{3,2,1,0:T(8,128)(2,1)S(1)}, bf16[1,2,128,1280]{3,2,1,0:T(8,128)(2,1)}, u32[]{:S(2)}) copy-start(bf16[1,2,128,1280]{3,2,1,0:T(8,128)(2,1)} %param.9) | copy-start | bytes 1966084
  7.2 12.2 %copy-start.5 = (s32[3]{0:T(128)S(1)}, s32[3]{0:T(128)}, u32[]{:S(2)}) copy-start(s32[3]{0:T(128)} %param.13) | copy-start | bytes 40
  7.2 12.9 %copy-start.3 = (f32[1280]{0:T(1024)S(1)}, f32[1280]{0:T(1024)}, u32[]{:S(2)}) copy-start(f32[1280]{0:T(1024)} %param.10) | copy-start | bytes 15364
  7.2 113.4 %all-reduce.5.cloned.1.call-start = ((), (), s32[]{:S(2)}) async-start(), calls=%async_computation | async-start | bytes 3932160 | tf_op jit(solution)/shard_map/psum | solution.py:89
  21.8 0.7 copy-start.6
  21.8 9.4 %copy-start = (bf16[480,1280]{1,0:T(8,128)(2,1)S(1)}, bf16[480,1280]{1,0:T(8,128)(2,1)}, u32[]{:S(2)}) copy-start(bf16[480,1280]{1,0:T(8,128)(2,1)} %param.7) | copy-start | bytes 3686404
  21.8 9.4 %copy-start.4 = (f32[1280]{0:T(1024)S(1)}, f32[1280]{0:T(1024)}, u32[]{:S(2)}) copy-start(f32[1280]{0:T(1024)} %param.8) | copy-start | bytes 15364
  137.9 1.7 copy-start.2
Sparse Core Ops, SparseCore 0:
  22.0 98.6 all-reduce.4

commit v2 on v1

--- a/solution.py
+++ b/solution.py
@@ -66,15 +66,18 @@
     )(tok_clip, key_clip, query_normed, keys, values, grad_out)
 
 
-def local(query, query_gain, cond, key_gain, grad_out, clip_len, clip_owner):
-    tok_rows = query.shape[0]
+def local(query, query_gain, cond, key_gain, grad_out, clip_len, clip_owner, seq_count):
+    tok_rows, feat_width = query.shape
     clip_count = clip_len.shape[0]
     cond_depth = cond.shape[2]
+    piece = cond_depth // seq_count
     my_index = lax.axis_index("seq")
     first_pos = my_index * tok_rows
     position = first_pos + jnp.arange(tok_rows, dtype=jnp.int32)
     starts = jnp.cumsum(clip_len) - clip_len
     clip_of = jnp.sum((position[:, None] >= starts[None, :]).astype(jnp.int32), axis=1) - 1
+    device_pos = jnp.arange(seq_count, dtype=jnp.int32) * tok_rows
+    device_first = jnp.sum((device_pos[:, None] >= starts[None, :]).astype(jnp.int32), axis=1) - 1
     query_wide = query.astype(jnp.float32)
     own_key = cond[0, 0].astype(jnp.float32)
     sums = lax.psum(
@@ -85,40 +88,50 @@
     key_scale = lax.rsqrt(sums[1] / D + EPS)
     own_key_normed = (own_key * key_scale[:, None] * key_gain).astype(jnp.bfloat16)
     own_slab = jnp.stack([own_key_normed, cond[0, 1]])
-    owned = clip_owner == my_index
-    slabs = lax.psum(
-        jnp.where(owned[:, None, None, None], own_slab[None], jnp.zeros_like(own_slab)[None]),
-        "seq",
-    )
-    first_clip = clip_of[0]
-    second_clip = first_clip + 1
-    second_index = jnp.minimum(second_clip, clip_count - 1)
-    slab_a = lax.dynamic_index_in_dim(slabs, first_clip, 0, keepdims=False)
-    slab_b = lax.dynamic_index_in_dim(slabs, second_index, 0, keepdims=False)
-    keys = jnp.concatenate([slab_a[0], slab_b[0]], axis=0)
-    values = jnp.concatenate([slab_a[1], slab_b[1]], axis=0)
+    spread = own_slab.reshape(2, seq_count, piece, feat_width).transpose(1, 0, 2, 3)
+    gathered = lax.all_to_all(spread, "seq", 0, 0, tiled=True)
+    clip_rows = jnp.take(gathered, clip_owner, axis=0)
+    slot_clip = jnp.stack([device_first, device_first + 1], axis=1)
+    wanted = jnp.take(clip_rows, jnp.minimum(slot_clip, clip_count - 1), axis=0)
+    arrived = lax.all_to_all(wanted, "seq", 0, 0, tiled=True)
+    mine = arrived.transpose(1, 2, 0, 3, 4).reshape(2, 2, cond_depth, feat_width)
+    keys = mine[:, 0].reshape(2 * cond_depth, feat_width)
+    values = mine[:, 1].reshape(2 * cond_depth, feat_width)
+    first_clip = device_first[my_index]
     key_clip = jnp.concatenate(
-        [jnp.full((cond_depth,), first_clip, jnp.int32), jnp.full((cond_depth,), second_clip, jnp.int32)]
+        [jnp.full((cond_depth,), first_clip, jnp.int32), jnp.full((cond_depth,), first_clip + 1, jnp.int32)]
     )
     grad_query, key_grad, value_grad = attend(
         clip_of[:, None], key_clip[None, :], query_normed, keys, values, grad_out
     )
-    part_a = jnp.stack([key_grad[:cond_depth], value_grad[:cond_depth]])
-    part_b = jnp.stack([key_grad[cond_depth:], value_grad[cond_depth:]])
-    clip_ids = jnp.arange(clip_count, dtype=jnp.int32)[:, None, None, None]
-    partial_grads = jnp.where(clip_ids == first_clip, part_a[None], 0.0) + jnp.where(
-        clip_ids == second_clip, part_b[None], 0.0
+    partial = jnp.stack(
+        [key_grad.reshape(2, cond_depth, feat_width), value_grad.reshape(2, cond_depth, feat_width)], axis=1
+    ).astype(jnp.bfloat16)
+    spread_grads = partial.reshape(2, 2, seq_count, piece, feat_width).transpose(2, 0, 1, 3, 4)
+    pieces = lax.all_to_all(spread_grads, "seq", 0, 0, tiled=True)
+    source_clip = slot_clip.reshape(2 * seq_count)
+    onehot = (source_clip[:, None] == jnp.arange(clip_count, dtype=jnp.int32)[None, :]).astype(jnp.bfloat16)
+    summed = jnp.einsum(
+        "sc,sx->cx", onehot, pieces.reshape(2 * seq_count, -1), preferred_element_type=jnp.float32
+    ).astype(jnp.bfloat16).reshape(clip_count, 2, piece, feat_width)
+    owns = clip_owner[None, :] == jnp.arange(seq_count, dtype=jnp.int32)[:, None]
+    owned_clip = jnp.sum(jnp.where(owns, jnp.arange(clip_count, dtype=jnp.int32)[None, :], 0), axis=1)
+    outgoing = jnp.where(
+        jnp.any(owns, axis=1)[:, None, None, None], jnp.take(summed, owned_clip, axis=0), jnp.zeros((), jnp.bfloat16)
     )
-    summed = lax.psum(partial_grads, "seq")
-    my_clip = jnp.sum(jnp.where(owned, jnp.arange(clip_count, dtype=jnp.int32), 0))
-    mine = lax.dynamic_index_in_dim(summed, my_clip, 0, keepdims=False)
-    owned_grads = jnp.where(jnp.any(owned), mine, 0.0).astype(jnp.bfloat16)
+    returned = lax.all_to_all(outgoing, "seq", 0, 0, tiled=True)
+    owned_grads = returned.transpose(1, 0, 2, 3).reshape(2, cond_depth, feat_width)
     return (grad_query, owned_grads[None])
 
 
 def solution(mesh):
+    seq_count = mesh.shape["seq"]
+
+    def body(*args):
+        return local(*args, seq_count)
+
     return jax.shard_map(
-        local,
+        body,
         mesh=mesh,
         in_specs=(
             P("seq", "mp"),

time: 308 us -> 150 us (0.49)
  blocking collectives: 165 us -> 29.6 us
  between operations: 18.7 us -> 1.5 us
  waiting for transfers between devices: 88 us -> 72.3 us
  starting transfers between devices: 0.04 us -> 13.2 us
  other arithmetic: 13.4 us -> 9.06 us
    psum x1 -> x0, blocking collectives: 157 us -> none  [local(): summed = lax.psum(partial_grads, 'seq')]
    psum x1 -> x0, waiting for transfers between devices: 88 us -> none  [local(): lax.psum(jnp.where(owned[:, None, None, None], own_slab[None], jnp.zeros_...]
    all_to_all x0 -> x3, waiting for transfers between devices: none -> 72.3 us  [the longest x1 31 us: local(): pieces = lax.all_to_all(spread_grads, 'seq', 0, 0, tiled=True)]
    all_to_all x0 -> x1, blocking collectives: none -> 21.3 us  [local(): returned = lax.all_to_all(outgoing, 'seq', 0, 0, tiled=True)]
    all_to_all x0 -> x3, starting transfers between devices: none -> 13.2 us  [the longest x1 5.83 us: local(): gathered = lax.all_to_all(spread, 'seq', 0, 0, tiled=True)]
  transfers between devices with their start and end apart: 1 -> 3, of which waited for: 1 -> 3; matrix products, arithmetic and copies ran while one was open for 2% -> 3% of each run, Pallas kernels for 0% -> 0%
where the time goes in v2:
time: 150 us; the launch traced here: 149 us
  waiting for transfers between devices  72.3 us (48%)
  blocking collectives  29.6 us (20%)
  Pallas kernels  14.8 us (10%)
  starting transfers between devices  13.2 us (9%)
  other arithmetic  9.06 us (6%)
  local copies, waits for them, and re-layouts  8.2 us (5%)
  between operations  1.5 us (1%)
    all_to_all x1, waiting for transfers between devices, local(): pieces = lax.all_to_all(spread_grads, 'seq', 0, 0, tiled=True)  31 us
    all_to_all x1, waiting for transfers between devices, local(): arrived = lax.all_to_all(wanted, 'seq', 0, 0, tiled=True)  25.9 us
    all_to_all x1, blocking collectives, local(): returned = lax.all_to_all(outgoing, 'seq', 0, 0, tiled=True)  21.3 us
    all_to_all x1, waiting for transfers between devices, local(): gathered = lax.all_to_all(spread, 'seq', 0, 0, tiled=True)  15.5 us
    pallas_call x1, Pallas kernels, attend(): pl.pallas_call(attend_kernel, grid=(head_count,), in_specs=[pl.BlockSpec(...  14.8 us
    psum x1, blocking collectives, local(): lax.psum((jnp.sum(query_wide * query_wide, axis=1), jnp.sum(own_key * own...  8.34 us
    all_to_all x1, starting transfers between devices, local(): gathered = lax.all_to_all(spread, 'seq', 0, 0, tiled=True)  5.83 us
    all_to_all x1, starting transfers between devices, local(): arrived = lax.all_to_all(wanted, 'seq', 0, 0, tiled=True)  3.77 us
  transfers between devices with their start and end apart: 3, of which 3 were waited for; matrix products, arithmetic and copies ran while one was open for 3% of the time, Pallas kernels for 0%

profile of v2, /device:TPU:0, one launch (start us, length us, event | category | flops | bytes accessed | tf_op | source)
XLA Modules:
  0.0 149.1 jit_solution(15157545788168355358)
XLA Ops:
  0.7 1.3 slice_convert_fusion
  1.9 0.1 multiply_reduce_fusion
  2.1 0.2 copy-done
  2.3 0.3 fusion
  2.6 8.3 %all-reduce.1 = (f32[480]{0:T(512)S(1)}, f32[128]{0:T(128)S(1)}) all-reduce(f32[480]{0:T(512)S(1)} %fusion, f32[128]{0:T(128)S(1)} %multiply_reduce_fusion), channel_id=1, replica_groups=mesh['seq'=8,'mp'=4] {'mp'}, use_global_device_ids=true, to_apply=%region_4.5 | all-reduce | flops 608 | bytes 4864 | tf_op jit(solution)/shard_map/psum | solution.py:83
  11.2 0.9 maximum_bitcast_fusion
  12.1 5.8 %all-to-all-start = ((bf16[8,2,16,1280]{3,2,1,0:T(8,128)(2,1)}), bf16[8,2,16,1280]{3,2,1,0:T(8,128)(2,1)S(1)}, u32[]{:S(2)}, u32[]{:S(2)}) async-start(bf16[8,2,16,1280]{3,2,1,0:T(8,128)(2,1)} %maximum_bitcast_fusion), calls=%async_computation | async-start | bytes 1310720 | tf_op jit(solution)/shard_map/all_to_all | solution.py:92
  18.0 0.2 reduce-window.9
  18.6 15.5 %all-to-all-done = bf16[8,2,16,1280]{3,2,1,0:T(8,128)(2,1)S(1)} async-done(((bf16[8,2,16,1280]{3,2,1,0:T(8,128)(2,1)}), bf16[8,2,16,1280]{3,2,1,0:T(8,128)(2,1)S(1)}, u32[]{:S(2)}, u32[]{:S(2)}) %all-to-all-start) | async-done | bytes 655392 | tf_op jit(solution)/shard_map/all_to_all | solution.py:92
  34.1 0.6 gather_fusion
  34.8 0.6 gather_fusion.1
  35.4 1.2 copy_select_fusion
  36.7 3.8 %all-to-all-start.1 = ((bf16[8,2,2,16,1280]{4,3,1,2,0:T(8,128)(2,1)}), bf16[8,2,2,16,1280]{4,3,1,2,0:T(8,128)(2,1)S(1)}, u32[]{:S(2)}, u32[]{:S(2)}) async-start(bf16[8,2,2,16,1280]{4,3,1,2,0:T(8,128)(2,1)} %copy_select_fusion), calls=%async_computation.1 | async-start | bytes 2621440 | tf_op jit(solution)/shard_map/all_to_all | solution.py:96
  40.5 0.8 copy.41.tok_clip_ref
  41.4 0.6 dynamic_slice.3
  42.6 0.6 broadcast_in_dim.77
  43.3 0.6 concatenate.15
  43.9 1.4 fusion.2.q_ref
  45.3 25.9 %all-to-all-done.1 = bf16[8,2,2,16,1280]{4,3,1,2,0:T(8,128)(2,1)S(1)} async-done(((bf16[8,2,2,16,1280]{4,3,1,2,0:T(8,128)(2,1)}), bf16[8,2,2,16,1280]{4,3,1,2,0:T(8,128)(2,1)S(1)}, u32[]{:S(2)}, u32[]{:S(2)}) %all-to-all-start.1) | async-done | bytes 1310752 | tf_op jit(solution)/shard_map/all_to_all | solution.py:96
  71.2 1.1 fusion.7
  72.4 14.8 %shard_map.86 = (bf16[480,1280]{1,0:T(8,128)(2,1)}, f32[256,1280]{1,0:T(8,128)}, f32[256,1280]{1,0:T(8,128)}) custom-call(s32[480,1]{1,0:T(8,128)} %copy.41.tok_clip_ref, s32[1,256]{1,0:T(1,128)} %bitcast.54, bf16[480,1280]{1,0:T(8,128)(2,1)} %fusion.2.q_ref, bf16[256,1280]{1,0:T(8,128)(2,1)} %bitcast.45, bf16[256,1280]{1,0:T(8,128)(2,1)} %bitcast.44, ...), custom_call_target="tpu_custom_call" | custom-call | tf_op jit(solution)/shard_map/pallas_call | solution.py:48
  87.2 1.5 convert.9
  88.7 0.2 copy-done.2
  89.0 1.2 copy_bitcast_fusion
  90.1 3.6 %all-to-all-start.2 = ((bf16[8,2,2,16,1280]{4,3,2,1,0:T(8,128)(2,1)}), bf16[8,2,2,16,1280]{4,3,2,1,0:T(8,128)(2,1)S(1)}, u32[]{:S(2)}, u32[]{:S(2)}) async-start(bf16[8,2,2,16,1280]{4,3,2,1,0:T(8,128)(2,1)} %copy_bitcast_fusion), calls=%async_computation.2 | async-start | bytes 2621440 | tf_op jit(solution)/shard_map/all_to_all | solution.py:111
  94.1 31.0 %all-to-all-done.2 = bf16[8,2,2,16,1280]{4,3,2,1,0:T(8,128)(2,1)S(1)} async-done(((bf16[8,2,2,16,1280]{4,3,2,1,0:T(8,128)(2,1)}), bf16[8,2,2,16,1280]{4,3,2,1,0:T(8,128)(2,1)S(1)}, u32[]{:S(2)}, u32[]{:S(2)}) %all-to-all-start.2) | async-done | bytes 1310752 | tf_op jit(solution)/shard_map/all_to_all | solution.py:111
  125.1 0.6 reshape.201
  125.7 0.5 convolution_convert_fusion
  126.2 0.6 gather_fusion.2
  126.8 0.2 select_select_fusion
  127.0 21.3 %all_to_all.20 = bf16[8,2,16,1280]{3,2,1,0:T(8,128)(2,1)S(1)} all-to-all(bf16[8,2,16,1280]{3,2,1,0:T(8,128)(2,1)S(1)} %select_select_fusion), channel_id=1, replica_groups=mesh['seq'=8,'mp'=4] {'seq'}, dimensions={0} | all-to-all | bytes 1310720 | tf_op jit(solution)/shard_map/all_to_all | solution.py:122
  148.3 0.9 copy.45
  (45 shorter events, 1.4 us)
Async XLA Ops:
  0.6 1.3 copy-start.1
  0.6 1.7 %copy-start = (bf16[480,1280]{1,0:T(8,128)(2,1)S(1)}, bf16[480,1280]{1,0:T(8,128)(2,1)}, u32[]{:S(2)}) copy-start(bf16[480,1280]{1,0:T(8,128)(2,1)} %param.7) | copy-start | bytes 3686404
  0.6 10.4 %copy-start.3 = (f32[1280]{0:T(1024)S(1)}, f32[1280]{0:T(1024)}, u32[]{:S(2)}) copy-start(f32[1280]{0:T(1024)} %param.10) | copy-start | bytes 15364
  11.2 6.8 %copy-start.5 = (s32[3]{0:T(128)S(1)}, s32[3]{0:T(128)}, u32[]{:S(2)}) copy-start(s32[3]{0:T(128)} %param.12) | copy-start | bytes 40
  11.2 7.3 %copy-start.6 = (s32[3]{0:T(128)S(1)}, s32[3]{0:T(128)}, u32[]{:S(2)}) copy-start(s32[3]{0:T(128)} %param.13) | copy-start | bytes 40
  12.1 22.0 %all-to-all-start = ((bf16[8,2,16,1280]{3,2,1,0:T(8,128)(2,1)}), bf16[8,2,16,1280]{3,2,1,0:T(8,128)(2,1)S(1)}, u32[]{:S(2)}, u32[]{:S(2)}) async-start(bf16[8,2,16,1280]{3,2,1,0:T(8,128)(2,1)} %maximum_bitcast_fusion), calls=%async_computation | async-start | bytes 1310720 | tf_op jit(solution)/shard_map/all_to_all | solution.py:92
  36.6 7.2 %copy-start.4 = (f32[1280]{0:T(1024)S(1)}, f32[1280]{0:T(1024)}, u32[]{:S(2)}) copy-start(f32[1280]{0:T(1024)} %param.8) | copy-start | bytes 15364
  36.7 34.5 %all-to-all-start.1 = ((bf16[8,2,2,16,1280]{4,3,1,2,0:T(8,128)(2,1)}), bf16[8,2,2,16,1280]{4,3,1,2,0:T(8,128)(2,1)S(1)}, u32[]{:S(2)}, u32[]{:S(2)}) async-start(bf16[8,2,2,16,1280]{4,3,1,2,0:T(8,128)(2,1)} %copy_select_fusion), calls=%async_computation.1 | async-start | bytes 2621440 | tf_op jit(solution)/shard_map/all_to_all | solution.py:96
  87.2 1.7 %copy-start.2 = (f32[256,1280]{1,0:T(8,128)S(1)}, f32[256,1280]{1,0:T(8,128)}, u32[]{:S(2)}) copy-start(f32[256,1280]{1,0:T(8,128)} %get-tuple-element.7) | copy-start | bytes 3932164
  90.1 34.9 %all-to-all-start.2 = ((bf16[8,2,2,16,1280]{4,3,2,1,0:T(8,128)(2,1)}), bf16[8,2,2,16,1280]{4,3,2,1,0:T(8,128)(2,1)S(1)}, u32[]{:S(2)}, u32[]{:S(2)}) async-start(bf16[8,2,2,16,1280]{4,3,2,1,0:T(8,128)(2,1)} %copy_bitcast_fusion), calls=%async_computation.2 | async-start | bytes 2621440 | tf_op jit(solution)/shard_map/all_to_all | solution.py:111

commit v3 on v2

--- a/solution.py
+++ b/solution.py
@@ -15,39 +15,44 @@
 MASKED = -1e30
 
 
+HEADS_PER_STEP = 2
+
+
 def attend_kernel(tok_clip_ref, key_clip_ref, q_ref, k_ref, v_ref, g_ref, dq_ref, dk_ref, dv_ref):
     score_scale = 1.0 / math.sqrt(HEAD_DIM)
-    q = q_ref[...]
-    k = k_ref[...]
-    v = v_ref[...]
-    g = g_ref[...]
     allowed = tok_clip_ref[...] == key_clip_ref[...]
     nt = (((1,), (1,)), ((), ()))
     tn = (((0,), (0,)), ((), ()))
-    scores = lax.dot_general(q, k, nt, preferred_element_type=jnp.float32) * score_scale
-    scores = jnp.where(allowed, scores, MASKED)
-    row_max = jnp.max(scores, axis=1, keepdims=True)
-    weights = jnp.exp(scores - row_max)
-    normed = weights / jnp.sum(weights, axis=1, keepdims=True)
-    weights_low = normed.astype(jnp.bfloat16)
-    attended = jnp.dot(weights_low, v, preferred_element_type=jnp.float32).astype(jnp.bfloat16)
-    delta = jnp.sum(g.astype(jnp.float32) * attended.astype(jnp.float32), axis=1, keepdims=True)
-    grad_weights = lax.dot_general(g, v, nt, preferred_element_type=jnp.float32)
-    grad_scores = (normed * (grad_weights - delta) * score_scale).astype(jnp.bfloat16)
-    dq_ref[...] = jnp.dot(grad_scores, k, preferred_element_type=jnp.float32).astype(dq_ref.dtype)
-    dk_ref[...] = lax.dot_general(grad_scores, q, tn, preferred_element_type=jnp.float32)
-    dv_ref[...] = lax.dot_general(weights_low, g, tn, preferred_element_type=jnp.float32)
+    for head in range(HEADS_PER_STEP):
+        cols = slice(head * HEAD_DIM, (head + 1) * HEAD_DIM)
+        q = q_ref[:, cols]
+        k = k_ref[:, cols]
+        v = v_ref[:, cols]
+        g = g_ref[:, cols]
+        scores = lax.dot_general(q, k, nt, preferred_element_type=jnp.float32) * score_scale
+        scores = jnp.where(allowed, scores, MASKED)
+        row_max = jnp.max(scores, axis=1, keepdims=True)
+        weights = jnp.exp(scores - row_max)
+        normed = weights * (1.0 / jnp.sum(weights, axis=1, keepdims=True))
+        weights_low = normed.astype(jnp.bfloat16)
+        attended = jnp.dot(weights_low, v, preferred_element_type=jnp.float32).astype(jnp.bfloat16)
+        delta = jnp.sum(g.astype(jnp.float32) * attended.astype(jnp.float32), axis=1, keepdims=True)
+        grad_weights = lax.dot_general(g, v, nt, preferred_element_type=jnp.float32)
+        grad_scores = (normed * (grad_weights - delta) * score_scale).astype(jnp.bfloat16)
+        dq_ref[:, cols] = jnp.dot(grad_scores, k, preferred_element_type=jnp.float32).astype(dq_ref.dtype)
+        dk_ref[:, cols] = lax.dot_general(grad_scores, q, tn, preferred_element_type=jnp.float32)
+        dv_ref[:, cols] = lax.dot_general(weights_low, g, tn, preferred_element_type=jnp.float32)
 
 
 def attend(tok_clip, key_clip, query_normed, keys, values, grad_out):
     tok_rows, feat_width = query_normed.shape
     key_rows = keys.shape[0]
-    head_count = feat_width // HEAD_DIM
-    tok_spec = pl.BlockSpec((tok_rows, HEAD_DIM), lambda h: (0, h))
-    key_spec = pl.BlockSpec((key_rows, HEAD_DIM), lambda h: (0, h))
+    step_width = HEADS_PER_STEP * HEAD_DIM
+    tok_spec = pl.BlockSpec((tok_rows, step_width), lambda h: (0, h))
+    key_spec = pl.BlockSpec((key_rows, step_width), lambda h: (0, h))
     return pl.pallas_call(
         attend_kernel,
-        grid=(head_count,),
+        grid=(feat_width // step_width,),
         in_specs=[
             pl.BlockSpec((tok_rows, 1), lambda h: (0, 0)),
             pl.BlockSpec((1, key_rows), lambda h: (0, 0)),

time: 150 us -> 147 us (0.980)
  Pallas kernels: 14.8 us -> 12.5 us
    pallas_call x1, Pallas kernels: 14.8 us -> 12.5 us  [attend(): pl.pallas_call(attend_kernel, grid=(feat_width // step_width,), in_specs=...]
where the time goes in v3:
time: 147 us
  waiting for transfers between devices  72.3 us (49%)
  blocking collectives  29.6 us (20%)
  starting transfers between devices  13.2 us (9%)
  Pallas kernels  12.5 us (9%)
  other arithmetic  9.06 us (6%)
  local copies, waits for them, and re-layouts  8.2 us (6%)
  between operations  1.5 us (1%)
    all_to_all x1, waiting for transfers between devices, local(): pieces = lax.all_to_all(spread_grads, 'seq', 0, 0, tiled=True)  31 us
    all_to_all x1, waiting for transfers between devices, local(): arrived = lax.all_to_all(wanted, 'seq', 0, 0, tiled=True)  25.9 us
    all_to_all x1, blocking collectives, local(): returned = lax.all_to_all(outgoing, 'seq', 0, 0, tiled=True)  21.3 us
    all_to_all x1, waiting for transfers between devices, local(): gathered = lax.all_to_all(spread, 'seq', 0, 0, tiled=True)  15.5 us
    pallas_call x1, Pallas kernels, attend(): pl.pallas_call(attend_kernel, grid=(feat_width // step_width,), in_specs=...  12.5 us
    psum x1, blocking collectives, local(): lax.psum((jnp.sum(query_wide * query_wide, axis=1), jnp.sum(own_key * own...  8.34 us
    all_to_all x1, starting transfers between devices, local(): gathered = lax.all_to_all(spread, 'seq', 0, 0, tiled=True)  5.83 us
    all_to_all x1, starting transfers between devices, local(): arrived = lax.all_to_all(wanted, 'seq', 0, 0, tiled=True)  3.77 us
  transfers between devices with their start and end apart: 3, of which 3 were waited for; matrix products, arithmetic and copies ran while one was open for 3% of the time, Pallas kernels for 0%

profile of v3, /device:TPU:0, one launch (start us, length us, event | category | flops | bytes accessed | tf_op | source)
XLA Modules:
  0.0 146.9 jit_solution(8050865447016670953)
XLA Ops:
  0.7 1.3 slice_convert_fusion
  1.9 0.1 multiply_reduce_fusion
  2.1 0.2 copy-done
  2.3 0.3 fusion
  2.6 8.3 %all-reduce.1 = (f32[480]{0:T(512)S(1)}, f32[128]{0:T(128)S(1)}) all-reduce(f32[480]{0:T(512)S(1)} %fusion, f32[128]{0:T(128)S(1)} %multiply_reduce_fusion), channel_id=1, replica_groups=mesh['seq'=8,'mp'=4] {'mp'}, use_global_device_ids=true, to_apply=%region_4.5 | all-reduce | flops 608 | bytes 4864 | tf_op jit(solution)/shard_map/psum | solution.py:88
  11.2 0.9 maximum_bitcast_fusion
  12.1 5.8 %all-to-all-start = ((bf16[8,2,16,1280]{3,2,1,0:T(8,128)(2,1)}), bf16[8,2,16,1280]{3,2,1,0:T(8,128)(2,1)S(1)}, u32[]{:S(2)}, u32[]{:S(2)}) async-start(bf16[8,2,16,1280]{3,2,1,0:T(8,128)(2,1)} %maximum_bitcast_fusion), calls=%async_computation | async-start | bytes 1310720 | tf_op jit(solution)/shard_map/all_to_all | solution.py:97
  18.0 0.2 reduce-window.9
  18.6 15.5 %all-to-all-done = bf16[8,2,16,1280]{3,2,1,0:T(8,128)(2,1)S(1)} async-done(((bf16[8,2,16,1280]{3,2,1,0:T(8,128)(2,1)}), bf16[8,2,16,1280]{3,2,1,0:T(8,128)(2,1)S(1)}, u32[]{:S(2)}, u32[]{:S(2)}) %all-to-all-start) | async-done | bytes 655392 | tf_op jit(solution)/shard_map/all_to_all | solution.py:97
  34.1 0.6 gather_fusion
  34.8 0.6 gather_fusion.1
  35.4 1.2 copy_select_fusion
  36.7 3.8 %all-to-all-start.1 = ((bf16[8,2,2,16,1280]{4,3,1,2,0:T(8,128)(2,1)}), bf16[8,2,2,16,1280]{4,3,1,2,0:T(8,128)(2,1)S(1)}, u32[]{:S(2)}, u32[]{:S(2)}) async-start(bf16[8,2,2,16,1280]{4,3,1,2,0:T(8,128)(2,1)} %copy_select_fusion), calls=%async_computation.1 | async-start | bytes 2621440 | tf_op jit(solution)/shard_map/all_to_all | solution.py:101
  40.5 0.8 copy.41.tok_clip_ref
  41.4 0.6 dynamic_slice.3
  42.6 0.6 broadcast_in_dim.77
  43.3 0.6 concatenate.15
  43.9 1.4 fusion.2.q_ref
  45.3 25.9 %all-to-all-done.1 = bf16[8,2,2,16,1280]{4,3,1,2,0:T(8,128)(2,1)S(1)} async-done(((bf16[8,2,2,16,1280]{4,3,1,2,0:T(8,128)(2,1)}), bf16[8,2,2,16,1280]{4,3,1,2,0:T(8,128)(2,1)S(1)}, u32[]{:S(2)}, u32[]{:S(2)}) %all-to-all-start.1) | async-done | bytes 1310752 | tf_op jit(solution)/shard_map/all_to_all | solution.py:101
  71.2 1.1 fusion.7
  72.4 12.5 %shard_map.86 = (bf16[480,1280]{1,0:T(8,128)(2,1)}, f32[256,1280]{1,0:T(8,128)}, f32[256,1280]{1,0:T(8,128)}) custom-call(s32[480,1]{1,0:T(8,128)} %copy.41.tok_clip_ref, s32[1,256]{1,0:T(1,128)} %bitcast.54, bf16[480,1280]{1,0:T(8,128)(2,1)} %fusion.2.q_ref, bf16[256,1280]{1,0:T(8,128)(2,1)} %bitcast.45, bf16[256,1280]{1,0:T(8,128)(2,1)} %bitcast.44, ...), custom_call_target="tpu_custom_call" | custom-call | tf_op jit(solution)/shard_map/pallas_call | solution.py:53
  84.9 1.5 %convert.9 = bf16[256,1280]{1,0:T(8,128)(2,1)S(1)} convert(f32[256,1280]{1,0:T(8,128)} %get-tuple-element.6) | non-fusion elementwise | flops 327680 | bytes 1966080 | tf_op jit(solution)/shard_map/convert.4
  86.4 0.2 copy-done.2
  86.7 1.2 copy_bitcast_fusion
  87.9 3.6 %all-to-all-start.2 = ((bf16[8,2,2,16,1280]{4,3,2,1,0:T(8,128)(2,1)}), bf16[8,2,2,16,1280]{4,3,2,1,0:T(8,128)(2,1)S(1)}, u32[]{:S(2)}, u32[]{:S(2)}) async-start(bf16[8,2,2,16,1280]{4,3,2,1,0:T(8,128)(2,1)} %copy_bitcast_fusion), calls=%async_computation.2 | async-start | bytes 2621440 | tf_op jit(solution)/shard_map/all_to_all | solution.py:116
  91.8 31.0 %all-to-all-done.2 = bf16[8,2,2,16,1280]{4,3,2,1,0:T(8,128)(2,1)S(1)} async-done(((bf16[8,2,2,16,1280]{4,3,2,1,0:T(8,128)(2,1)}), bf16[8,2,2,16,1280]{4,3,2,1,0:T(8,128)(2,1)S(1)}, u32[]{:S(2)}, u32[]{:S(2)}) %all-to-all-start.2) | async-done | bytes 1310752 | tf_op jit(solution)/shard_map/all_to_all | solution.py:116
  122.8 0.6 reshape.201
  123.4 0.5 convolution_convert_fusion
  123.9 0.6 gather_fusion.2
  124.5 0.2 select_select_fusion
  124.7 21.3 %all_to_all.20 = bf16[8,2,16,1280]{3,2,1,0:T(8,128)(2,1)S(1)} all-to-all(bf16[8,2,16,1280]{3,2,1,0:T(8,128)(2,1)S(1)} %select_select_fusion), channel_id=1, replica_groups=mesh['seq'=8,'mp'=4] {'seq'}, dimensions={0} | all-to-all | bytes 1310720 | tf_op jit(solution)/shard_map/all_to_all | solution.py:127
  146.0 0.9 copy.45
  (45 shorter events, 1.4 us)
Async XLA Ops:
  0.6 1.3 copy-start.1
  0.6 1.7 %copy-start = (bf16[480,1280]{1,0:T(8,128)(2,1)S(1)}, bf16[480,1280]{1,0:T(8,128)(2,1)}, u32[]{:S(2)}) copy-start(bf16[480,1280]{1,0:T(8,128)(2,1)} %param.7) | copy-start | bytes 3686404
  0.6 10.4 %copy-start.3 = (f32[1280]{0:T(1024)S(1)}, f32[1280]{0:T(1024)}, u32[]{:S(2)}) copy-start(f32[1280]{0:T(1024)} %param.10) | copy-start | bytes 15364
  11.2 6.8 %copy-start.5 = (s32[3]{0:T(128)S(1)}, s32[3]{0:T(128)}, u32[]{:S(2)}) copy-start(s32[3]{0:T(128)} %param.12) | copy-start | bytes 40
  11.2 7.3 %copy-start.6 = (s32[3]{0:T(128)S(1)}, s32[3]{0:T(128)}, u32[]{:S(2)}) copy-start(s32[3]{0:T(128)} %param.13) | copy-start | bytes 40
  12.1 22.0 %all-to-all-start = ((bf16[8,2,16,1280]{3,2,1,0:T(8,128)(2,1)}), bf16[8,2,16,1280]{3,2,1,0:T(8,128)(2,1)S(1)}, u32[]{:S(2)}, u32[]{:S(2)}) async-start(bf16[8,2,16,1280]{3,2,1,0:T(8,128)(2,1)} %maximum_bitcast_fusion), calls=%async_computation | async-start | bytes 1310720 | tf_op jit(solution)/shard_map/all_to_all | solution.py:97
  36.6 7.2 %copy-start.4 = (f32[1280]{0:T(1024)S(1)}, f32[1280]{0:T(1024)}, u32[]{:S(2)}) copy-start(f32[1280]{0:T(1024)} %param.8) | copy-start | bytes 15364
  36.7 34.5 %all-to-all-start.1 = ((bf16[8,2,2,16,1280]{4,3,1,2,0:T(8,128)(2,1)}), bf16[8,2,2,16,1280]{4,3,1,2,0:T(8,128)(2,1)S(1)}, u32[]{:S(2)}, u32[]{:S(2)}) async-start(bf16[8,2,2,16,1280]{4,3,1,2,0:T(8,128)(2,1)} %copy_select_fusion), calls=%async_computation.1 | async-start | bytes 2621440 | tf_op jit(solution)/shard_map/all_to_all | solution.py:101
  84.9 1.7 %copy-start.2 = (f32[256,1280]{1,0:T(8,128)S(1)}, f32[256,1280]{1,0:T(8,128)}, u32[]{:S(2)}) copy-start(f32[256,1280]{1,0:T(8,128)} %get-tuple-element.7) | copy-start | bytes 3932164
  87.9 34.9 %all-to-all-start.2 = ((bf16[8,2,2,16,1280]{4,3,2,1,0:T(8,128)(2,1)}), bf16[8,2,2,16,1280]{4,3,2,1,0:T(8,128)(2,1)S(1)}, u32[]{:S(2)}, u32[]{:S(2)}) async-start(bf16[8,2,2,16,1280]{4,3,2,1,0:T(8,128)(2,1)} %copy_bitcast_fusion), calls=%async_computation.2 | async-start | bytes 2621440 | tf_op jit(solution)/shard_map/all_to_all | solution.py:116

commit v4 on v3

--- a/solution.py
+++ b/solution.py
@@ -18,33 +18,58 @@
 HEADS_PER_STEP = 2
 
 
-def attend_kernel(tok_clip_ref, key_clip_ref, q_ref, k_ref, v_ref, g_ref, dq_ref, dk_ref, dv_ref):
+def attend_kernel(tok_slot_ref, q_ref, k_ref, v_ref, g_ref, dq_ref, dk_ref, dv_ref):
     score_scale = 1.0 / math.sqrt(HEAD_DIM)
-    allowed = tok_clip_ref[...] == key_clip_ref[...]
+    depth = k_ref.shape[0] // 2
+    in_first = tok_slot_ref[...] == 0
     nt = (((1,), (1,)), ((), ()))
     tn = (((0,), (0,)), ((), ()))
     for head in range(HEADS_PER_STEP):
         cols = slice(head * HEAD_DIM, (head + 1) * HEAD_DIM)
         q = q_ref[:, cols]
-        k = k_ref[:, cols]
-        v = v_ref[:, cols]
         g = g_ref[:, cols]
-        scores = lax.dot_general(q, k, nt, preferred_element_type=jnp.float32) * score_scale
-        scores = jnp.where(allowed, scores, MASKED)
+        k0 = k_ref[:depth, cols]
+        k1 = k_ref[depth:, cols]
+        v0 = v_ref[:depth, cols]
+        v1 = v_ref[depth:, cols]
+        scores = jnp.where(
+            in_first,
+            lax.dot_general(q, k0, nt, preferred_element_type=jnp.float32),
+            lax.dot_general(q, k1, nt, preferred_element_type=jnp.float32),
+        ) * score_scale
         row_max = jnp.max(scores, axis=1, keepdims=True)
         weights = jnp.exp(scores - row_max)
         normed = weights * (1.0 / jnp.sum(weights, axis=1, keepdims=True))
         weights_low = normed.astype(jnp.bfloat16)
-        attended = jnp.dot(weights_low, v, preferred_element_type=jnp.float32).astype(jnp.bfloat16)
+        attended = jnp.where(
+            in_first,
+            jnp.dot(weights_low, v0, preferred_element_type=jnp.float32),
+            jnp.dot(weights_low, v1, preferred_element_type=jnp.float32),
+        ).astype(jnp.bfloat16)
         delta = jnp.sum(g.astype(jnp.float32) * attended.astype(jnp.float32), axis=1, keepdims=True)
-        grad_weights = lax.dot_general(g, v, nt, preferred_element_type=jnp.float32)
+        grad_weights = jnp.where(
+            in_first,
+            lax.dot_general(g, v0, nt, preferred_element_type=jnp.float32),
+            lax.dot_general(g, v1, nt, preferred_element_type=jnp.float32),
+        )
         grad_scores = (normed * (grad_weights - delta) * score_scale).astype(jnp.bfloat16)
-        dq_ref[:, cols] = jnp.dot(grad_scores, k, preferred_element_type=jnp.float32).astype(dq_ref.dtype)
-        dk_ref[:, cols] = lax.dot_general(grad_scores, q, tn, preferred_element_type=jnp.float32)
-        dv_ref[:, cols] = lax.dot_general(weights_low, g, tn, preferred_element_type=jnp.float32)
+        dq_ref[:, cols] = jnp.where(
+            in_first,
+            jnp.dot(grad_scores, k0, preferred_element_type=jnp.float32),
+            jnp.dot(grad_scores, k1, preferred_element_type=jnp.float32),
+        ).astype(dq_ref.dtype)
+        zero = jnp.zeros_like(grad_scores)
+        gs0 = jnp.where(in_first, grad_scores, zero)
+        gs1 = jnp.where(in_first, zero, grad_scores)
+        w0 = jnp.where(in_first, weights_low, zero)
+        w1 = jnp.where(in_first, zero, weights_low)
+        dk_ref[:depth, cols] = lax.dot_general(gs0, q, tn, preferred_element_type=jnp.float32)
+        dk_ref[depth:, cols] = lax.dot_general(gs1, q, tn, preferred_element_type=jnp.float32)
+        dv_ref[:depth, cols] = lax.dot_general(w0, g, tn, preferred_element_type=jnp.float32)
+        dv_ref[depth:, cols] = lax.dot_general(w1, g, tn, preferred_element_type=jnp.float32)
 
 
-def attend(tok_clip, key_clip, query_normed, keys, values, grad_out):
+def attend(tok_slot, query_normed, keys, values, grad_out):
     tok_rows, feat_width = query_normed.shape
     key_rows = keys.shape[0]
     step_width = HEADS_PER_STEP * HEAD_DIM
@@ -55,7 +80,6 @@
         grid=(feat_width // step_width,),
         in_specs=[
             pl.BlockSpec((tok_rows, 1), lambda h: (0, 0)),
-            pl.BlockSpec((1, key_rows), lambda h: (0, 0)),
             tok_spec,
             key_spec,
             key_spec,
@@ -68,7 +92,7 @@
             jax.ShapeDtypeStruct((key_rows, feat_width), jnp.float32),
         ],
         compiler_params=pltpu.CompilerParams(dimension_semantics=("arbitrary",)),
-    )(tok_clip, key_clip, query_normed, keys, values, grad_out)
+    )(tok_slot, query_normed, keys, values, grad_out)
 
 
 def local(query, query_gain, cond, key_gain, grad_out, clip_len, clip_owner, seq_count):
@@ -102,13 +126,8 @@
     mine = arrived.transpose(1, 2, 0, 3, 4).reshape(2, 2, cond_depth, feat_width)
     keys = mine[:, 0].reshape(2 * cond_depth, feat_width)
     values = mine[:, 1].reshape(2 * cond_depth, feat_width)
-    first_clip = device_first[my_index]
-    key_clip = jnp.concatenate(
-        [jnp.full((cond_depth,), first_clip, jnp.int32), jnp.full((cond_depth,), first_clip + 1, jnp.int32)]
-    )
-    grad_query, key_grad, value_grad = attend(
-        clip_of[:, None], key_clip[None, :], query_normed, keys, values, grad_out
-    )
+    tok_slot = clip_of - device_first[my_index]
+    grad_query, key_grad, value_grad = attend(tok_slot[:, None], query_normed, keys, values, grad_out)
     partial = jnp.stack(
         [key_grad.reshape(2, cond_depth, feat_width), value_grad.reshape(2, cond_depth, feat_width)], axis=1
     ).astype(jnp.bfloat16)

time: 147 us -> 147 us (level)
  no operation moved by 1% of the time
where the time goes in v4:
time: 147 us; the launch traced here: 146 us
  waiting for transfers between devices  73.6 us (50%)
  blocking collectives  29.6 us (20%)
  starting transfers between devices  13.2 us (9%)
  Pallas kernels  11.9 us (8%)
  other arithmetic  9.71 us (7%)
  local copies, waits for them, and re-layouts  6.97 us (5%)
    all_to_all x1, waiting for transfers between devices, local(): pieces = lax.all_to_all(spread_grads, 'seq', 0, 0, tiled=True)  31 us
    all_to_all x1, waiting for transfers between devices, local(): arrived = lax.all_to_all(wanted, 'seq', 0, 0, tiled=True)  27.1 us
    all_to_all x1, blocking collectives, local(): returned = lax.all_to_all(outgoing, 'seq', 0, 0, tiled=True)  21.3 us
    all_to_all x1, waiting for transfers between devices, local(): gathered = lax.all_to_all(spread, 'seq', 0, 0, tiled=True)  15.5 us
    pallas_call x1, Pallas kernels, attend(): pl.pallas_call(attend_kernel, grid=(feat_width // step_width,), in_specs=...  11.9 us
    psum x1, blocking collectives, local(): lax.psum((jnp.sum(query_wide * query_wide, axis=1), jnp.sum(own_key * own...  8.34 us
    all_to_all x1, starting transfers between devices, local(): gathered = lax.all_to_all(spread, 'seq', 0, 0, tiled=True)  5.83 us
    all_to_all x1, starting transfers between devices, local(): arrived = lax.all_to_all(wanted, 'seq', 0, 0, tiled=True)  3.77 us
  transfers between devices with their start and end apart: 3, of which 3 were waited for; matrix products, arithmetic and copies ran while one was open for 3% of the time, Pallas kernels for 0%

profile of v4, /device:TPU:0, one launch (start us, length us, event | category | flops | bytes accessed | tf_op | source)
XLA Modules:
  0.0 146.2 jit_solution(11884510213912583399)
XLA Ops:
  0.7 1.3 slice_convert_fusion
  1.9 0.1 multiply_reduce_fusion
  2.1 0.2 copy-done
  2.3 0.3 fusion
  2.6 8.3 %all-reduce = (f32[480]{0:T(512)S(1)}, f32[128]{0:T(128)S(1)}) all-reduce(f32[480]{0:T(512)S(1)} %fusion, f32[128]{0:T(128)S(1)} %multiply_reduce_fusion), channel_id=1, replica_groups=mesh['seq'=8,'mp'=4] {'mp'}, use_global_device_ids=true, to_apply=%region_4.5 | all-reduce | flops 608 | bytes 4864 | tf_op jit(solution)/shard_map/psum | solution.py:112
  11.1 0.1 multiply_convert_fusion
  11.2 0.9 maximum_bitcast_fusion
  12.1 5.8 %all-to-all-start = ((bf16[8,2,16,1280]{3,2,1,0:T(8,128)(2,1)}), bf16[8,2,16,1280]{3,2,1,0:T(8,128)(2,1)S(1)}, u32[]{:S(2)}, u32[]{:S(2)}) async-start(bf16[8,2,16,1280]{3,2,1,0:T(8,128)(2,1)} %maximum_bitcast_fusion), calls=%async_computation | async-start | bytes 1310720 | tf_op jit(solution)/shard_map/all_to_all | solution.py:121
  18.0 0.2 reduce-window.9
  18.6 15.5 %all-to-all-done = bf16[8,2,16,1280]{3,2,1,0:T(8,128)(2,1)S(1)} async-done(((bf16[8,2,16,1280]{3,2,1,0:T(8,128)(2,1)}), bf16[8,2,16,1280]{3,2,1,0:T(8,128)(2,1)S(1)}, u32[]{:S(2)}, u32[]{:S(2)}) %all-to-all-start) | async-done | bytes 655392 | tf_op jit(solution)/shard_map/all_to_all | solution.py:121
  34.1 0.6 gather_fusion
  34.8 0.6 gather_fusion.1
  35.4 1.2 copy_select_fusion
  36.7 3.8 %all-to-all-start.1 = ((bf16[8,2,2,16,1280]{4,3,1,2,0:T(8,128)(2,1)}), bf16[8,2,2,16,1280]{4,3,1,2,0:T(8,128)(2,1)S(1)}, u32[]{:S(2)}, u32[]{:S(2)}) async-start(bf16[8,2,2,16,1280]{4,3,1,2,0:T(8,128)(2,1)} %copy_select_fusion), calls=%async_computation.1 | async-start | bytes 2621440 | tf_op jit(solution)/shard_map/all_to_all | solution.py:125
  40.4 0.6 dynamic_slice.3
  41.1 0.6 add_subtract_fusion
  41.8 0.8 copy.41.tok_slot_ref
  42.6 1.4 fusion.2.q_ref
  44.0 27.1 %all-to-all-done.1 = bf16[8,2,2,16,1280]{4,3,1,2,0:T(8,128)(2,1)S(1)} async-done(((bf16[8,2,2,16,1280]{4,3,1,2,0:T(8,128)(2,1)}), bf16[8,2,2,16,1280]{4,3,1,2,0:T(8,128)(2,1)S(1)}, u32[]{:S(2)}, u32[]{:S(2)}) %all-to-all-start.1) | async-done | bytes 1310752 | tf_op jit(solution)/shard_map/all_to_all | solution.py:125
  71.2 1.1 fusion.7
  72.4 11.9 %shard_map.86 = (bf16[480,1280]{1,0:T(8,128)(2,1)}, f32[256,1280]{1,0:T(8,128)}, f32[256,1280]{1,0:T(8,128)}) custom-call(s32[480,1]{1,0:T(8,128)} %copy.41.tok_slot_ref, bf16[480,1280]{1,0:T(8,128)(2,1)} %fusion.2.q_ref, bf16[256,1280]{1,0:T(8,128)(2,1)} %bitcast.48, bf16[256,1280]{1,0:T(8,128)(2,1)} %bitcast.47, bf16[480,1280]{1,0:T(8,128)(2,1)} %g_ref.1), custom_call_target="tpu_custom_call" | custom-call | tf_op jit(solution)/shard_map/pallas_call | solution.py:78
  84.3 1.5 %convert.9 = bf16[256,1280]{1,0:T(8,128)(2,1)S(1)} convert(f32[256,1280]{1,0:T(8,128)} %get-tuple-element.6) | non-fusion elementwise | flops 327680 | bytes 1966080 | tf_op jit(solution)/shard_map/convert.4
  85.8 0.2 copy-done.2
  86.0 1.2 copy_bitcast_fusion
  87.2 3.6 %all-to-all-start.2 = ((bf16[8,2,2,16,1280]{4,3,2,1,0:T(8,128)(2,1)}), bf16[8,2,2,16,1280]{4,3,2,1,0:T(8,128)(2,1)S(1)}, u32[]{:S(2)}, u32[]{:S(2)}) async-start(bf16[8,2,2,16,1280]{4,3,2,1,0:T(8,128)(2,1)} %copy_bitcast_fusion), calls=%async_computation.2 | async-start | bytes 2621440 | tf_op jit(solution)/shard_map/all_to_all | solution.py:135
  91.2 31.0 %all-to-all-done.2 = bf16[8,2,2,16,1280]{4,3,2,1,0:T(8,128)(2,1)S(1)} async-done(((bf16[8,2,2,16,1280]{4,3,2,1,0:T(8,128)(2,1)}), bf16[8,2,2,16,1280]{4,3,2,1,0:T(8,128)(2,1)S(1)}, u32[]{:S(2)}, u32[]{:S(2)}) %all-to-all-start.2) | async-done | bytes 1310752 | tf_op jit(solution)/shard_map/all_to_all | solution.py:135
  122.2 0.6 reshape.206
  122.8 0.5 convolution_convert_fusion
  123.3 0.6 gather_fusion.2
  123.9 0.2 select_select_fusion
  124.1 21.3 %all_to_all.20 = bf16[8,2,16,1280]{3,2,1,0:T(8,128)(2,1)S(1)} all-to-all(bf16[8,2,16,1280]{3,2,1,0:T(8,128)(2,1)S(1)} %select_select_fusion), channel_id=1, replica_groups=mesh['seq'=8,'mp'=4] {'seq'}, dimensions={0} | all-to-all | bytes 1310720 | tf_op jit(solution)/shard_map/all_to_all | solution.py:146
  145.4 0.9 copy.45
  (43 shorter events, 1.3 us)
Async XLA Ops:
  0.6 1.3 copy-start.1
  0.6 1.7 %copy-start = (bf16[480,1280]{1,0:T(8,128)(2,1)S(1)}, bf16[480,1280]{1,0:T(8,128)(2,1)}, u32[]{:S(2)}) copy-start(bf16[480,1280]{1,0:T(8,128)(2,1)} %param.7) | copy-start | bytes 3686404
  0.6 10.4 %copy-start.3 = (f32[1280]{0:T(1024)S(1)}, f32[1280]{0:T(1024)}, u32[]{:S(2)}) copy-start(f32[1280]{0:T(1024)} %param.10) | copy-start | bytes 15364
  11.2 6.8 %copy-start.5 = (s32[3]{0:T(128)S(1)}, s32[3]{0:T(128)}, u32[]{:S(2)}) copy-start(s32[3]{0:T(128)} %param.12) | copy-start | bytes 40
  11.2 7.3 %copy-start.6 = (s32[3]{0:T(128)S(1)}, s32[3]{0:T(128)}, u32[]{:S(2)}) copy-start(s32[3]{0:T(128)} %param.13) | copy-start | bytes 40
  12.1 22.0 %all-to-all-start = ((bf16[8,2,16,1280]{3,2,1,0:T(8,128)(2,1)}), bf16[8,2,16,1280]{3,2,1,0:T(8,128)(2,1)S(1)}, u32[]{:S(2)}, u32[]{:S(2)}) async-start(bf16[8,2,16,1280]{3,2,1,0:T(8,128)(2,1)} %maximum_bitcast_fusion), calls=%async_computation | async-start | bytes 1310720 | tf_op jit(solution)/shard_map/all_to_all | solution.py:121
  36.6 6.0 %copy-start.4 = (f32[1280]{0:T(1024)S(1)}, f32[1280]{0:T(1024)}, u32[]{:S(2)}) copy-start(f32[1280]{0:T(1024)} %param.8) | copy-start | bytes 15364
  36.7 34.5 %all-to-all-start.1 = ((bf16[8,2,2,16,1280]{4,3,1,2,0:T(8,128)(2,1)}), bf16[8,2,2,16,1280]{4,3,1,2,0:T(8,128)(2,1)S(1)}, u32[]{:S(2)}, u32[]{:S(2)}) async-start(bf16[8,2,2,16,1280]{4,3,1,2,0:T(8,128)(2,1)} %copy_select_fusion), calls=%async_computation.1 | async-start | bytes 2621440 | tf_op jit(solution)/shard_map/all_to_all | solution.py:125
  84.3 1.7 %copy-start.2 = (f32[256,1280]{1,0:T(8,128)S(1)}, f32[256,1280]{1,0:T(8,128)}, u32[]{:S(2)}) copy-start(f32[256,1280]{1,0:T(8,128)} %get-tuple-element.7) | copy-start | bytes 3932164
  87.2 34.9 %all-to-all-start.2 = ((bf16[8,2,2,16,1280]{4,3,2,1,0:T(8,128)(2,1)}), bf16[8,2,2,16,1280]{4,3,2,1,0:T(8,128)(2,1)S(1)}, u32[]{:S(2)}, u32[]{:S(2)}) async-start(bf16[8,2,2,16,1280]{4,3,2,1,0:T(8,128)(2,1)} %copy_bitcast_fusion), calls=%async_computation.2 | async-start | bytes 2621440 | tf_op jit(solution)/shard_map/all_to_all | solution.py:135

commit v5 on v4

--- a/solution.py
+++ b/solution.py
@@ -108,15 +108,10 @@
     device_pos = jnp.arange(seq_count, dtype=jnp.int32) * tok_rows
     device_first = jnp.sum((device_pos[:, None] >= starts[None, :]).astype(jnp.int32), axis=1) - 1
     query_wide = query.astype(jnp.float32)
-    own_key = cond[0, 0].astype(jnp.float32)
-    sums = lax.psum(
-        (jnp.sum(query_wide * query_wide, axis=1), jnp.sum(own_key * own_key, axis=1)), "mp"
-    )
-    query_scale = lax.rsqrt(sums[0] / D + EPS)
+    query_sumsq = lax.psum(jnp.sum(query_wide * query_wide, axis=1), "mp")
+    query_scale = lax.rsqrt(query_sumsq / D + EPS)
     query_normed = (query_wide * query_scale[:, None] * query_gain).astype(jnp.bfloat16)
-    key_scale = lax.rsqrt(sums[1] / D + EPS)
-    own_key_normed = (own_key * key_scale[:, None] * key_gain).astype(jnp.bfloat16)
-    own_slab = jnp.stack([own_key_normed, cond[0, 1]])
+    own_slab = cond[0]
     spread = own_slab.reshape(2, seq_count, piece, feat_width).transpose(1, 0, 2, 3)
     gathered = lax.all_to_all(spread, "seq", 0, 0, tiled=True)
     clip_rows = jnp.take(gathered, clip_owner, axis=0)
@@ -124,7 +119,10 @@
     wanted = jnp.take(clip_rows, jnp.minimum(slot_clip, clip_count - 1), axis=0)
     arrived = lax.all_to_all(wanted, "seq", 0, 0, tiled=True)
     mine = arrived.transpose(1, 2, 0, 3, 4).reshape(2, 2, cond_depth, feat_width)
-    keys = mine[:, 0].reshape(2 * cond_depth, feat_width)
+    key_raw = mine[:, 0].reshape(2 * cond_depth, feat_width).astype(jnp.float32)
+    key_sumsq = lax.psum(jnp.sum(key_raw * key_raw, axis=1), "mp")
+    key_scale = lax.rsqrt(key_sumsq / D + EPS)
+    keys = (key_raw * key_scale[:, None] * key_gain).astype(jnp.bfloat16)
     values = mine[:, 1].reshape(2 * cond_depth, feat_width)
     tok_slot = clip_of - device_first[my_index]
     grad_query, key_grad, value_grad = attend(tok_slot[:, None], query_normed, keys, values, grad_out)

time: 147 us -> 149 us (1.014)
  blocking collectives: 29.6 us -> 26.7 us
  starting transfers between devices: 13.2 us -> 15.9 us
  waiting for transfers between devices: 73.6 us -> 75.8 us
    psum x1, blocking collectives: 8.34 us -> 5.67 us  [local(): query_sumsq = lax.psum(jnp.sum(query_wide * query_wide, axis=1), 'mp')]
    transpose x0 -> x1, local copies, waits for them, and re-layouts: none -> 1.99 us  [local(): own_slab.reshape(2, seq_count, piece, feat_width).transpose(1, 0, 2, 3)]
    all_to_all x1, waiting for transfers between devices: 27.1 us -> 29.1 us  [local(): arrived = lax.all_to_all(wanted, 'seq', 0, 0, tiled=True)]
  transfers between devices with their start and end apart: 3 -> 3, of which waited for: 3 -> 3; matrix products, arithmetic and copies ran while one was open for 3% -> 2% of each run, Pallas kernels for 0% -> 0%
where the time goes in v5:
time: 149 us
  waiting for transfers between devices  75.8 us (51%)
  blocking collectives  26.7 us (18%)
  starting transfers between devices  15.9 us (11%)
  Pallas kernels  11.9 us (8%)
  other arithmetic  9.46 us (6%)
  local copies, waits for them, and re-layouts  7.51 us (5%)
    all_to_all x1, waiting for transfers between devices, local(): pieces = lax.all_to_all(spread_grads, 'seq', 0, 0, tiled=True)  30.1 us
    all_to_all x1, waiting for transfers between devices, local(): arrived = lax.all_to_all(wanted, 'seq', 0, 0, tiled=True)  29.1 us
    all_to_all x1, blocking collectives, local(): returned = lax.all_to_all(outgoing, 'seq', 0, 0, tiled=True)  21 us
    all_to_all x1, waiting for transfers between devices, local(): gathered = lax.all_to_all(spread, 'seq', 0, 0, tiled=True)  16.7 us
    pallas_call x1, Pallas kernels, attend(): pl.pallas_call(attend_kernel, grid=(feat_width // step_width,), in_specs=...  11.9 us
    all_to_all x1, starting transfers between devices, local(): gathered = lax.all_to_all(spread, 'seq', 0, 0, tiled=True)  7.28 us
    psum x1, blocking collectives, local(): query_sumsq = lax.psum(jnp.sum(query_wide * query_wide, axis=1), 'mp')  5.67 us
    all_to_all x1, starting transfers between devices, local(): pieces = lax.all_to_all(spread_grads, 'seq', 0, 0, tiled=True)  4.85 us
  transfers between devices with their start and end apart: 3, of which 3 were waited for; matrix products, arithmetic and copies ran while one was open for 2% of the time, Pallas kernels for 0%

profile of v5, /device:TPU:0, one launch (start us, length us, event | category | flops | bytes accessed | tf_op | source)
XLA Modules:
  0.0 148.6 jit_solution(17583596544874975233)
XLA Ops:
  0.7 2.0 %copy.39 = bf16[8,2,16,1280]{3,2,1,0:T(8,128)(2,1)} copy(bf16[8,2,16,1280]{3,2,0,1:T(8,128)(2,1)} %bitcast.54) | data formatting | bytes 1310720 | tf_op jit(solution)/shard_map/transpose | solution.py:115
  2.6 7.3 %all-to-all-start = ((bf16[8,2,16,1280]{3,2,1,0:T(8,128)(2,1)}), bf16[8,2,16,1280]{3,2,1,0:T(8,128)(2,1)S(1)}, u32[]{:S(2)}, u32[]{:S(2)}) async-start(bf16[8,2,16,1280]{3,2,1,0:T(8,128)(2,1)} %copy.39), calls=%async_computation | async-start | bytes 1310720 | tf_op jit(solution)/shard_map/all_to_all | solution.py:116
  9.9 0.2 reduce-window.9
  10.2 0.1 copy.38
  10.6 16.7 %all-to-all-done = bf16[8,2,16,1280]{3,2,1,0:T(8,128)(2,1)S(1)} async-done(((bf16[8,2,16,1280]{3,2,1,0:T(8,128)(2,1)}), bf16[8,2,16,1280]{3,2,1,0:T(8,128)(2,1)S(1)}, u32[]{:S(2)}, u32[]{:S(2)}) %all-to-all-start) | async-done | bytes 655392 | tf_op jit(solution)/shard_map/all_to_all | solution.py:116
  27.2 0.6 gather_fusion
  27.9 0.6 gather_fusion.1
  28.5 1.2 copy_select_fusion
  29.8 3.8 %all-to-all-start.1 = ((bf16[8,2,2,16,1280]{4,3,1,2,0:T(8,128)(2,1)}), bf16[8,2,2,16,1280]{4,3,1,2,0:T(8,128)(2,1)S(1)}, u32[]{:S(2)}, u32[]{:S(2)}) async-start(bf16[8,2,2,16,1280]{4,3,1,2,0:T(8,128)(2,1)} %copy_select_fusion), calls=%async_computation.1 | async-start | bytes 2621440 | tf_op jit(solution)/shard_map/all_to_all | solution.py:120
  33.5 0.6 dynamic_slice.3
  34.2 0.6 add_subtract_fusion
  34.9 0.8 copy.43.tok_slot_ref
  35.7 0.3 fusion
  36.1 29.1 %all-to-all-done.1 = bf16[8,2,2,16,1280]{4,3,1,2,0:T(8,128)(2,1)S(1)} async-done(((bf16[8,2,2,16,1280]{4,3,1,2,0:T(8,128)(2,1)}), bf16[8,2,2,16,1280]{4,3,1,2,0:T(8,128)(2,1)S(1)}, u32[]{:S(2)}, u32[]{:S(2)}) %all-to-all-start.1) | async-done | bytes 1310752 | tf_op jit(solution)/shard_map/all_to_all | solution.py:120
  65.1 0.1 copy.42
  65.2 1.0 fusion.9
  66.2 0.2 multiply_reduce_fusion
  66.4 5.7 %all-reduce = (f32[480]{0:T(512)S(1)}, f32[256]{0:T(256)S(1)}) all-reduce(f32[480]{0:T(512)S(1)} %fusion, f32[256]{0:T(256)S(1)} %bitcast.57), channel_id=1, replica_groups=mesh['seq'=8,'mp'=4] {'mp'}, use_global_device_ids=true, to_apply=%region_4.5 | all-reduce | flops 736 | bytes 5888 | tf_op jit(solution)/shard_map/psum | solution.py:111
  72.1 1.4 fusion.2.q_ref
  73.5 1.0 fusion.4.k_ref
  74.5 11.9 %shard_map.86 = (bf16[480,1280]{1,0:T(8,128)(2,1)}, f32[256,1280]{1,0:T(8,128)}, f32[256,1280]{1,0:T(8,128)}) custom-call(s32[480,1]{1,0:T(8,128)} %copy.43.tok_slot_ref, bf16[480,1280]{1,0:T(8,128)(2,1)} %fusion.2.q_ref, bf16[256,1280]{1,0:T(8,128)(2,1)} %fusion.4.k_ref, bf16[256,1280]{1,0:T(8,128)(2,1)} %bitcast.52, bf16[480,1280]{1,0:T(8,128)(2,1)} %g_ref.1), custom_call_target="tpu_custom_call" | custom-call | tf_op jit(solution)/shard_map/pallas_call | solution.py:78
  86.4 1.5 %convert.9 = bf16[256,1280]{1,0:T(8,128)(2,1)S(1)} convert(f32[256,1280]{1,0:T(8,128)} %get-tuple-element.6) | non-fusion elementwise | flops 327680 | bytes 1966080 | tf_op jit(solution)/shard_map/convert.4
  87.9 0.2 copy-done.1
  88.2 1.2 copy_bitcast_fusion
  89.4 4.8 %all-to-all-start.2 = ((bf16[8,2,2,16,1280]{4,3,2,1,0:T(8,128)(2,1)}), bf16[8,2,2,16,1280]{4,3,2,1,0:T(8,128)(2,1)S(1)}, u32[]{:S(2)}, u32[]{:S(2)}) async-start(bf16[8,2,2,16,1280]{4,3,2,1,0:T(8,128)(2,1)} %copy_bitcast_fusion), calls=%async_computation.2 | async-start | bytes 2621440 | tf_op jit(solution)/shard_map/all_to_all | solution.py:133
  94.6 30.1 %all-to-all-done.2 = bf16[8,2,2,16,1280]{4,3,2,1,0:T(8,128)(2,1)S(1)} async-done(((bf16[8,2,2,16,1280]{4,3,2,1,0:T(8,128)(2,1)}), bf16[8,2,2,16,1280]{4,3,2,1,0:T(8,128)(2,1)S(1)}, u32[]{:S(2)}, u32[]{:S(2)}) %all-to-all-start.2) | async-done | bytes 1310752 | tf_op jit(solution)/shard_map/all_to_all | solution.py:133
  124.8 0.6 reshape.166
  125.4 0.5 convolution_convert_fusion
  125.9 0.6 gather_fusion.2
  126.5 0.2 select_select_fusion
  126.7 21.0 %all_to_all.20 = bf16[8,2,16,1280]{3,2,1,0:T(8,128)(2,1)S(1)} all-to-all(bf16[8,2,16,1280]{3,2,1,0:T(8,128)(2,1)S(1)} %select_select_fusion), channel_id=1, replica_groups=mesh['seq'=8,'mp'=4] {'seq'}, dimensions={0} | all-to-all | bytes 1310720 | tf_op jit(solution)/shard_map/all_to_all | solution.py:144
  147.7 0.9 copy.47
  (39 shorter events, 1.0 us)
Async XLA Ops:
  0.6 9.3 %copy-start.4 = (s32[3]{0:T(128)S(1)}, s32[3]{0:T(128)}, u32[]{:S(2)}) copy-start(s32[3]{0:T(128)} %param.12) | copy-start | bytes 40
  0.6 9.9 %copy-start.5 = (s32[3]{0:T(128)S(1)}, s32[3]{0:T(128)}, u32[]{:S(2)}) copy-start(s32[3]{0:T(128)} %param.13) | copy-start | bytes 40
  2.6 24.6 %all-to-all-start = ((bf16[8,2,16,1280]{3,2,1,0:T(8,128)(2,1)}), bf16[8,2,16,1280]{3,2,1,0:T(8,128)(2,1)S(1)}, u32[]{:S(2)}, u32[]{:S(2)}) async-start(bf16[8,2,16,1280]{3,2,1,0:T(8,128)(2,1)} %copy.39), calls=%async_computation | async-start | bytes 1310720 | tf_op jit(solution)/shard_map/all_to_all | solution.py:116
  29.8 6.0 %copy-start = (bf16[480,1280]{1,0:T(8,128)(2,1)S(1)}, bf16[480,1280]{1,0:T(8,128)(2,1)}, u32[]{:S(2)}) copy-start(bf16[480,1280]{1,0:T(8,128)(2,1)} %param.7) | copy-start | bytes 3686404
  29.8 35.3 %all-to-all-start.1 = ((bf16[8,2,2,16,1280]{4,3,1,2,0:T(8,128)(2,1)}), bf16[8,2,2,16,1280]{4,3,1,2,0:T(8,128)(2,1)S(1)}, u32[]{:S(2)}, u32[]{:S(2)}) async-start(bf16[8,2,2,16,1280]{4,3,1,2,0:T(8,128)(2,1)} %copy_select_fusion), calls=%async_computation.1 | async-start | bytes 2621440 | tf_op jit(solution)/shard_map/all_to_all | solution.py:120
  65.2 6.9 %copy-start.2 = (f32[1280]{0:T(1024)S(1)}, f32[1280]{0:T(1024)}, u32[]{:S(2)}) copy-start(f32[1280]{0:T(1024)} %param.8) | copy-start | bytes 15364
  66.4 7.1 %copy-start.3 = (f32[1280]{0:T(1024)S(1)}, f32[1280]{0:T(1024)}, u32[]{:S(2)}) copy-start(f32[1280]{0:T(1024)} %param.10) | copy-start | bytes 15364
  86.4 1.7 %copy-start.1 = (f32[256,1280]{1,0:T(8,128)S(1)}, f32[256,1280]{1,0:T(8,128)}, u32[]{:S(2)}) copy-start(f32[256,1280]{1,0:T(8,128)} %get-tuple-element.7) | copy-start | bytes 3932164
  89.4 35.4 %all-to-all-start.2 = ((bf16[8,2,2,16,1280]{4,3,2,1,0:T(8,128)(2,1)}), bf16[8,2,2,16,1280]{4,3,2,1,0:T(8,128)(2,1)S(1)}, u32[]{:S(2)}, u32[]{:S(2)}) async-start(bf16[8,2,2,16,1280]{4,3,2,1,0:T(8,128)(2,1)} %copy_bitcast_fusion), calls=%async_computation.2 | async-start | bytes 2621440 | tf_op jit(solution)/shard_map/all_to_all | solution.py:133

commit v6 on v4

--- a/solution.py
+++ b/solution.py
@@ -63,10 +63,11 @@
         gs1 = jnp.where(in_first, zero, grad_scores)
         w0 = jnp.where(in_first, weights_low, zero)
         w1 = jnp.where(in_first, zero, weights_low)
-        dk_ref[:depth, cols] = lax.dot_general(gs0, q, tn, preferred_element_type=jnp.float32)
-        dk_ref[depth:, cols] = lax.dot_general(gs1, q, tn, preferred_element_type=jnp.float32)
-        dv_ref[:depth, cols] = lax.dot_general(w0, g, tn, preferred_element_type=jnp.float32)
-        dv_ref[depth:, cols] = lax.dot_general(w1, g, tn, preferred_element_type=jnp.float32)
+        low = dk_ref.dtype
+        dk_ref[:depth, cols] = lax.dot_general(gs0, q, tn, preferred_element_type=jnp.float32).astype(low)
+        dk_ref[depth:, cols] = lax.dot_general(gs1, q, tn, preferred_element_type=jnp.float32).astype(low)
+        dv_ref[:depth, cols] = lax.dot_general(w0, g, tn, preferred_element_type=jnp.float32).astype(low)
+        dv_ref[depth:, cols] = lax.dot_general(w1, g, tn, preferred_element_type=jnp.float32).astype(low)
 
 
 def attend(tok_slot, query_normed, keys, values, grad_out):
@@ -88,8 +89,8 @@
         out_specs=[tok_spec, key_spec, key_spec],
         out_shape=[
             jax.ShapeDtypeStruct((tok_rows, feat_width), jnp.bfloat16),
-            jax.ShapeDtypeStruct((key_rows, feat_width), jnp.float32),
-            jax.ShapeDtypeStruct((key_rows, feat_width), jnp.float32),
+            jax.ShapeDtypeStruct((key_rows, feat_width), jnp.bfloat16),
+            jax.ShapeDtypeStruct((key_rows, feat_width), jnp.bfloat16),
         ],
         compiler_params=pltpu.CompilerParams(dimension_semantics=("arbitrary",)),
     )(tok_slot, query_normed, keys, values, grad_out)
@@ -119,9 +120,8 @@
     own_slab = jnp.stack([own_key_normed, cond[0, 1]])
     spread = own_slab.reshape(2, seq_count, piece, feat_width).transpose(1, 0, 2, 3)
     gathered = lax.all_to_all(spread, "seq", 0, 0, tiled=True)
-    clip_rows = jnp.take(gathered, clip_owner, axis=0)
     slot_clip = jnp.stack([device_first, device_first + 1], axis=1)
-    wanted = jnp.take(clip_rows, jnp.minimum(slot_clip, clip_count - 1), axis=0)
+    wanted = jnp.take(gathered, clip_owner[jnp.minimum(slot_clip, clip_count - 1)], axis=0)
     arrived = lax.all_to_all(wanted, "seq", 0, 0, tiled=True)
     mine = arrived.transpose(1, 2, 0, 3, 4).reshape(2, 2, cond_depth, feat_width)
     keys = mine[:, 0].reshape(2 * cond_depth, feat_width)
@@ -130,7 +130,7 @@
     grad_query, key_grad, value_grad = attend(tok_slot[:, None], query_normed, keys, values, grad_out)
     partial = jnp.stack(
         [key_grad.reshape(2, cond_depth, feat_width), value_grad.reshape(2, cond_depth, feat_width)], axis=1
-    ).astype(jnp.bfloat16)
+    )
     spread_grads = partial.reshape(2, 2, seq_count, piece, feat_width).transpose(2, 0, 1, 3, 4)
     pieces = lax.all_to_all(spread_grads, "seq", 0, 0, tiled=True)
     source_clip = slot_clip.reshape(2 * seq_count)

time: 147 us -> 146 us (level)
    another operation x3 -> x1, other arithmetic: 1.73 us -> 0.18 us
  transfers between devices with their start and end apart: 3 -> 3, of which waited for: 3 -> 3; matrix products, arithmetic and copies ran while one was open for 3% -> 4% of each run, Pallas kernels for 0% -> 0%
where the time goes in v6:
time: 146 us; the launch traced here: 145 us
  waiting for transfers between devices  72.7 us (50%)
  blocking collectives  29.6 us (20%)
  starting transfers between devices  13.2 us (9%)
  Pallas kernels  11.9 us (8%)
  other arithmetic  9.39 us (6%)
  local copies, waits for them, and re-layouts  7.16 us (5%)
    all_to_all x1, waiting for transfers between devices, local(): pieces = lax.all_to_all(spread_grads, 'seq', 0, 0, tiled=True)  31 us
    all_to_all x1, waiting for transfers between devices, local(): arrived = lax.all_to_all(wanted, 'seq', 0, 0, tiled=True)  27.1 us
    all_to_all x1, blocking collectives, local(): returned = lax.all_to_all(outgoing, 'seq', 0, 0, tiled=True)  21.3 us
    all_to_all x1, waiting for transfers between devices, local(): gathered = lax.all_to_all(spread, 'seq', 0, 0, tiled=True)  14.5 us
    pallas_call x1, Pallas kernels, attend(): pl.pallas_call(attend_kernel, grid=(feat_width // step_width,), in_specs=...  11.9 us
    psum x1, blocking collectives, local(): lax.psum((jnp.sum(query_wide * query_wide, axis=1), jnp.sum(own_key * own...  8.34 us
    all_to_all x1, starting transfers between devices, local(): gathered = lax.all_to_all(spread, 'seq', 0, 0, tiled=True)  5.83 us
    all_to_all x1, starting transfers between devices, local(): arrived = lax.all_to_all(wanted, 'seq', 0, 0, tiled=True)  3.77 us
  transfers between devices with their start and end apart: 3, of which 3 were waited for; matrix products, arithmetic and copies ran while one was open for 4% of the time, Pallas kernels for 0%

profile of v6, /device:TPU:0, one launch (start us, length us, event | category | flops | bytes accessed | tf_op | source)
XLA Modules:
  0.0 145.1 jit_solution(15677843774111095700)
XLA Ops:
  0.7 1.3 slice_convert_fusion
  1.9 0.1 multiply_reduce_fusion
  2.1 0.2 copy-done.1
  2.3 0.3 fusion
  2.6 8.3 %all-reduce = (f32[480]{0:T(512)S(1)}, f32[128]{0:T(128)S(1)}) all-reduce(f32[480]{0:T(512)S(1)} %fusion, f32[128]{0:T(128)S(1)} %multiply_reduce_fusion), channel_id=1, replica_groups=mesh['seq'=8,'mp'=4] {'mp'}, use_global_device_ids=true, to_apply=%region_4.5 | all-reduce | flops 608 | bytes 4864 | tf_op jit(solution)/shard_map/psum | solution.py:113
  11.1 0.1 multiply_convert_fusion
  11.2 0.9 maximum_bitcast_fusion
  12.1 5.8 %all-to-all-start = ((bf16[8,2,16,1280]{3,2,1,0:T(8,128)(2,1)}), bf16[8,2,16,1280]{3,2,1,0:T(8,128)(2,1)S(1)}, u32[]{:S(2)}, u32[]{:S(2)}) async-start(bf16[8,2,16,1280]{3,2,1,0:T(8,128)(2,1)} %maximum_bitcast_fusion), calls=%async_computation | async-start | bytes 1310720 | tf_op jit(solution)/shard_map/all_to_all | solution.py:122
  18.0 0.2 reduce-window.9
  18.4 0.7 gather_fusion
  19.6 14.5 %all-to-all-done = bf16[8,2,16,1280]{3,2,1,0:T(8,128)(2,1)S(1)} async-done(((bf16[8,2,16,1280]{3,2,1,0:T(8,128)(2,1)}), bf16[8,2,16,1280]{3,2,1,0:T(8,128)(2,1)S(1)}, u32[]{:S(2)}, u32[]{:S(2)}) %all-to-all-start) | async-done | bytes 655392 | tf_op jit(solution)/shard_map/all_to_all | solution.py:122
  34.1 0.6 gather_fusion.1
  34.7 1.3 copy_select_fusion
  36.0 3.8 %all-to-all-start.1 = ((bf16[8,2,2,16,1280]{4,3,1,2,0:T(8,128)(2,1)}), bf16[8,2,2,16,1280]{4,3,1,2,0:T(8,128)(2,1)S(1)}, u32[]{:S(2)}, u32[]{:S(2)}) async-start(bf16[8,2,2,16,1280]{4,3,1,2,0:T(8,128)(2,1)} %copy_select_fusion), calls=%async_computation.1 | async-start | bytes 2621440 | tf_op jit(solution)/shard_map/all_to_all | solution.py:125
  39.8 0.6 dynamic_slice.3
  40.4 0.1 convert_reduce_fusion
  40.5 0.6 add_subtract_fusion
  41.1 0.8 copy.60.tok_slot_ref
  42.0 1.4 fusion.2.q_ref
  43.4 27.1 %all-to-all-done.1 = bf16[8,2,2,16,1280]{4,3,1,2,0:T(8,128)(2,1)S(1)} async-done(((bf16[8,2,2,16,1280]{4,3,1,2,0:T(8,128)(2,1)}), bf16[8,2,2,16,1280]{4,3,1,2,0:T(8,128)(2,1)S(1)}, u32[]{:S(2)}, u32[]{:S(2)}) %all-to-all-start.1) | async-done | bytes 1310752 | tf_op jit(solution)/shard_map/all_to_all | solution.py:125
  70.5 0.1 copy.59
  70.6 1.1 fusion.7
  71.8 11.9 %shard_map.86 = (bf16[480,1280]{1,0:T(8,128)(2,1)}, bf16[256,1280]{1,0:T(8,128)(2,1)}, bf16[256,1280]{1,0:T(8,128)(2,1)}) custom-call(s32[480,1]{1,0:T(8,128)} %copy.60.tok_slot_ref, bf16[480,1280]{1,0:T(8,128)(2,1)} %fusion.2.q_ref, bf16[256,1280]{1,0:T(8,128)(2,1)} %bitcast.48, bf16[256,1280]{1,0:T(8,128)(2,1)} %bitcast.47, bf16[480,1280]{1,0:T(8,128)(2,1)} %g_ref.1), custom_call_target="tpu_custom_call" | custom-call | tf_op jit(solution)/shard_map/pallas_call | solution.py:79
  83.6 2.5 %copy_bitcast_fusion = bf16[8,2,2,16,1280]{4,3,2,1,0:T(8,128)(2,1)} fusion(bf16[2,1,8,16,1280]{4,3,2,0,1:T(8,128)(2,1)} %bitcast.52, bf16[2,1,8,16,1280]{4,3,2,0,1:T(8,128)(2,1)} %bitcast.51), kind=kLoop, calls=%fused_computation.10 | loop fusion | flops 655360 | bytes 2621440 | tf_op jit(solution)/shard_map/transpose | solution.py:134
  86.1 3.6 %all-to-all-start.2 = ((bf16[8,2,2,16,1280]{4,3,2,1,0:T(8,128)(2,1)}), bf16[8,2,2,16,1280]{4,3,2,1,0:T(8,128)(2,1)S(1)}, u32[]{:S(2)}, u32[]{:S(2)}) async-start(bf16[8,2,2,16,1280]{4,3,2,1,0:T(8,128)(2,1)} %copy_bitcast_fusion), calls=%async_computation.2 | async-start | bytes 2621440 | tf_op jit(solution)/shard_map/all_to_all | solution.py:135
  90.1 31.0 %all-to-all-done.2 = bf16[8,2,2,16,1280]{4,3,2,1,0:T(8,128)(2,1)S(1)} async-done(((bf16[8,2,2,16,1280]{4,3,2,1,0:T(8,128)(2,1)}), bf16[8,2,2,16,1280]{4,3,2,1,0:T(8,128)(2,1)S(1)}, u32[]{:S(2)}, u32[]{:S(2)}) %all-to-all-start.2) | async-done | bytes 1310752 | tf_op jit(solution)/shard_map/all_to_all | solution.py:135
  121.1 0.6 reshape.207
  121.7 0.5 convolution_convert_fusion
  122.2 0.6 gather_fusion.2
  122.8 0.2 select_select_fusion
  123.0 21.3 %all_to_all.20 = bf16[8,2,16,1280]{3,2,1,0:T(8,128)(2,1)S(1)} all-to-all(bf16[8,2,16,1280]{3,2,1,0:T(8,128)(2,1)S(1)} %select_select_fusion), channel_id=1, replica_groups=mesh['seq'=8,'mp'=4] {'seq'}, dimensions={0} | all-to-all | bytes 1310720 | tf_op jit(solution)/shard_map/all_to_all | solution.py:146
  144.3 0.9 copy.64
  (41 shorter events, 1.2 us)
Async XLA Ops:
  0.6 1.3 copy-start.2
  0.6 1.7 %copy-start.1 = (bf16[480,1280]{1,0:T(8,128)(2,1)S(1)}, bf16[480,1280]{1,0:T(8,128)(2,1)}, u32[]{:S(2)}) copy-start(bf16[480,1280]{1,0:T(8,128)(2,1)} %param.7) | copy-start | bytes 3686404
  0.6 10.4 %copy-start.3 = (f32[1280]{0:T(1024)S(1)}, f32[1280]{0:T(1024)}, u32[]{:S(2)}) copy-start(f32[1280]{0:T(1024)} %param.10) | copy-start | bytes 15364
  11.2 6.8 %copy-start.5 = (s32[3]{0:T(128)S(1)}, s32[3]{0:T(128)}, u32[]{:S(2)}) copy-start(s32[3]{0:T(128)} %param.12) | copy-start | bytes 40
  11.2 7.2 %copy-start = (s32[3]{0:T(128)S(1)}, s32[3]{0:T(128)}, u32[]{:S(2)}) copy-start(s32[3]{0:T(128)} %param.13) | copy-start | bytes 40
  12.1 22.0 %all-to-all-start = ((bf16[8,2,16,1280]{3,2,1,0:T(8,128)(2,1)}), bf16[8,2,16,1280]{3,2,1,0:T(8,128)(2,1)S(1)}, u32[]{:S(2)}, u32[]{:S(2)}) async-start(bf16[8,2,16,1280]{3,2,1,0:T(8,128)(2,1)} %maximum_bitcast_fusion), calls=%async_computation | async-start | bytes 1310720 | tf_op jit(solution)/shard_map/all_to_all | solution.py:122
  36.0 6.0 %copy-start.4 = (f32[1280]{0:T(1024)S(1)}, f32[1280]{0:T(1024)}, u32[]{:S(2)}) copy-start(f32[1280]{0:T(1024)} %param.8) | copy-start | bytes 15364
  36.0 34.5 %all-to-all-start.1 = ((bf16[8,2,2,16,1280]{4,3,1,2,0:T(8,128)(2,1)}), bf16[8,2,2,16,1280]{4,3,1,2,0:T(8,128)(2,1)S(1)}, u32[]{:S(2)}, u32[]{:S(2)}) async-start(bf16[8,2,2,16,1280]{4,3,1,2,0:T(8,128)(2,1)} %copy_select_fusion), calls=%async_computation.1 | async-start | bytes 2621440 | tf_op jit(solution)/shard_map/all_to_all | solution.py:125
  86.1 34.9 %all-to-all-start.2 = ((bf16[8,2,2,16,1280]{4,3,2,1,0:T(8,128)(2,1)}), bf16[8,2,2,16,1280]{4,3,2,1,0:T(8,128)(2,1)S(1)}, u32[]{:S(2)}, u32[]{:S(2)}) async-start(bf16[8,2,2,16,1280]{4,3,2,1,0:T(8,128)(2,1)} %copy_bitcast_fusion), calls=%async_computation.2 | async-start | bytes 2621440 | tf_op jit(solution)/shard_map/all_to_all | solution.py:135

commit v7 on v6

--- a/solution.py
+++ b/solution.py
@@ -18,20 +18,22 @@
 HEADS_PER_STEP = 2
 
 
-def attend_kernel(tok_slot_ref, q_ref, k_ref, v_ref, g_ref, dq_ref, dk_ref, dv_ref):
+def attend_kernel(tok_slot_ref, q_ref, kv_ref, g_ref, dq_ref, dkv_ref):
     score_scale = 1.0 / math.sqrt(HEAD_DIM)
-    depth = k_ref.shape[0] // 2
+    holders, _, _, piece, _ = kv_ref.shape
+    depth = holders * piece
     in_first = tok_slot_ref[...] == 0
     nt = (((1,), (1,)), ((), ()))
     tn = (((0,), (0,)), ((), ()))
+    low = dkv_ref.dtype
     for head in range(HEADS_PER_STEP):
         cols = slice(head * HEAD_DIM, (head + 1) * HEAD_DIM)
         q = q_ref[:, cols]
         g = g_ref[:, cols]
-        k0 = k_ref[:depth, cols]
-        k1 = k_ref[depth:, cols]
-        v0 = v_ref[:depth, cols]
-        v1 = v_ref[depth:, cols]
+        k0 = kv_ref[:, 0, 0, :, cols].reshape(depth, HEAD_DIM)
+        k1 = kv_ref[:, 1, 0, :, cols].reshape(depth, HEAD_DIM)
+        v0 = kv_ref[:, 0, 1, :, cols].reshape(depth, HEAD_DIM)
+        v1 = kv_ref[:, 1, 1, :, cols].reshape(depth, HEAD_DIM)
         scores = jnp.where(
             in_first,
             lax.dot_general(q, k0, nt, preferred_element_type=jnp.float32),
@@ -63,37 +65,34 @@
         gs1 = jnp.where(in_first, zero, grad_scores)
         w0 = jnp.where(in_first, weights_low, zero)
         w1 = jnp.where(in_first, zero, weights_low)
-        low = dk_ref.dtype
-        dk_ref[:depth, cols] = lax.dot_general(gs0, q, tn, preferred_element_type=jnp.float32).astype(low)
-        dk_ref[depth:, cols] = lax.dot_general(gs1, q, tn, preferred_element_type=jnp.float32).astype(low)
-        dv_ref[:depth, cols] = lax.dot_general(w0, g, tn, preferred_element_type=jnp.float32).astype(low)
-        dv_ref[depth:, cols] = lax.dot_general(w1, g, tn, preferred_element_type=jnp.float32).astype(low)
+        for slot, (gs, w) in enumerate(((gs0, w0), (gs1, w1))):
+            dk = lax.dot_general(gs, q, tn, preferred_element_type=jnp.float32).astype(low)
+            dv = lax.dot_general(w, g, tn, preferred_element_type=jnp.float32).astype(low)
+            dkv_ref[:, slot, 0, :, cols] = dk.reshape(holders, piece, HEAD_DIM)
+            dkv_ref[:, slot, 1, :, cols] = dv.reshape(holders, piece, HEAD_DIM)
 
 
-def attend(tok_slot, query_normed, keys, values, grad_out):
+def attend(tok_slot, query_normed, kv, grad_out):
     tok_rows, feat_width = query_normed.shape
-    key_rows = keys.shape[0]
     step_width = HEADS_PER_STEP * HEAD_DIM
     tok_spec = pl.BlockSpec((tok_rows, step_width), lambda h: (0, h))
-    key_spec = pl.BlockSpec((key_rows, step_width), lambda h: (0, h))
+    kv_spec = pl.BlockSpec(kv.shape[:4] + (step_width,), lambda h: (0, 0, 0, 0, h))
     return pl.pallas_call(
         attend_kernel,
         grid=(feat_width // step_width,),
         in_specs=[
             pl.BlockSpec((tok_rows, 1), lambda h: (0, 0)),
             tok_spec,
-            key_spec,
-            key_spec,
+            kv_spec,
             tok_spec,
         ],
-        out_specs=[tok_spec, key_spec, key_spec],
+        out_specs=[tok_spec, kv_spec],
         out_shape=[
             jax.ShapeDtypeStruct((tok_rows, feat_width), jnp.bfloat16),
-            jax.ShapeDtypeStruct((key_rows, feat_width), jnp.bfloat16),
-            jax.ShapeDtypeStruct((key_rows, feat_width), jnp.bfloat16),
+            jax.ShapeDtypeStruct(kv.shape, jnp.bfloat16),
         ],
         compiler_params=pltpu.CompilerParams(dimension_semantics=("arbitrary",)),
-    )(tok_slot, query_normed, keys, values, grad_out)
+    )(tok_slot, query_normed, kv, grad_out)
 
 
 def local(query, query_gain, cond, key_gain, grad_out, clip_len, clip_owner, seq_count):
@@ -123,15 +122,13 @@
     slot_clip = jnp.stack([device_first, device_first + 1], axis=1)
     wanted = jnp.take(gathered, clip_owner[jnp.minimum(slot_clip, clip_count - 1)], axis=0)
     arrived = lax.all_to_all(wanted, "seq", 0, 0, tiled=True)
-    mine = arrived.transpose(1, 2, 0, 3, 4).reshape(2, 2, cond_depth, feat_width)
-    keys = mine[:, 0].reshape(2 * cond_depth, feat_width)
-    values = mine[:, 1].reshape(2 * cond_depth, feat_width)
     tok_slot = clip_of - device_first[my_index]
-    grad_query, key_grad, value_grad = attend(tok_slot[:, None], query_normed, keys, values, grad_out)
-    partial = jnp.stack(
-        [key_grad.reshape(2, cond_depth, feat_width), value_grad.reshape(2, cond_depth, feat_width)], axis=1
-    )
-    spread_grads = partial.reshape(2, 2, seq_count, piece, feat_width).transpose(2, 0, 1, 3, 4)
+    if piece % 16 == 0:
+        grad_query, spread_grads = attend(tok_slot[:, None], query_normed, arrived, grad_out)
+    else:
+        mine = arrived.transpose(1, 2, 0, 3, 4).reshape(1, 2, 2, cond_depth, feat_width)
+        grad_query, grad_slots = attend(tok_slot[:, None], query_normed, mine, grad_out)
+        spread_grads = grad_slots[0].reshape(2, 2, seq_count, piece, feat_width).transpose(2, 0, 1, 3, 4)
     pieces = lax.all_to_all(spread_grads, "seq", 0, 0, tiled=True)
     source_clip = slot_clip.reshape(2 * seq_count)
     onehot = (source_clip[:, None] == jnp.arange(clip_count, dtype=jnp.int32)[None, :]).astype(jnp.bfloat16)

time: 146 us -> 143 us (0.979)
  other arithmetic: 9.39 us -> 6.88 us
    transpose x1 -> x0, other arithmetic: 2.52 us -> none  [local(): partial.reshape(2, 2, seq_count, piece, feat_width).transpose(2, 0, 1, 3, 4)]
where the time goes in v7:
time: 143 us; the launch traced here: 142 us
  waiting for transfers between devices  72.7 us (51%)
  blocking collectives  29.6 us (21%)
  starting transfers between devices  13.2 us (9%)
  Pallas kernels  11.8 us (8%)
  local copies, waits for them, and re-layouts  6.98 us (5%)
  other arithmetic  6.88 us (5%)
    all_to_all x1, waiting for transfers between devices, local(): pieces = lax.all_to_all(spread_grads, 'seq', 0, 0, tiled=True)  31 us
    all_to_all x1, waiting for transfers between devices, local(): arrived = lax.all_to_all(wanted, 'seq', 0, 0, tiled=True)  27.1 us
    all_to_all x1, blocking collectives, local(): returned = lax.all_to_all(outgoing, 'seq', 0, 0, tiled=True)  21.3 us
    all_to_all x1, waiting for transfers between devices, local(): gathered = lax.all_to_all(spread, 'seq', 0, 0, tiled=True)  14.5 us
    pallas_call x1, Pallas kernels, attend(): pl.pallas_call(attend_kernel, grid=(feat_width // step_width,), in_specs=...  11.8 us
    psum x1, blocking collectives, local(): lax.psum((jnp.sum(query_wide * query_wide, axis=1), jnp.sum(own_key * own...  8.34 us
    all_to_all x1, starting transfers between devices, local(): gathered = lax.all_to_all(spread, 'seq', 0, 0, tiled=True)  5.83 us
    all_to_all x1, starting transfers between devices, local(): arrived = lax.all_to_all(wanted, 'seq', 0, 0, tiled=True)  3.77 us
  transfers between devices with their start and end apart: 3, of which 3 were waited for; matrix products, arithmetic and copies ran while one was open for 4% of the time, Pallas kernels for 0%

profile of v7, /device:TPU:0, one launch (start us, length us, event | category | flops | bytes accessed | tf_op | source)
XLA Modules:
  0.0 142.4 jit_solution(4528073815225783945)
XLA Ops:
  0.7 1.3 slice_convert_fusion
  1.9 0.1 multiply_reduce_fusion
  2.1 0.2 copy-done.2
  2.3 0.3 fusion
  2.6 8.3 %all-reduce = (f32[480]{0:T(512)S(1)}, f32[128]{0:T(128)S(1)}) all-reduce(f32[480]{0:T(512)S(1)} %fusion, f32[128]{0:T(128)S(1)} %multiply_reduce_fusion), channel_id=1, replica_groups=mesh['seq'=8,'mp'=4] {'mp'}, use_global_device_ids=true, to_apply=%region_4.5 | all-reduce | flops 608 | bytes 4864 | tf_op jit(solution)/shard_map/psum | solution.py:112
  11.1 0.1 multiply_convert_fusion
  11.2 0.9 maximum_bitcast_fusion
  12.1 5.8 %all-to-all-start = ((bf16[8,2,16,1280]{3,2,1,0:T(8,128)(2,1)}), bf16[8,2,16,1280]{3,2,1,0:T(8,128)(2,1)S(1)}, u32[]{:S(2)}, u32[]{:S(2)}) async-start(bf16[8,2,16,1280]{3,2,1,0:T(8,128)(2,1)} %maximum_bitcast_fusion), calls=%async_computation | async-start | bytes 1310720 | tf_op jit(solution)/shard_map/all_to_all | solution.py:121
  18.0 0.2 reduce-window.9
  18.2 0.1 convert_reduce_fusion.1
  18.4 0.7 gather_fusion
  19.6 14.5 %all-to-all-done = bf16[8,2,16,1280]{3,2,1,0:T(8,128)(2,1)S(1)} async-done(((bf16[8,2,16,1280]{3,2,1,0:T(8,128)(2,1)}), bf16[8,2,16,1280]{3,2,1,0:T(8,128)(2,1)S(1)}, u32[]{:S(2)}, u32[]{:S(2)}) %all-to-all-start) | async-done | bytes 655392 | tf_op jit(solution)/shard_map/all_to_all | solution.py:121
  34.1 0.6 gather_fusion.1
  34.7 1.2 broadcast_select_fusion
  36.0 3.8 %all-to-all-start.1 = ((bf16[8,2,2,16,1280]{4,3,2,1,0:T(8,128)(2,1)}), bf16[8,2,2,16,1280]{4,3,2,1,0:T(8,128)(2,1)S(1)}, u32[]{:S(2)}, u32[]{:S(2)}) async-start(bf16[8,2,2,16,1280]{4,3,2,1,0:T(8,128)(2,1)} %broadcast_select_fusion), calls=%async_computation.1 | async-start | bytes 2621440 | tf_op jit(solution)/shard_map/all_to_all | solution.py:124
  39.8 0.6 dynamic_slice.3
  40.4 0.1 convert_reduce_fusion
  40.4 0.6 add_subtract_fusion
  41.1 0.8 copy.37.tok_slot_ref
  41.9 1.4 fusion.2.q_ref
  43.4 27.1 %all-to-all-done.1.kv_ref = bf16[8,2,2,16,1280]{4,3,2,1,0:T(8,128)(2,1)S(1)} async-done(((bf16[8,2,2,16,1280]{4,3,2,1,0:T(8,128)(2,1)}), bf16[8,2,2,16,1280]{4,3,2,1,0:T(8,128)(2,1)S(1)}, u32[]{:S(2)}, u32[]{:S(2)}) %all-to-all-start.1) | async-done | bytes 1310752 | tf_op jit(solution)/shard_map/all_to_all | solution.py:124
  70.5 1.1 copy-done.1
  71.5 11.8 %shard_map.86 = (bf16[480,1280]{1,0:T(8,128)(2,1)}, bf16[8,2,2,16,1280]{4,3,2,1,0:T(8,128)(2,1)}) custom-call(s32[480,1]{1,0:T(8,128)} %copy.37.tok_slot_ref, bf16[480,1280]{1,0:T(8,128)(2,1)} %fusion.2.q_ref, bf16[8,2,2,16,1280]{4,3,2,1,0:T(8,128)(2,1)} %copy-done.1, bf16[480,1280]{1,0:T(8,128)(2,1)} %g_ref.1), custom_call_target="tpu_custom_call" | custom-call | tf_op jit(solution)/shard_map/pallas_call | solution.py:80
  83.3 3.6 %all-to-all-start.2 = ((bf16[8,2,2,16,1280]{4,3,2,1,0:T(8,128)(2,1)}), bf16[8,2,2,16,1280]{4,3,2,1,0:T(8,128)(2,1)S(1)}, u32[]{:S(2)}, u32[]{:S(2)}) async-start(bf16[8,2,2,16,1280]{4,3,2,1,0:T(8,128)(2,1)} %get-tuple-element.5), calls=%async_computation.2 | async-start | bytes 2621440 | tf_op jit(solution)/shard_map/all_to_all | solution.py:132
  87.2 0.1 fusion.4
  87.3 31.0 %all-to-all-done.2 = bf16[8,2,2,16,1280]{4,3,2,1,0:T(8,128)(2,1)S(1)} async-done(((bf16[8,2,2,16,1280]{4,3,2,1,0:T(8,128)(2,1)}), bf16[8,2,2,16,1280]{4,3,2,1,0:T(8,128)(2,1)S(1)}, u32[]{:S(2)}, u32[]{:S(2)}) %all-to-all-start.2) | async-done | bytes 1310752 | tf_op jit(solution)/shard_map/all_to_all | solution.py:132
  118.3 0.6 reshape.198
  118.9 0.5 convolution_convert_fusion
  119.4 0.6 gather_fusion.2
  120.0 0.2 select_select_fusion
  120.2 21.3 %all_to_all.20 = bf16[8,2,16,1280]{3,2,1,0:T(8,128)(2,1)S(1)} all-to-all(bf16[8,2,16,1280]{3,2,1,0:T(8,128)(2,1)S(1)} %select_select_fusion), channel_id=1, replica_groups=mesh['seq'=8,'mp'=4] {'seq'}, dimensions={0} | all-to-all | bytes 1310720 | tf_op jit(solution)/shard_map/all_to_all | solution.py:143
  141.5 0.9 copy.39
  (40 shorter events, 1.1 us)
Async XLA Ops:
  0.6 1.3 copy-start.3
  0.6 1.7 %copy-start.2 = (bf16[480,1280]{1,0:T(8,128)(2,1)S(1)}, bf16[480,1280]{1,0:T(8,128)(2,1)}, u32[]{:S(2)}) copy-start(bf16[480,1280]{1,0:T(8,128)(2,1)} %param.7) | copy-start | bytes 3686404
  0.6 10.4 %copy-start.4 = (f32[1280]{0:T(1024)S(1)}, f32[1280]{0:T(1024)}, u32[]{:S(2)}) copy-start(f32[1280]{0:T(1024)} %param.10) | copy-start | bytes 15364
  11.2 6.8 %copy-start.6 = (s32[3]{0:T(128)S(1)}, s32[3]{0:T(128)}, u32[]{:S(2)}) copy-start(s32[3]{0:T(128)} %param.12) | copy-start | bytes 40
  11.2 7.2 %copy-start = (s32[3]{0:T(128)S(1)}, s32[3]{0:T(128)}, u32[]{:S(2)}) copy-start(s32[3]{0:T(128)} %param.13) | copy-start | bytes 40
  12.1 22.0 %all-to-all-start = ((bf16[8,2,16,1280]{3,2,1,0:T(8,128)(2,1)}), bf16[8,2,16,1280]{3,2,1,0:T(8,128)(2,1)S(1)}, u32[]{:S(2)}, u32[]{:S(2)}) async-start(bf16[8,2,16,1280]{3,2,1,0:T(8,128)(2,1)} %maximum_bitcast_fusion), calls=%async_computation | async-start | bytes 1310720 | tf_op jit(solution)/shard_map/all_to_all | solution.py:121
  36.0 6.0 %copy-start.5 = (f32[1280]{0:T(1024)S(1)}, f32[1280]{0:T(1024)}, u32[]{:S(2)}) copy-start(f32[1280]{0:T(1024)} %param.8) | copy-start | bytes 15364
  36.0 34.5 %all-to-all-start.1 = ((bf16[8,2,2,16,1280]{4,3,2,1,0:T(8,128)(2,1)}), bf16[8,2,2,16,1280]{4,3,2,1,0:T(8,128)(2,1)S(1)}, u32[]{:S(2)}, u32[]{:S(2)}) async-start(bf16[8,2,2,16,1280]{4,3,2,1,0:T(8,128)(2,1)} %broadcast_select_fusion), calls=%async_computation.1 | async-start | bytes 2621440 | tf_op jit(solution)/shard_map/all_to_all | solution.py:124
  70.5 1.1 copy-start.1
  83.3 35.0 %all-to-all-start.2 = ((bf16[8,2,2,16,1280]{4,3,2,1,0:T(8,128)(2,1)}), bf16[8,2,2,16,1280]{4,3,2,1,0:T(8,128)(2,1)S(1)}, u32[]{:S(2)}, u32[]{:S(2)}) async-start(bf16[8,2,2,16,1280]{4,3,2,1,0:T(8,128)(2,1)} %get-tuple-element.5), calls=%async_computation.2 | async-start | bytes 2621440 | tf_op jit(solution)/shard_map/all_to_all | solution.py:132

commit v8 on v7

--- a/solution.py
+++ b/solution.py
@@ -117,10 +117,10 @@
     key_scale = lax.rsqrt(sums[1] / D + EPS)
     own_key_normed = (own_key * key_scale[:, None] * key_gain).astype(jnp.bfloat16)
     own_slab = jnp.stack([own_key_normed, cond[0, 1]])
-    spread = own_slab.reshape(2, seq_count, piece, feat_width).transpose(1, 0, 2, 3)
-    gathered = lax.all_to_all(spread, "seq", 0, 0, tiled=True)
+    spread = own_slab.reshape(2, seq_count, piece, feat_width)
+    gathered = lax.all_to_all(spread, "seq", 1, 0, tiled=True).reshape(seq_count, 2, piece, feat_width)
     slot_clip = jnp.stack([device_first, device_first + 1], axis=1)
-    wanted = jnp.take(gathered, clip_owner[jnp.minimum(slot_clip, clip_count - 1)], axis=0)
+    wanted = jnp.take(gathered, clip_owner[jnp.minimum(slot_clip, clip_count - 1)], axis=0, mode="clip")
     arrived = lax.all_to_all(wanted, "seq", 0, 0, tiled=True)
     tok_slot = clip_of - device_first[my_index]
     if piece % 16 == 0:
@@ -138,10 +138,9 @@
     owns = clip_owner[None, :] == jnp.arange(seq_count, dtype=jnp.int32)[:, None]
     owned_clip = jnp.sum(jnp.where(owns, jnp.arange(clip_count, dtype=jnp.int32)[None, :], 0), axis=1)
     outgoing = jnp.where(
-        jnp.any(owns, axis=1)[:, None, None, None], jnp.take(summed, owned_clip, axis=0), jnp.zeros((), jnp.bfloat16)
+        jnp.any(owns, axis=1)[:, None, None, None], jnp.take(summed, owned_clip, axis=0, mode="clip"), jnp.zeros((), jnp.bfloat16)
     )
-    returned = lax.all_to_all(outgoing, "seq", 0, 0, tiled=True)
-    owned_grads = returned.transpose(1, 0, 2, 3).reshape(2, cond_depth, feat_width)
+    owned_grads = lax.all_to_all(outgoing, "seq", 0, 2, tiled=True).reshape(2, cond_depth, feat_width)
     return (grad_query, owned_grads[None])
 
 

time: 143 us -> 143 us (level)
  no operation moved by 1% of the time
where the time goes in v8:
time: 143 us; the launch traced here: 142 us
  waiting for transfers between devices  73.1 us (51%)
  blocking collectives  29.6 us (21%)
  starting transfers between devices  13.2 us (9%)
  Pallas kernels  11.8 us (8%)
  local copies, waits for them, and re-layouts  7.63 us (5%)
  other arithmetic  5.54 us (4%)
    all_to_all x1, waiting for transfers between devices, local(): pieces = lax.all_to_all(spread_grads, 'seq', 0, 0, tiled=True)  31 us
    all_to_all x1, waiting for transfers between devices, local(): arrived = lax.all_to_all(wanted, 'seq', 0, 0, tiled=True)  27.1 us
    all_to_all x1, blocking collectives, local(): lax.all_to_all(outgoing, 'seq', 0, 2, tiled=True)  21.3 us
    all_to_all x1, waiting for transfers between devices, local(): lax.all_to_all(spread, 'seq', 1, 0, tiled=True)  15 us
    pallas_call x1, Pallas kernels, attend(): pl.pallas_call(attend_kernel, grid=(feat_width // step_width,), in_specs=...  11.8 us
    psum x1, blocking collectives, local(): lax.psum((jnp.sum(query_wide * query_wide, axis=1), jnp.sum(own_key * own...  8.34 us
    all_to_all x1, starting transfers between devices, local(): lax.all_to_all(spread, 'seq', 1, 0, tiled=True)  5.83 us
    all_to_all x1, starting transfers between devices, local(): arrived = lax.all_to_all(wanted, 'seq', 0, 0, tiled=True)  3.77 us
  transfers between devices with their start and end apart: 3, of which 3 were waited for; matrix products, arithmetic and copies ran while one was open for 4% of the time, Pallas kernels for 0%

profile of v8, /device:TPU:0, one launch (start us, length us, event | category | flops | bytes accessed | tf_op | source)
XLA Modules:
  0.0 142.1 jit_solution(14380085470305647309)
XLA Ops:
  0.7 1.3 slice_convert_fusion
  1.9 0.1 multiply_reduce_fusion
  2.1 0.2 copy-done.2
  2.3 0.3 fusion
  2.6 8.3 %all-reduce = (f32[480]{0:T(512)S(1)}, f32[128]{0:T(128)S(1)}) all-reduce(f32[480]{0:T(512)S(1)} %fusion, f32[128]{0:T(128)S(1)} %multiply_reduce_fusion), channel_id=1, replica_groups=mesh['seq'=8,'mp'=4] {'mp'}, use_global_device_ids=true, to_apply=%region_4.5 | all-reduce | flops 608 | bytes 4864 | tf_op jit(solution)/shard_map/psum | solution.py:112
  11.1 0.1 multiply_convert_fusion
  11.2 0.9 pad_maximum_fusion
  12.1 5.8 %all-to-all-start = ((bf16[2,8,16,1280]{3,2,0,1:T(8,128)(2,1)}), bf16[2,8,16,1280]{3,2,0,1:T(8,128)(2,1)S(1)}, u32[]{:S(2)}, u32[]{:S(2)}) async-start(bf16[2,8,16,1280]{3,2,0,1:T(8,128)(2,1)} %pad_maximum_fusion), calls=%async_computation | async-start | bytes 1310720 | tf_op jit(solution)/shard_map/all_to_all | solution.py:121
  18.0 0.2 reduce-window.9
  18.2 0.1 convert_reduce_fusion.1
  18.4 0.7 gather_fusion
  19.1 15.0 %all-to-all-done = bf16[2,8,16,1280]{3,2,0,1:T(8,128)(2,1)S(1)} async-done(((bf16[2,8,16,1280]{3,2,0,1:T(8,128)(2,1)}), bf16[2,8,16,1280]{3,2,0,1:T(8,128)(2,1)S(1)}, u32[]{:S(2)}, u32[]{:S(2)}) %all-to-all-start) | async-done | bytes 655392 | tf_op jit(solution)/shard_map/all_to_all | solution.py:121
  34.1 1.7 %gather_fusion.1 = bf16[16,2,16,1280]{3,2,1,0:T(8,128)(2,1)} fusion(bf16[8,2,16,1280]{3,2,1,0:T(8,128)(2,1)S(1)} %bitcast.32, s32[1024]{0:T(1024)S(1)} %pad_clamp_fusion.1), kind=kCustom, calls=%fused_computation.1 | custom fusion | bytes 2621504 | tf_op jit(solution)/shard_map/jit(_take)/gather | solution.py:123
  35.8 3.8 %all-to-all-start.1 = ((bf16[8,2,2,16,1280]{4,3,2,1,0:T(8,128)(2,1)}), bf16[8,2,2,16,1280]{4,3,2,1,0:T(8,128)(2,1)S(1)}, u32[]{:S(2)}, u32[]{:S(2)}) async-start(bf16[8,2,2,16,1280]{4,3,2,1,0:T(8,128)(2,1)} %bitcast.12), calls=%async_computation.1 | async-start | bytes 2621440 | tf_op jit(solution)/shard_map/all_to_all | solution.py:124
  39.6 0.6 dynamic_slice.3
  40.2 0.1 convert_reduce_fusion
  40.3 0.6 add_subtract_fusion
  40.9 0.8 copy.21.tok_slot_ref
  41.8 1.4 fusion.2.q_ref
  43.2 27.1 %all-to-all-done.1.kv_ref = bf16[8,2,2,16,1280]{4,3,2,1,0:T(8,128)(2,1)S(1)} async-done(((bf16[8,2,2,16,1280]{4,3,2,1,0:T(8,128)(2,1)}), bf16[8,2,2,16,1280]{4,3,2,1,0:T(8,128)(2,1)S(1)}, u32[]{:S(2)}, u32[]{:S(2)}) %all-to-all-start.1) | async-done | bytes 1310752 | tf_op jit(solution)/shard_map/all_to_all | solution.py:124
  70.3 1.1 copy-done.1
  71.3 11.8 %shard_map.86 = (bf16[480,1280]{1,0:T(8,128)(2,1)}, bf16[8,2,2,16,1280]{4,3,2,1,0:T(8,128)(2,1)}) custom-call(s32[480,1]{1,0:T(8,128)} %copy.21.tok_slot_ref, bf16[480,1280]{1,0:T(8,128)(2,1)} %fusion.2.q_ref, bf16[8,2,2,16,1280]{4,3,2,1,0:T(8,128)(2,1)} %copy-done.1, bf16[480,1280]{1,0:T(8,128)(2,1)} %g_ref.1), custom_call_target="tpu_custom_call" | custom-call | tf_op jit(solution)/shard_map/pallas_call | solution.py:80
  83.1 3.6 %all-to-all-start.2 = ((bf16[8,2,2,16,1280]{4,3,2,1,0:T(8,128)(2,1)}), bf16[8,2,2,16,1280]{4,3,2,1,0:T(8,128)(2,1)S(1)}, u32[]{:S(2)}, u32[]{:S(2)}) async-start(bf16[8,2,2,16,1280]{4,3,2,1,0:T(8,128)(2,1)} %get-tuple-element.5), calls=%async_computation.2 | async-start | bytes 2621440 | tf_op jit(solution)/shard_map/all_to_all | solution.py:132
  86.9 0.1 select_reduce_fusion
  87.0 0.1 fusion.4
  87.1 31.0 %all-to-all-done.2 = bf16[8,2,2,16,1280]{4,3,2,1,0:T(8,128)(2,1)S(1)} async-done(((bf16[8,2,2,16,1280]{4,3,2,1,0:T(8,128)(2,1)}), bf16[8,2,2,16,1280]{4,3,2,1,0:T(8,128)(2,1)S(1)}, u32[]{:S(2)}, u32[]{:S(2)}) %all-to-all-start.2) | async-done | bytes 1310752 | tf_op jit(solution)/shard_map/all_to_all | solution.py:132
  118.1 0.6 reshape.167
  118.7 0.5 convolution_convert_fusion
  119.2 0.6 gather_fusion.2
  119.8 0.1 broadcast_select_fusion
  119.9 21.3 %all_to_all.43 = bf16[8,2,16,1280]{3,2,1,0:T(8,128)(2,1)S(1)} all-to-all(bf16[8,2,16,1280]{3,2,1,0:T(8,128)(2,1)S(1)} %broadcast_select_fusion), channel_id=1, replica_groups=mesh['seq'=8,'mp'=4] {'seq'}, dimensions={0} | all-to-all | bytes 1310720 | tf_op jit(solution)/shard_map/all_to_all | solution.py:143
  141.2 0.9 copy.23
  (30 shorter events, 0.5 us)
Async XLA Ops:
  0.6 1.3 copy-start.3
  0.6 1.7 %copy-start.2 = (bf16[480,1280]{1,0:T(8,128)(2,1)S(1)}, bf16[480,1280]{1,0:T(8,128)(2,1)}, u32[]{:S(2)}) copy-start(bf16[480,1280]{1,0:T(8,128)(2,1)} %param.7) | copy-start | bytes 3686404
  0.6 10.4 %copy-start.4 = (f32[1280]{0:T(1024)S(1)}, f32[1280]{0:T(1024)}, u32[]{:S(2)}) copy-start(f32[1280]{0:T(1024)} %param.10) | copy-start | bytes 15364
  11.2 6.8 %copy-start.6 = (s32[3]{0:T(128)S(1)}, s32[3]{0:T(128)}, u32[]{:S(2)}) copy-start(s32[3]{0:T(128)} %param.12) | copy-start | bytes 40
  11.2 7.2 %copy-start = (s32[3]{0:T(128)S(1)}, s32[3]{0:T(128)}, u32[]{:S(2)}) copy-start(s32[3]{0:T(128)} %param.13) | copy-start | bytes 40
  12.1 22.0 %all-to-all-start = ((bf16[2,8,16,1280]{3,2,0,1:T(8,128)(2,1)}), bf16[2,8,16,1280]{3,2,0,1:T(8,128)(2,1)S(1)}, u32[]{:S(2)}, u32[]{:S(2)}) async-start(bf16[2,8,16,1280]{3,2,0,1:T(8,128)(2,1)} %pad_maximum_fusion), calls=%async_computation | async-start | bytes 1310720 | tf_op jit(solution)/shard_map/all_to_all | solution.py:121
  35.8 6.0 %copy-start.5 = (f32[1280]{0:T(1024)S(1)}, f32[1280]{0:T(1024)}, u32[]{:S(2)}) copy-start(f32[1280]{0:T(1024)} %param.8) | copy-start | bytes 15364
  35.8 34.5 %all-to-all-start.1 = ((bf16[8,2,2,16,1280]{4,3,2,1,0:T(8,128)(2,1)}), bf16[8,2,2,16,1280]{4,3,2,1,0:T(8,128)(2,1)S(1)}, u32[]{:S(2)}, u32[]{:S(2)}) async-start(bf16[8,2,2,16,1280]{4,3,2,1,0:T(8,128)(2,1)} %bitcast.12), calls=%async_computation.1 | async-start | bytes 2621440 | tf_op jit(solution)/shard_map/all_to_all | solution.py:124
  70.3 1.1 copy-start.1
  83.1 34.9 %all-to-all-start.2 = ((bf16[8,2,2,16,1280]{4,3,2,1,0:T(8,128)(2,1)}), bf16[8,2,2,16,1280]{4,3,2,1,0:T(8,128)(2,1)S(1)}, u32[]{:S(2)}, u32[]{:S(2)}) async-start(bf16[8,2,2,16,1280]{4,3,2,1,0:T(8,128)(2,1)} %get-tuple-element.5), calls=%async_computation.2 | async-start | bytes 2621440 | tf_op jit(solution)/shard_map/all_to_all | solution.py:132

commit v9 on v8

--- a/solution.py
+++ b/solution.py
@@ -18,7 +18,7 @@
 HEADS_PER_STEP = 2
 
 
-def attend_kernel(tok_slot_ref, q_ref, kv_ref, g_ref, dq_ref, dkv_ref):
+def attend_kernel(tok_slot_ref, q_ref, kv_ref, g_ref, gs_ref, dkv_ref):
     score_scale = 1.0 / math.sqrt(HEAD_DIM)
     holders, _, _, piece, _ = kv_ref.shape
     depth = holders * piece
@@ -55,11 +55,7 @@
             lax.dot_general(g, v1, nt, preferred_element_type=jnp.float32),
         )
         grad_scores = (normed * (grad_weights - delta) * score_scale).astype(jnp.bfloat16)
-        dq_ref[:, cols] = jnp.where(
-            in_first,
-            jnp.dot(grad_scores, k0, preferred_element_type=jnp.float32),
-            jnp.dot(grad_scores, k1, preferred_element_type=jnp.float32),
-        ).astype(dq_ref.dtype)
+        gs_ref[:, cols] = grad_scores
         zero = jnp.zeros_like(grad_scores)
         gs0 = jnp.where(in_first, grad_scores, zero)
         gs1 = jnp.where(in_first, zero, grad_scores)
@@ -72,12 +68,28 @@
             dkv_ref[:, slot, 1, :, cols] = dv.reshape(holders, piece, HEAD_DIM)
 
 
+def grad_query_kernel(tok_slot_ref, gs_ref, kv_ref, dq_ref):
+    holders, _, _, piece, _ = kv_ref.shape
+    depth = holders * piece
+    in_first = tok_slot_ref[...] == 0
+    for head in range(HEADS_PER_STEP):
+        cols = slice(head * HEAD_DIM, (head + 1) * HEAD_DIM)
+        grad_scores = gs_ref[:, cols]
+        k0 = kv_ref[:, 0, 0, :, cols].reshape(depth, HEAD_DIM)
+        k1 = kv_ref[:, 1, 0, :, cols].reshape(depth, HEAD_DIM)
+        dq_ref[:, cols] = jnp.where(
+            in_first,
+            jnp.dot(grad_scores, k0, preferred_element_type=jnp.float32),
+            jnp.dot(grad_scores, k1, preferred_element_type=jnp.float32),
+        ).astype(dq_ref.dtype)
+
+
 def attend(tok_slot, query_normed, kv, grad_out):
     tok_rows, feat_width = query_normed.shape
     step_width = HEADS_PER_STEP * HEAD_DIM
     tok_spec = pl.BlockSpec((tok_rows, step_width), lambda h: (0, h))
     kv_spec = pl.BlockSpec(kv.shape[:4] + (step_width,), lambda h: (0, 0, 0, 0, h))
-    return pl.pallas_call(
+    grad_scores, grad_kv = pl.pallas_call(
         attend_kernel,
         grid=(feat_width // step_width,),
         in_specs=[
@@ -93,6 +105,15 @@
         ],
         compiler_params=pltpu.CompilerParams(dimension_semantics=("arbitrary",)),
     )(tok_slot, query_normed, kv, grad_out)
+    grad_query = pl.pallas_call(
+        grad_query_kernel,
+        grid=(feat_width // step_width,),
+        in_specs=[pl.BlockSpec((tok_rows, 1), lambda h: (0, 0)), tok_spec, kv_spec],
+        out_specs=tok_spec,
+        out_shape=jax.ShapeDtypeStruct((tok_rows, feat_width), jnp.bfloat16),
+        compiler_params=pltpu.CompilerParams(dimension_semantics=("arbitrary",)),
+    )(tok_slot, grad_scores, kv)
+    return grad_query, grad_kv
 
 
 def local(query, query_gain, cond, key_gain, grad_out, clip_len, clip_owner, seq_count):

time: 143 us -> 143 us (level)
  blocking collectives: 29.6 us -> 8.34 us
  waiting for transfers between devices: 73.1 us -> 85.3 us
  Pallas kernels: 11.8 us -> 16.9 us
  starting transfers between devices: 13.2 us -> 16.8 us
    all_to_all x1 -> x0, blocking collectives: 21.3 us -> none  [local(): lax.all_to_all(outgoing, 'seq', 0, 2, tiled=True)]
    all_to_all x0 -> x1, waiting for transfers between devices: none -> 12.2 us  [local(): lax.all_to_all(outgoing, 'seq', 0, 2, tiled=True)]
    pallas_call x0 -> x1, Pallas kernels: none -> 5.25 us  [attend(): pl.pallas_call(grad_query_kernel, grid=(feat_width // step_width,), in_sp...]
    all_to_all x0 -> x1, starting transfers between devices: none -> 3.64 us  [local(): lax.all_to_all(outgoing, 'seq', 0, 2, tiled=True)]
  transfers between devices with their start and end apart: 3 -> 4, of which waited for: 3 -> 4; matrix products, arithmetic and copies ran while one was open for 4% -> 4% of each run, Pallas kernels for 0% -> 4%
where the time goes in v9:
time: 143 us
  waiting for transfers between devices  85.3 us (60%)
  Pallas kernels  16.9 us (12%)
  starting transfers between devices  16.8 us (12%)
  blocking collectives  8.34 us (6%)
  local copies, waits for them, and re-layouts  7.64 us (5%)
  other arithmetic  6.35 us (4%)
    all_to_all x1, waiting for transfers between devices, local(): pieces = lax.all_to_all(spread_grads, 'seq', 0, 0, tiled=True)  31 us
    all_to_all x1, waiting for transfers between devices, local(): arrived = lax.all_to_all(wanted, 'seq', 0, 0, tiled=True)  27.1 us
    all_to_all x1, waiting for transfers between devices, local(): lax.all_to_all(spread, 'seq', 1, 0, tiled=True)  15 us
    all_to_all x1, waiting for transfers between devices, local(): lax.all_to_all(outgoing, 'seq', 0, 2, tiled=True)  12.2 us
    pallas_call x1, Pallas kernels, attend(): pl.pallas_call(attend_kernel, grid=(feat_width // step_width,), in_specs=...  11.7 us
    psum x1, blocking collectives, local(): lax.psum((jnp.sum(query_wide * query_wide, axis=1), jnp.sum(own_key * own...  8.34 us
    all_to_all x1, starting transfers between devices, local(): lax.all_to_all(spread, 'seq', 1, 0, tiled=True)  5.83 us
    pallas_call x1, Pallas kernels, attend(): pl.pallas_call(grad_query_kernel, grid=(feat_width // step_width,), in_sp...  5.25 us
  transfers between devices with their start and end apart: 4, of which 4 were waited for; matrix products, arithmetic and copies ran while one was open for 4% of the time, Pallas kernels for 4%

profile of v9, /device:TPU:0, one launch (start us, length us, event | category | flops | bytes accessed | tf_op | source)
XLA Modules:
  0.0 142.6 jit_solution(3757172963883674746)
XLA Ops:
  0.7 1.3 slice_convert_fusion
  1.9 0.1 multiply_reduce_fusion
  2.1 0.2 copy-done.2
  2.3 0.3 fusion
  2.6 8.3 %all-reduce = (f32[480]{0:T(512)S(1)}, f32[128]{0:T(128)S(1)}) all-reduce(f32[480]{0:T(512)S(1)} %fusion, f32[128]{0:T(128)S(1)} %multiply_reduce_fusion), channel_id=1, replica_groups=mesh['seq'=8,'mp'=4] {'mp'}, use_global_device_ids=true, to_apply=%region_4.5 | all-reduce | flops 608 | bytes 4864 | tf_op jit(solution)/shard_map/psum | solution.py:133
  11.1 0.1 multiply_convert_fusion
  11.2 0.9 pad_maximum_fusion
  12.1 5.8 %all-to-all-start = ((bf16[2,8,16,1280]{3,2,0,1:T(8,128)(2,1)}), bf16[2,8,16,1280]{3,2,0,1:T(8,128)(2,1)S(1)}, u32[]{:S(2)}, u32[]{:S(2)}) async-start(bf16[2,8,16,1280]{3,2,0,1:T(8,128)(2,1)} %pad_maximum_fusion), calls=%async_computation | async-start | bytes 1310720 | tf_op jit(solution)/shard_map/all_to_all | solution.py:142
  18.0 0.2 reduce-window.9
  18.2 0.1 convert_reduce_fusion.1
  18.4 0.7 gather_fusion
  19.1 15.0 %all-to-all-done = bf16[2,8,16,1280]{3,2,0,1:T(8,128)(2,1)S(1)} async-done(((bf16[2,8,16,1280]{3,2,0,1:T(8,128)(2,1)}), bf16[2,8,16,1280]{3,2,0,1:T(8,128)(2,1)S(1)}, u32[]{:S(2)}, u32[]{:S(2)}) %all-to-all-start) | async-done | bytes 655392 | tf_op jit(solution)/shard_map/all_to_all | solution.py:142
  34.1 1.7 %gather_fusion.1 = bf16[16,2,16,1280]{3,2,1,0:T(8,128)(2,1)} fusion(bf16[8,2,16,1280]{3,2,1,0:T(8,128)(2,1)S(1)} %bitcast.32, s32[1024]{0:T(1024)S(1)} %pad_clamp_fusion.1), kind=kCustom, calls=%fused_computation.1 | custom fusion | bytes 2621504 | tf_op jit(solution)/shard_map/jit(_take)/gather | solution.py:144
  35.8 3.8 %all-to-all-start.1 = ((bf16[8,2,2,16,1280]{4,3,2,1,0:T(8,128)(2,1)}), bf16[8,2,2,16,1280]{4,3,2,1,0:T(8,128)(2,1)S(1)}, u32[]{:S(2)}, u32[]{:S(2)}) async-start(bf16[8,2,2,16,1280]{4,3,2,1,0:T(8,128)(2,1)} %bitcast.12), calls=%async_computation.1 | async-start | bytes 2621440 | tf_op jit(solution)/shard_map/all_to_all | solution.py:145
  39.6 0.6 dynamic_slice.3
  40.2 0.1 convert_reduce_fusion
  40.3 0.6 add_subtract_fusion
  40.9 0.8 copy.24.tok_slot_ref
  41.8 1.4 fusion.2.q_ref
  43.1 27.1 %all-to-all-done.1.kv_ref = bf16[8,2,2,16,1280]{4,3,2,1,0:T(8,128)(2,1)S(1)} async-done(((bf16[8,2,2,16,1280]{4,3,2,1,0:T(8,128)(2,1)}), bf16[8,2,2,16,1280]{4,3,2,1,0:T(8,128)(2,1)S(1)}, u32[]{:S(2)}, u32[]{:S(2)}) %all-to-all-start.1) | async-done | bytes 1310752 | tf_op jit(solution)/shard_map/all_to_all | solution.py:145
  70.3 1.1 copy-done.1
  71.3 11.7 %shard_map.86 = (bf16[480,1280]{1,0:T(8,128)(2,1)}, bf16[8,2,2,16,1280]{4,3,2,1,0:T(8,128)(2,1)}) custom-call(s32[480,1]{1,0:T(8,128)} %copy.24.tok_slot_ref, bf16[480,1280]{1,0:T(8,128)(2,1)} %fusion.2.q_ref, bf16[8,2,2,16,1280]{4,3,2,1,0:T(8,128)(2,1)} %copy-done.1, bf16[480,1280]{1,0:T(8,128)(2,1)} %g_ref.1), custom_call_target="tpu_custom_call" | custom-call | tf_op jit(solution)/shard_map/pallas_call | solution.py:92
  83.0 3.6 %all-to-all-start.2 = ((bf16[8,2,2,16,1280]{4,3,2,1,0:T(8,128)(2,1)}), bf16[8,2,2,16,1280]{4,3,2,1,0:T(8,128)(2,1)S(1)}, u32[]{:S(2)}, u32[]{:S(2)}) async-start(bf16[8,2,2,16,1280]{4,3,2,1,0:T(8,128)(2,1)} %get-tuple-element.5), calls=%async_computation.2 | async-start | bytes 2621440 | tf_op jit(solution)/shard_map/all_to_all | solution.py:153
  87.0 31.0 %all-to-all-done.2 = bf16[8,2,2,16,1280]{4,3,2,1,0:T(8,128)(2,1)S(1)} async-done(((bf16[8,2,2,16,1280]{4,3,2,1,0:T(8,128)(2,1)}), bf16[8,2,2,16,1280]{4,3,2,1,0:T(8,128)(2,1)S(1)}, u32[]{:S(2)}, u32[]{:S(2)}) %all-to-all-start.2) | async-done | bytes 1310752 | tf_op jit(solution)/shard_map/all_to_all | solution.py:153
  118.0 0.6 reshape.167
  118.6 0.5 convolution_convert_fusion
  119.1 0.6 gather_fusion.2
  119.7 1.0 broadcast_select_fusion
  120.6 3.6 %all-to-all-start.3 = ((bf16[8,2,16,1280]{3,2,1,0:T(8,128)(2,1)}), bf16[8,2,16,1280]{3,2,1,0:T(8,128)(2,1)S(1)}, u32[]{:S(2)}, u32[]{:S(2)}) async-start(bf16[8,2,16,1280]{3,2,1,0:T(8,128)(2,1)} %broadcast_select_fusion), calls=%async_computation.3 | async-start | bytes 1310720 | tf_op jit(solution)/shard_map/all_to_all | solution.py:164
  124.3 5.3 %shard_map.87 = bf16[480,1280]{1,0:T(8,128)(2,1)} custom-call(s32[480,1]{1,0:T(8,128)} %copy.24.tok_slot_ref, bf16[480,1280]{1,0:T(8,128)(2,1)} %get-tuple-element.4.gs_ref, bf16[8,2,2,16,1280]{4,3,2,1,0:T(8,128)(2,1)} %copy-done.1), custom_call_target="tpu_custom_call" | custom-call | tf_op jit(solution)/shard_map/pallas_call | solution.py:108
  129.5 12.2 %all-to-all-done.3 = bf16[8,2,16,1280]{3,2,1,0:T(8,128)(2,1)S(1)} async-done(((bf16[8,2,16,1280]{3,2,1,0:T(8,128)(2,1)}), bf16[8,2,16,1280]{3,2,1,0:T(8,128)(2,1)S(1)}, u32[]{:S(2)}, u32[]{:S(2)}) %all-to-all-start.3) | async-done | bytes 655392 | tf_op jit(solution)/shard_map/all_to_all | solution.py:164
  141.8 0.9 copy.26
  (32 shorter events, 0.7 us)
Async XLA Ops:
  0.6 1.3 copy-start.3
  0.6 1.7 %copy-start.2 = (bf16[480,1280]{1,0:T(8,128)(2,1)S(1)}, bf16[480,1280]{1,0:T(8,128)(2,1)}, u32[]{:S(2)}) copy-start(bf16[480,1280]{1,0:T(8,128)(2,1)} %param.7) | copy-start | bytes 3686404
  0.6 10.4 %copy-start.4 = (f32[1280]{0:T(1024)S(1)}, f32[1280]{0:T(1024)}, u32[]{:S(2)}) copy-start(f32[1280]{0:T(1024)} %param.10) | copy-start | bytes 15364
  11.2 6.8 %copy-start.6 = (s32[3]{0:T(128)S(1)}, s32[3]{0:T(128)}, u32[]{:S(2)}) copy-start(s32[3]{0:T(128)} %param.12) | copy-start | bytes 40
  11.2 7.2 %copy-start = (s32[3]{0:T(128)S(1)}, s32[3]{0:T(128)}, u32[]{:S(2)}) copy-start(s32[3]{0:T(128)} %param.13) | copy-start | bytes 40
  12.1 22.0 %all-to-all-start = ((bf16[2,8,16,1280]{3,2,0,1:T(8,128)(2,1)}), bf16[2,8,16,1280]{3,2,0,1:T(8,128)(2,1)S(1)}, u32[]{:S(2)}, u32[]{:S(2)}) async-start(bf16[2,8,16,1280]{3,2,0,1:T(8,128)(2,1)} %pad_maximum_fusion), calls=%async_computation | async-start | bytes 1310720 | tf_op jit(solution)/shard_map/all_to_all | solution.py:142
  35.8 6.0 %copy-start.5 = (f32[1280]{0:T(1024)S(1)}, f32[1280]{0:T(1024)}, u32[]{:S(2)}) copy-start(f32[1280]{0:T(1024)} %param.8) | copy-start | bytes 15364
  35.8 34.5 %all-to-all-start.1 = ((bf16[8,2,2,16,1280]{4,3,2,1,0:T(8,128)(2,1)}), bf16[8,2,2,16,1280]{4,3,2,1,0:T(8,128)(2,1)S(1)}, u32[]{:S(2)}, u32[]{:S(2)}) async-start(bf16[8,2,2,16,1280]{4,3,2,1,0:T(8,128)(2,1)} %bitcast.12), calls=%async_computation.1 | async-start | bytes 2621440 | tf_op jit(solution)/shard_map/all_to_all | solution.py:145
  70.3 1.1 copy-start.1
  83.0 34.9 %all-to-all-start.2 = ((bf16[8,2,2,16,1280]{4,3,2,1,0:T(8,128)(2,1)}), bf16[8,2,2,16,1280]{4,3,2,1,0:T(8,128)(2,1)S(1)}, u32[]{:S(2)}, u32[]{:S(2)}) async-start(bf16[8,2,2,16,1280]{4,3,2,1,0:T(8,128)(2,1)} %get-tuple-element.5), calls=%async_computation.2 | async-start | bytes 2621440 | tf_op jit(solution)/shard_map/all_to_all | solution.py:153
  120.6 21.1 %all-to-all-start.3 = ((bf16[8,2,16,1280]{3,2,1,0:T(8,128)(2,1)}), bf16[8,2,16,1280]{3,2,1,0:T(8,128)(2,1)S(1)}, u32[]{:S(2)}, u32[]{:S(2)}) async-start(bf16[8,2,16,1280]{3,2,1,0:T(8,128)(2,1)} %broadcast_select_fusion), calls=%async_computation.3 | async-start | bytes 1310720 | tf_op jit(solution)/shard_map/all_to_all | solution.py:164

commit v10 on v8

--- a/solution.py
+++ b/solution.py
@@ -107,14 +107,8 @@
     clip_of = jnp.sum((position[:, None] >= starts[None, :]).astype(jnp.int32), axis=1) - 1
     device_pos = jnp.arange(seq_count, dtype=jnp.int32) * tok_rows
     device_first = jnp.sum((device_pos[:, None] >= starts[None, :]).astype(jnp.int32), axis=1) - 1
-    query_wide = query.astype(jnp.float32)
     own_key = cond[0, 0].astype(jnp.float32)
-    sums = lax.psum(
-        (jnp.sum(query_wide * query_wide, axis=1), jnp.sum(own_key * own_key, axis=1)), "mp"
-    )
-    query_scale = lax.rsqrt(sums[0] / D + EPS)
-    query_normed = (query_wide * query_scale[:, None] * query_gain).astype(jnp.bfloat16)
-    key_scale = lax.rsqrt(sums[1] / D + EPS)
+    key_scale = lax.rsqrt(lax.psum(jnp.sum(own_key * own_key, axis=1), "mp") / D + EPS)
     own_key_normed = (own_key * key_scale[:, None] * key_gain).astype(jnp.bfloat16)
     own_slab = jnp.stack([own_key_normed, cond[0, 1]])
     spread = own_slab.reshape(2, seq_count, piece, feat_width)
@@ -122,6 +116,11 @@
     slot_clip = jnp.stack([device_first, device_first + 1], axis=1)
     wanted = jnp.take(gathered, clip_owner[jnp.minimum(slot_clip, clip_count - 1)], axis=0, mode="clip")
     arrived = lax.all_to_all(wanted, "seq", 0, 0, tiled=True)
+    query_wide = query.astype(jnp.float32)
+    after_first = (gathered[0, 0, 0, 0] * 0).astype(jnp.float32)
+    query_sumsq = lax.psum(jnp.sum(query_wide * query_wide, axis=1) + after_first, "mp")
+    query_scale = lax.rsqrt(query_sumsq / D + EPS)
+    query_normed = (query_wide * query_scale[:, None] * query_gain).astype(jnp.bfloat16)
     tok_slot = clip_of - device_first[my_index]
     if piece % 16 == 0:
         grad_query, spread_grads = attend(tok_slot[:, None], query_normed, arrived, grad_out)

time: 143 us -> 142 us (level)
  waiting for transfers between devices: 73.1 us -> 64.8 us
  blocking collectives: 29.6 us -> 36.4 us
    all_to_all x1, waiting for transfers between devices: 27.1 us -> 18.8 us  [local(): arrived = lax.all_to_all(wanted, 'seq', 0, 0, tiled=True)]
    psum x1 -> x2, blocking collectives: 8.34 us -> 15.1 us  [the longest x1 8.34 us: local(): lax.psum(jnp.sum(own_key * own_key, axis=1), 'mp') / D + EPS]
where the time goes in v10:
time: 142 us
  waiting for transfers between devices  64.8 us (46%)
  blocking collectives  36.4 us (26%)
  starting transfers between devices  13.2 us (9%)
  Pallas kernels  11.8 us (8%)
  local copies, waits for them, and re-layouts  7.98 us (6%)
  other arithmetic  5.48 us (4%)
  between operations  1.45 us (1%)
    all_to_all x1, waiting for transfers between devices, local(): pieces = lax.all_to_all(spread_grads, 'seq', 0, 0, tiled=True)  31 us
    all_to_all x1, blocking collectives, local(): lax.all_to_all(outgoing, 'seq', 0, 2, tiled=True)  21.3 us
    all_to_all x1, waiting for transfers between devices, local(): arrived = lax.all_to_all(wanted, 'seq', 0, 0, tiled=True)  18.8 us
    all_to_all x1, waiting for transfers between devices, local(): lax.all_to_all(spread, 'seq', 1, 0, tiled=True)  15 us
    pallas_call x1, Pallas kernels, attend(): pl.pallas_call(attend_kernel, grid=(feat_width // step_width,), in_specs=...  11.8 us
    psum x1, blocking collectives, local(): lax.psum(jnp.sum(own_key * own_key, axis=1), 'mp') / D + EPS  8.34 us
    psum x1, blocking collectives, local(): lax.psum(jnp.sum(query_wide * query_wide, axis=1) + after_first, 'mp')  6.77 us
    all_to_all x1, starting transfers between devices, local(): lax.all_to_all(spread, 'seq', 1, 0, tiled=True)  5.83 us
  transfers between devices with their start and end apart: 3, of which 3 were waited for; matrix products, arithmetic and copies ran while one was open for 4% of the time, Pallas kernels for 0%

profile of v10, /device:TPU:0, one launch (start us, length us, event | category | flops | bytes accessed | tf_op | source)
XLA Modules:
  0.0 141.5 jit_solution(15899577292102772371)
XLA Ops:
  0.6 1.2 slice_convert_fusion
  1.9 0.1 multiply_reduce_fusion
  2.1 8.3 %psum.14 = f32[128]{0:T(128)S(1)} all-reduce(f32[128]{0:T(128)S(1)} %multiply_reduce_fusion), channel_id=1, replica_groups=mesh['seq'=8,'mp'=4] {'mp'}, use_global_device_ids=true, to_apply=%region_5.6 | all-reduce | flops 128 | bytes 1024 | tf_op jit(solution)/shard_map/psum | solution.py:111
  10.5 0.1 multiply_convert_fusion
  10.7 0.9 pad_maximum_fusion
  11.5 5.8 %all-to-all-start = ((bf16[2,8,16,1280]{3,2,0,1:T(8,128)(2,1)}), bf16[2,8,16,1280]{3,2,0,1:T(8,128)(2,1)S(1)}, u32[]{:S(2)}, u32[]{:S(2)}) async-start(bf16[2,8,16,1280]{3,2,0,1:T(8,128)(2,1)} %pad_maximum_fusion), calls=%async_computation | async-start | bytes 1310720 | tf_op jit(solution)/shard_map/all_to_all | solution.py:115
  17.4 0.2 reduce-window.9
  17.6 0.1 convert_reduce_fusion.1
  17.9 0.7 gather_fusion
  18.5 15.0 %all-to-all-done = bf16[2,8,16,1280]{3,2,0,1:T(8,128)(2,1)S(1)} async-done(((bf16[2,8,16,1280]{3,2,0,1:T(8,128)(2,1)}), bf16[2,8,16,1280]{3,2,0,1:T(8,128)(2,1)S(1)}, u32[]{:S(2)}, u32[]{:S(2)}) %all-to-all-start) | async-done | bytes 655392 | tf_op jit(solution)/shard_map/all_to_all | solution.py:115
  33.5 1.7 %gather_fusion.1 = bf16[16,2,16,1280]{3,2,1,0:T(8,128)(2,1)} fusion(bf16[8,2,16,1280]{3,2,1,0:T(8,128)(2,1)S(1)} %bitcast.34, s32[1024]{0:T(1024)S(1)} %pad_clamp_fusion.1), kind=kCustom, calls=%fused_computation.1 | custom fusion | bytes 2621504 | tf_op jit(solution)/shard_map/jit(_take)/gather | solution.py:117
  35.2 3.8 %all-to-all-start.1 = ((bf16[8,2,2,16,1280]{4,3,2,1,0:T(8,128)(2,1)}), bf16[8,2,2,16,1280]{4,3,2,1,0:T(8,128)(2,1)S(1)}, u32[]{:S(2)}, u32[]{:S(2)}) async-start(bf16[8,2,2,16,1280]{4,3,2,1,0:T(8,128)(2,1)} %bitcast.15), calls=%async_computation.1 | async-start | bytes 2621440 | tf_op jit(solution)/shard_map/all_to_all | solution.py:118
  39.0 0.6 dynamic_slice.3
  39.6 0.1 convert_reduce_fusion
  39.7 0.6 add_subtract_fusion
  40.3 0.8 copy.21.tok_slot_ref
  41.2 0.3 fusion
  41.5 0.5 slice.18
  42.7 6.8 %psum.15 = f32[480]{0:T(512)S(1)} all-reduce(f32[480]{0:T(512)S(1)} %broadcast_add_fusion), channel_id=1, replica_groups=mesh['seq'=8,'mp'=4] {'mp'}, use_global_device_ids=true, to_apply=%region_6.7 | all-reduce | flops 480 | bytes 3840 | tf_op jit(solution)/shard_map/psum | solution.py:121
  49.5 1.4 %fusion.2.q_ref = bf16[480,1280]{1,0:T(8,128)(2,1)} fusion(bf16[480,1280]{1,0:T(8,128)(2,1)S(1)} %copy-done.2, f32[1280]{0:T(1024)S(1)} %copy-done.5, f32[480]{0:T(512)S(1)} %add_rsqrt_fusion), kind=kLoop, calls=%fused_computation.8 | loop fusion | flops 2457600 | bytes 2464640 | tf_op jit(solution)/shard_map/convert_element_type | solution.py:123
  50.9 18.8 %all-to-all-done.1.kv_ref = bf16[8,2,2,16,1280]{4,3,2,1,0:T(8,128)(2,1)S(1)} async-done(((bf16[8,2,2,16,1280]{4,3,2,1,0:T(8,128)(2,1)}), bf16[8,2,2,16,1280]{4,3,2,1,0:T(8,128)(2,1)S(1)}, u32[]{:S(2)}, u32[]{:S(2)}) %all-to-all-start.1) | async-done | bytes 1310752 | tf_op jit(solution)/shard_map/all_to_all | solution.py:118
  69.7 1.1 copy-done.1
  70.8 11.8 %shard_map.86 = (bf16[480,1280]{1,0:T(8,128)(2,1)}, bf16[8,2,2,16,1280]{4,3,2,1,0:T(8,128)(2,1)}) custom-call(s32[480,1]{1,0:T(8,128)} %copy.21.tok_slot_ref, bf16[480,1280]{1,0:T(8,128)(2,1)} %fusion.2.q_ref, bf16[8,2,2,16,1280]{4,3,2,1,0:T(8,128)(2,1)} %copy-done.1, bf16[480,1280]{1,0:T(8,128)(2,1)} %g_ref.1), custom_call_target="tpu_custom_call" | custom-call | tf_op jit(solution)/shard_map/pallas_call | solution.py:80
  82.6 3.6 %all-to-all-start.2 = ((bf16[8,2,2,16,1280]{4,3,2,1,0:T(8,128)(2,1)}), bf16[8,2,2,16,1280]{4,3,2,1,0:T(8,128)(2,1)S(1)}, u32[]{:S(2)}, u32[]{:S(2)}) async-start(bf16[8,2,2,16,1280]{4,3,2,1,0:T(8,128)(2,1)} %get-tuple-element.5), calls=%async_computation.2 | async-start | bytes 2621440 | tf_op jit(solution)/shard_map/all_to_all | solution.py:131
  86.4 0.1 fusion.4
  86.5 31.0 %all-to-all-done.2 = bf16[8,2,2,16,1280]{4,3,2,1,0:T(8,128)(2,1)S(1)} async-done(((bf16[8,2,2,16,1280]{4,3,2,1,0:T(8,128)(2,1)}), bf16[8,2,2,16,1280]{4,3,2,1,0:T(8,128)(2,1)S(1)}, u32[]{:S(2)}, u32[]{:S(2)}) %all-to-all-start.2) | async-done | bytes 1310752 | tf_op jit(solution)/shard_map/all_to_all | solution.py:131
  117.5 0.6 reshape.171
  118.1 0.5 convolution_convert_fusion
  118.6 0.6 gather_fusion.2
  119.2 0.1 broadcast_select_fusion
  119.4 21.3 %all_to_all.43 = bf16[8,2,16,1280]{3,2,1,0:T(8,128)(2,1)S(1)} all-to-all(bf16[8,2,16,1280]{3,2,1,0:T(8,128)(2,1)S(1)} %broadcast_select_fusion), channel_id=1, replica_groups=mesh['seq'=8,'mp'=4] {'seq'}, dimensions={0} | all-to-all | bytes 1310720 | tf_op jit(solution)/shard_map/all_to_all | solution.py:142
  140.6 0.9 copy.23
  (33 shorter events, 0.7 us)
Async XLA Ops:
  0.6 1.3 copy-start.3
  0.6 9.9 %copy-start.4 = (f32[1280]{0:T(1024)S(1)}, f32[1280]{0:T(1024)}, u32[]{:S(2)}) copy-start(f32[1280]{0:T(1024)} %param.10) | copy-start | bytes 15364
  10.6 6.8 %copy-start.6 = (s32[3]{0:T(128)S(1)}, s32[3]{0:T(128)}, u32[]{:S(2)}) copy-start(s32[3]{0:T(128)} %param.12) | copy-start | bytes 40
  10.6 7.2 %copy-start = (s32[3]{0:T(128)S(1)}, s32[3]{0:T(128)}, u32[]{:S(2)}) copy-start(s32[3]{0:T(128)} %param.13) | copy-start | bytes 40
  11.5 22.0 %all-to-all-start = ((bf16[2,8,16,1280]{3,2,0,1:T(8,128)(2,1)}), bf16[2,8,16,1280]{3,2,0,1:T(8,128)(2,1)S(1)}, u32[]{:S(2)}, u32[]{:S(2)}) async-start(bf16[2,8,16,1280]{3,2,0,1:T(8,128)(2,1)} %pad_maximum_fusion), calls=%async_computation | async-start | bytes 1310720 | tf_op jit(solution)/shard_map/all_to_all | solution.py:115
  35.2 6.0 %copy-start.2 = (bf16[480,1280]{1,0:T(8,128)(2,1)S(1)}, bf16[480,1280]{1,0:T(8,128)(2,1)}, u32[]{:S(2)}) copy-start(bf16[480,1280]{1,0:T(8,128)(2,1)} %param.7) | copy-start | bytes 3686404
  35.2 34.5 %all-to-all-start.1 = ((bf16[8,2,2,16,1280]{4,3,2,1,0:T(8,128)(2,1)}), bf16[8,2,2,16,1280]{4,3,2,1,0:T(8,128)(2,1)S(1)}, u32[]{:S(2)}, u32[]{:S(2)}) async-start(bf16[8,2,2,16,1280]{4,3,2,1,0:T(8,128)(2,1)} %bitcast.15), calls=%async_computation.1 | async-start | bytes 2621440 | tf_op jit(solution)/shard_map/all_to_all | solution.py:118
  39.0 10.5 %copy-start.5 = (f32[1280]{0:T(1024)S(1)}, f32[1280]{0:T(1024)}, u32[]{:S(2)}) copy-start(f32[1280]{0:T(1024)} %param.8) | copy-start | bytes 15364
  69.7 1.1 copy-start.1
  82.6 34.9 %all-to-all-start.2 = ((bf16[8,2,2,16,1280]{4,3,2,1,0:T(8,128)(2,1)}), bf16[8,2,2,16,1280]{4,3,2,1,0:T(8,128)(2,1)S(1)}, u32[]{:S(2)}, u32[]{:S(2)}) async-start(bf16[8,2,2,16,1280]{4,3,2,1,0:T(8,128)(2,1)} %get-tuple-element.5), calls=%async_computation.2 | async-start | bytes 2621440 | tf_op jit(solution)/shard_map/all_to_all | solution.py:131

commit v11 on v10

--- a/solution.py
+++ b/solution.py
@@ -130,15 +130,12 @@
         spread_grads = grad_slots[0].reshape(2, 2, seq_count, piece, feat_width).transpose(2, 0, 1, 3, 4)
     pieces = lax.all_to_all(spread_grads, "seq", 0, 0, tiled=True)
     source_clip = slot_clip.reshape(2 * seq_count)
-    onehot = (source_clip[:, None] == jnp.arange(clip_count, dtype=jnp.int32)[None, :]).astype(jnp.bfloat16)
-    summed = jnp.einsum(
-        "sc,sx->cx", onehot, pieces.reshape(2 * seq_count, -1), preferred_element_type=jnp.float32
-    ).astype(jnp.bfloat16).reshape(clip_count, 2, piece, feat_width)
     owns = clip_owner[None, :] == jnp.arange(seq_count, dtype=jnp.int32)[:, None]
     owned_clip = jnp.sum(jnp.where(owns, jnp.arange(clip_count, dtype=jnp.int32)[None, :], 0), axis=1)
-    outgoing = jnp.where(
-        jnp.any(owns, axis=1)[:, None, None, None], jnp.take(summed, owned_clip, axis=0, mode="clip"), jnp.zeros((), jnp.bfloat16)
-    )
+    route = (source_clip[None, :] == owned_clip[:, None]) & jnp.any(owns, axis=1)[:, None]
+    outgoing = jnp.einsum(
+        "ds,sx->dx", route.astype(jnp.bfloat16), pieces.reshape(2 * seq_count, -1), preferred_element_type=jnp.float32
+    ).astype(jnp.bfloat16).reshape(seq_count, 2, piece, feat_width)
     owned_grads = lax.all_to_all(outgoing, "seq", 0, 2, tiled=True).reshape(2, cond_depth, feat_width)
     return (grad_query, owned_grads[None])
 

time: 142 us -> 141 us (level)
  no operation moved by 1% of the time
where the time goes in v11:
time: 141 us
  waiting for transfers between devices  64.8 us (46%)
  blocking collectives  36.4 us (26%)
  starting transfers between devices  13.2 us (9%)
  Pallas kernels  11.8 us (8%)
  local copies, waits for them, and re-layouts  7.47 us (5%)
  other arithmetic  5.36 us (4%)
  between operations  1.44 us (1%)
    all_to_all x1, waiting for transfers between devices, local(): pieces = lax.all_to_all(spread_grads, 'seq', 0, 0, tiled=True)  31 us
    all_to_all x1, blocking collectives, local(): lax.all_to_all(outgoing, 'seq', 0, 2, tiled=True)  21.3 us
    all_to_all x1, waiting for transfers between devices, local(): arrived = lax.all_to_all(wanted, 'seq', 0, 0, tiled=True)  18.8 us
    all_to_all x1, waiting for transfers between devices, local(): lax.all_to_all(spread, 'seq', 1, 0, tiled=True)  15 us
    pallas_call x1, Pallas kernels, attend(): pl.pallas_call(attend_kernel, grid=(feat_width // step_width,), in_specs=...  11.8 us
    psum x1, blocking collectives, local(): lax.psum(jnp.sum(own_key * own_key, axis=1), 'mp') / D + EPS  8.34 us
    psum x1, blocking collectives, local(): lax.psum(jnp.sum(query_wide * query_wide, axis=1) + after_first, 'mp')  6.77 us
    all_to_all x1, starting transfers between devices, local(): lax.all_to_all(spread, 'seq', 1, 0, tiled=True)  5.83 us
  transfers between devices with their start and end apart: 3, of which 3 were waited for; matrix products, arithmetic and copies ran while one was open for 4% of the time, Pallas kernels for 0%

profile of v11, /device:TPU:0, one launch (start us, length us, event | category | flops | bytes accessed | tf_op | source)
XLA Modules:
  0.0 140.8 jit_solution(4744923364422813348)
XLA Ops:
  0.6 1.2 slice_convert_fusion
  1.9 0.1 multiply_reduce_fusion
  2.1 8.3 %psum.14 = f32[128]{0:T(128)S(1)} all-reduce(f32[128]{0:T(128)S(1)} %multiply_reduce_fusion), channel_id=1, replica_groups=mesh['seq'=8,'mp'=4] {'mp'}, use_global_device_ids=true, to_apply=%region_5.6 | all-reduce | flops 128 | bytes 1024 | tf_op jit(solution)/shard_map/psum | solution.py:111
  10.5 0.1 multiply_convert_fusion
  10.7 0.9 pad_maximum_fusion
  11.5 5.8 %all-to-all-start = ((bf16[2,8,16,1280]{3,2,0,1:T(8,128)(2,1)}), bf16[2,8,16,1280]{3,2,0,1:T(8,128)(2,1)S(1)}, u32[]{:S(2)}, u32[]{:S(2)}) async-start(bf16[2,8,16,1280]{3,2,0,1:T(8,128)(2,1)} %pad_maximum_fusion), calls=%async_computation | async-start | bytes 1310720 | tf_op jit(solution)/shard_map/all_to_all | solution.py:115
  17.4 0.2 reduce-window.9
  17.6 0.1 convert_reduce_fusion.1
  17.9 0.7 gather_fusion
  18.5 15.0 %all-to-all-done = bf16[2,8,16,1280]{3,2,0,1:T(8,128)(2,1)S(1)} async-done(((bf16[2,8,16,1280]{3,2,0,1:T(8,128)(2,1)}), bf16[2,8,16,1280]{3,2,0,1:T(8,128)(2,1)S(1)}, u32[]{:S(2)}, u32[]{:S(2)}) %all-to-all-start) | async-done | bytes 655392 | tf_op jit(solution)/shard_map/all_to_all | solution.py:115
  33.5 1.7 %gather_fusion.1 = bf16[16,2,16,1280]{3,2,1,0:T(8,128)(2,1)} fusion(bf16[8,2,16,1280]{3,2,1,0:T(8,128)(2,1)S(1)} %bitcast.33, s32[1024]{0:T(1024)S(1)} %pad_clamp_fusion), kind=kCustom, calls=%fused_computation.1 | custom fusion | bytes 2621504 | tf_op jit(solution)/shard_map/jit(_take)/gather | solution.py:117
  35.2 3.8 %all-to-all-start.1 = ((bf16[8,2,2,16,1280]{4,3,2,1,0:T(8,128)(2,1)}), bf16[8,2,2,16,1280]{4,3,2,1,0:T(8,128)(2,1)S(1)}, u32[]{:S(2)}, u32[]{:S(2)}) async-start(bf16[8,2,2,16,1280]{4,3,2,1,0:T(8,128)(2,1)} %bitcast.15), calls=%async_computation.1 | async-start | bytes 2621440 | tf_op jit(solution)/shard_map/all_to_all | solution.py:118
  39.0 0.6 dynamic_slice.3
  39.6 0.1 convert_reduce_fusion
  39.7 0.6 add_subtract_fusion
  40.3 0.8 copy.26.tok_slot_ref
  41.2 0.3 fusion
  41.5 0.5 slice.16
  42.7 6.8 %psum.15 = f32[480]{0:T(512)S(1)} all-reduce(f32[480]{0:T(512)S(1)} %broadcast_add_fusion), channel_id=1, replica_groups=mesh['seq'=8,'mp'=4] {'mp'}, use_global_device_ids=true, to_apply=%region_6.7 | all-reduce | flops 480 | bytes 3840 | tf_op jit(solution)/shard_map/psum | solution.py:121
  49.5 1.4 %fusion.2.q_ref = bf16[480,1280]{1,0:T(8,128)(2,1)} fusion(bf16[480,1280]{1,0:T(8,128)(2,1)S(1)} %copy-done.2, f32[1280]{0:T(1024)S(1)} %copy-done.5, f32[480]{0:T(512)S(1)} %add_rsqrt_fusion), kind=kLoop, calls=%fused_computation.7 | loop fusion | flops 2457600 | bytes 2464640 | tf_op jit(solution)/shard_map/convert_element_type | solution.py:123
  50.9 18.8 %all-to-all-done.1.kv_ref = bf16[8,2,2,16,1280]{4,3,2,1,0:T(8,128)(2,1)S(1)} async-done(((bf16[8,2,2,16,1280]{4,3,2,1,0:T(8,128)(2,1)}), bf16[8,2,2,16,1280]{4,3,2,1,0:T(8,128)(2,1)S(1)}, u32[]{:S(2)}, u32[]{:S(2)}) %all-to-all-start.1) | async-done | bytes 1310752 | tf_op jit(solution)/shard_map/all_to_all | solution.py:118
  69.7 1.1 copy-done.1
  70.8 11.8 %shard_map.86 = (bf16[480,1280]{1,0:T(8,128)(2,1)}, bf16[8,2,2,16,1280]{4,3,2,1,0:T(8,128)(2,1)}) custom-call(s32[480,1]{1,0:T(8,128)} %copy.26.tok_slot_ref, bf16[480,1280]{1,0:T(8,128)(2,1)} %fusion.2.q_ref, bf16[8,2,2,16,1280]{4,3,2,1,0:T(8,128)(2,1)} %copy-done.1, bf16[480,1280]{1,0:T(8,128)(2,1)} %g_ref.1), custom_call_target="tpu_custom_call" | custom-call | tf_op jit(solution)/shard_map/pallas_call | solution.py:80
  82.6 3.6 %all-to-all-start.2 = ((bf16[8,2,2,16,1280]{4,3,2,1,0:T(8,128)(2,1)}), bf16[8,2,2,16,1280]{4,3,2,1,0:T(8,128)(2,1)S(1)}, u32[]{:S(2)}, u32[]{:S(2)}) async-start(bf16[8,2,2,16,1280]{4,3,2,1,0:T(8,128)(2,1)} %get-tuple-element.5), calls=%async_computation.2 | async-start | bytes 2621440 | tf_op jit(solution)/shard_map/all_to_all | solution.py:131
  86.3 0.1 fusion.5
  86.4 0.1 select_reduce_fusion
  86.5 31.0 %all-to-all-done.2 = bf16[8,2,2,16,1280]{4,3,2,1,0:T(8,128)(2,1)S(1)} async-done(((bf16[8,2,2,16,1280]{4,3,2,1,0:T(8,128)(2,1)}), bf16[8,2,2,16,1280]{4,3,2,1,0:T(8,128)(2,1)S(1)}, u32[]{:S(2)}, u32[]{:S(2)}) %all-to-all-start.2) | async-done | bytes 1310752 | tf_op jit(solution)/shard_map/all_to_all | solution.py:131
  117.5 0.6 reshape.172
  118.1 0.4 convolution_convert_fusion
  118.5 0.1 copy.28
  118.6 21.3 %all_to_all.43 = bf16[8,2,16,1280]{3,2,1,0:T(8,128)(2,1)S(1)} all-to-all(bf16[8,2,16,1280]{3,2,1,0:T(8,128)(2,1)S(1)} %copy.28), channel_id=1, replica_groups=mesh['seq'=8,'mp'=4] {'seq'}, dimensions={0} | all-to-all | bytes 1310720 | tf_op jit(solution)/shard_map/all_to_all | solution.py:139
  139.9 0.9 copy.29
  (30 shorter events, 0.6 us)
Async XLA Ops:
  0.6 1.3 copy-start.3
  0.6 9.9 %copy-start.4 = (f32[1280]{0:T(1024)S(1)}, f32[1280]{0:T(1024)}, u32[]{:S(2)}) copy-start(f32[1280]{0:T(1024)} %param.10) | copy-start | bytes 15364
  10.6 6.8 %copy-start.6 = (s32[3]{0:T(128)S(1)}, s32[3]{0:T(128)}, u32[]{:S(2)}) copy-start(s32[3]{0:T(128)} %param.12) | copy-start | bytes 40
  10.6 7.2 %copy-start = (s32[3]{0:T(128)S(1)}, s32[3]{0:T(128)}, u32[]{:S(2)}) copy-start(s32[3]{0:T(128)} %param.13) | copy-start | bytes 40
  11.5 22.0 %all-to-all-start = ((bf16[2,8,16,1280]{3,2,0,1:T(8,128)(2,1)}), bf16[2,8,16,1280]{3,2,0,1:T(8,128)(2,1)S(1)}, u32[]{:S(2)}, u32[]{:S(2)}) async-start(bf16[2,8,16,1280]{3,2,0,1:T(8,128)(2,1)} %pad_maximum_fusion), calls=%async_computation | async-start | bytes 1310720 | tf_op jit(solution)/shard_map/all_to_all | solution.py:115
  35.2 6.0 %copy-start.2 = (bf16[480,1280]{1,0:T(8,128)(2,1)S(1)}, bf16[480,1280]{1,0:T(8,128)(2,1)}, u32[]{:S(2)}) copy-start(bf16[480,1280]{1,0:T(8,128)(2,1)} %param.7) | copy-start | bytes 3686404
  35.2 34.5 %all-to-all-start.1 = ((bf16[8,2,2,16,1280]{4,3,2,1,0:T(8,128)(2,1)}), bf16[8,2,2,16,1280]{4,3,2,1,0:T(8,128)(2,1)S(1)}, u32[]{:S(2)}, u32[]{:S(2)}) async-start(bf16[8,2,2,16,1280]{4,3,2,1,0:T(8,128)(2,1)} %bitcast.15), calls=%async_computation.1 | async-start | bytes 2621440 | tf_op jit(solution)/shard_map/all_to_all | solution.py:118
  39.0 10.5 %copy-start.5 = (f32[1280]{0:T(1024)S(1)}, f32[1280]{0:T(1024)}, u32[]{:S(2)}) copy-start(f32[1280]{0:T(1024)} %param.8) | copy-start | bytes 15364
  69.7 1.1 copy-start.1
  82.6 34.9 %all-to-all-start.2 = ((bf16[8,2,2,16,1280]{4,3,2,1,0:T(8,128)(2,1)}), bf16[8,2,2,16,1280]{4,3,2,1,0:T(8,128)(2,1)S(1)}, u32[]{:S(2)}, u32[]{:S(2)}) async-start(bf16[8,2,2,16,1280]{4,3,2,1,0:T(8,128)(2,1)} %get-tuple-element.5), calls=%async_computation.2 | async-start | bytes 2621440 | tf_op jit(solution)/shard_map/all_to_all | solution.py:131

commit v12 on v11

--- a/solution.py
+++ b/solution.py
@@ -114,7 +114,9 @@
     spread = own_slab.reshape(2, seq_count, piece, feat_width)
     gathered = lax.all_to_all(spread, "seq", 1, 0, tiled=True).reshape(seq_count, 2, piece, feat_width)
     slot_clip = jnp.stack([device_first, device_first + 1], axis=1)
-    wanted = jnp.take(gathered, clip_owner[jnp.minimum(slot_clip, clip_count - 1)], axis=0, mode="clip")
+    source = clip_owner[jnp.minimum(slot_clip, clip_count - 1)]
+    pick = (source[:, :, None] == jnp.arange(seq_count, dtype=jnp.int32)[None, None, :]).astype(jnp.bfloat16)
+    wanted = jnp.einsum("dsn,nkrf->dskrf", pick, gathered, preferred_element_type=jnp.float32).astype(jnp.bfloat16)
     arrived = lax.all_to_all(wanted, "seq", 0, 0, tiled=True)
     query_wide = query.astype(jnp.float32)
     after_first = (gathered[0, 0, 0, 0] * 0).astype(jnp.float32)
@@ -133,9 +135,10 @@
     owns = clip_owner[None, :] == jnp.arange(seq_count, dtype=jnp.int32)[:, None]
     owned_clip = jnp.sum(jnp.where(owns, jnp.arange(clip_count, dtype=jnp.int32)[None, :], 0), axis=1)
     route = (source_clip[None, :] == owned_clip[:, None]) & jnp.any(owns, axis=1)[:, None]
+    route = route.astype(jnp.bfloat16).reshape(seq_count, seq_count, 2)
     outgoing = jnp.einsum(
-        "ds,sx->dx", route.astype(jnp.bfloat16), pieces.reshape(2 * seq_count, -1), preferred_element_type=jnp.float32
-    ).astype(jnp.bfloat16).reshape(seq_count, 2, piece, feat_width)
+        "dns,nskrf->dkrf", route, pieces, preferred_element_type=jnp.float32
+    ).astype(jnp.bfloat16)
     owned_grads = lax.all_to_all(outgoing, "seq", 0, 2, tiled=True).reshape(2, cond_depth, feat_width)
     return (grad_query, owned_grads[None])
 

time: 141 us -> 141 us (level)
    gather x2 -> x3, local copies, waits for them, and re-layouts: 2.35 us -> 0.82 us  [local(): source = clip_owner[jnp.minimum(slot_clip, clip_count - 1)]]
where the time goes in v12:
time: 141 us
  waiting for transfers between devices  64.4 us (46%)
  blocking collectives  36.4 us (26%)
  starting transfers between devices  13.2 us (9%)
  Pallas kernels  11.8 us (8%)
  local copies, waits for them, and re-layouts  7.72 us (5%)
  other arithmetic  4.51 us (3%)
  matrix products  1.47 us (1%)
  between operations  1.44 us (1%)
    all_to_all x1, waiting for transfers between devices, local(): pieces = lax.all_to_all(spread_grads, 'seq', 0, 0, tiled=True)  31.2 us
    all_to_all x1, blocking collectives, local(): lax.all_to_all(outgoing, 'seq', 0, 2, tiled=True)  21.3 us
    all_to_all x1, waiting for transfers between devices, local(): arrived = lax.all_to_all(wanted, 'seq', 0, 0, tiled=True)  18.4 us
    all_to_all x1, waiting for transfers between devices, local(): lax.all_to_all(spread, 'seq', 1, 0, tiled=True)  14.8 us
    pallas_call x1, Pallas kernels, attend(): pl.pallas_call(attend_kernel, grid=(feat_width // step_width,), in_specs=...  11.8 us
    psum x1, blocking collectives, local(): lax.psum(jnp.sum(own_key * own_key, axis=1), 'mp') / D + EPS  8.34 us
    psum x1, blocking collectives, local(): lax.psum(jnp.sum(query_wide * query_wide, axis=1) + after_first, 'mp')  6.77 us
    all_to_all x1, starting transfers between devices, local(): lax.all_to_all(spread, 'seq', 1, 0, tiled=True)  5.83 us
  transfers between devices with their start and end apart: 3, of which 3 were waited for; matrix products, arithmetic and copies ran while one was open for 4% of the time, Pallas kernels for 0%

profile of v12, /device:TPU:0, one launch (start us, length us, event | category | flops | bytes accessed | tf_op | source)
XLA Modules:
  0.0 141.0 jit_solution(11759045944866355606)
XLA Ops:
  0.6 1.2 slice_convert_fusion
  1.9 0.1 multiply_reduce_fusion
  2.1 8.3 %psum.14 = f32[128]{0:T(128)S(1)} all-reduce(f32[128]{0:T(128)S(1)} %multiply_reduce_fusion), channel_id=1, replica_groups=mesh['seq'=8,'mp'=4] {'mp'}, use_global_device_ids=true, to_apply=%region_5.6 | all-reduce | flops 128 | bytes 1024 | tf_op jit(solution)/shard_map/psum | solution.py:111
  10.5 0.1 multiply_convert_fusion
  10.7 0.9 copy.32
  11.6 5.8 %all-to-all-start = ((bf16[2,8,16,1280]{3,2,0,1:T(8,128)(2,1)}), bf16[2,8,16,1280]{3,2,0,1:T(8,128)(2,1)S(1)}, u32[]{:S(2)}, u32[]{:S(2)}) async-start(bf16[2,8,16,1280]{3,2,0,1:T(8,128)(2,1)} %copy.32), calls=%async_computation | async-start | bytes 1310720 | tf_op jit(solution)/shard_map/all_to_all | solution.py:115
  17.5 0.2 reduce-window.9
  17.6 0.1 convert_reduce_fusion.1
  17.9 0.7 gather_fusion
  18.8 14.8 %all-to-all-done = bf16[2,8,16,1280]{3,2,0,1:T(8,128)(2,1)S(1)} async-done(((bf16[2,8,16,1280]{3,2,0,1:T(8,128)(2,1)}), bf16[2,8,16,1280]{3,2,0,1:T(8,128)(2,1)S(1)}, u32[]{:S(2)}, u32[]{:S(2)}) %all-to-all-start) | async-done | bytes 655392 | tf_op jit(solution)/shard_map/all_to_all | solution.py:115
  33.6 0.6 fusion.5
  34.2 1.3 copy.52
  35.5 3.8 %all-to-all-start.1 = ((bf16[8,2,2,16,1280]{4,3,2,1,0:T(8,128)(2,1)}), bf16[8,2,2,16,1280]{4,3,2,1,0:T(8,128)(2,1)S(1)}, u32[]{:S(2)}, u32[]{:S(2)}) async-start(bf16[8,2,2,16,1280]{4,3,2,1,0:T(8,128)(2,1)} %copy.52), calls=%async_computation.1 | async-start | bytes 2621440 | tf_op jit(solution)/shard_map/all_to_all | solution.py:120
  39.3 0.6 dynamic_slice.3
  39.9 0.1 convert_reduce_fusion
  40.0 0.6 add_subtract_fusion
  40.6 0.8 copy.37.tok_slot_ref
  41.5 0.3 fusion.1
  41.8 0.4 copy.53
  42.1 0.5 slice.14
  43.3 6.8 %psum.15 = f32[480]{0:T(512)S(1)} all-reduce(f32[480]{0:T(512)S(1)} %broadcast_add_fusion), channel_id=1, replica_groups=mesh['seq'=8,'mp'=4] {'mp'}, use_global_device_ids=true, to_apply=%region_6.7 | all-reduce | flops 480 | bytes 3840 | tf_op jit(solution)/shard_map/psum | solution.py:123
  50.1 1.4 %fusion.3.q_ref = bf16[480,1280]{1,0:T(8,128)(2,1)} fusion(bf16[480,1280]{1,0:T(8,128)(2,1)S(1)} %copy-done.2, f32[1280]{0:T(1024)S(1)} %copy-done.5, f32[480]{0:T(512)S(1)} %add_rsqrt_fusion), kind=kLoop, calls=%fused_computation.8 | loop fusion | flops 2457600 | bytes 2464640 | tf_op jit(solution)/shard_map/convert_element_type | solution.py:125
  51.5 18.4 %all-to-all-done.1.kv_ref = bf16[8,2,2,16,1280]{4,3,2,1,0:T(8,128)(2,1)S(1)} async-done(((bf16[8,2,2,16,1280]{4,3,2,1,0:T(8,128)(2,1)}), bf16[8,2,2,16,1280]{4,3,2,1,0:T(8,128)(2,1)S(1)}, u32[]{:S(2)}, u32[]{:S(2)}) %all-to-all-start.1) | async-done | bytes 1310752 | tf_op jit(solution)/shard_map/all_to_all | solution.py:120
  70.0 1.1 copy-done.1
  71.0 11.8 %shard_map.86 = (bf16[480,1280]{1,0:T(8,128)(2,1)}, bf16[8,2,2,16,1280]{4,3,2,1,0:T(8,128)(2,1)}) custom-call(s32[480,1]{1,0:T(8,128)} %copy.37.tok_slot_ref, bf16[480,1280]{1,0:T(8,128)(2,1)} %fusion.3.q_ref, bf16[8,2,2,16,1280]{4,3,2,1,0:T(8,128)(2,1)} %copy-done.1, bf16[480,1280]{1,0:T(8,128)(2,1)} %g_ref.1), custom_call_target="tpu_custom_call" | custom-call | tf_op jit(solution)/shard_map/pallas_call | solution.py:80
  82.9 3.6 %all-to-all-start.2 = ((bf16[8,2,2,16,1280]{4,3,2,1,0:T(8,128)(2,1)}), bf16[8,2,2,16,1280]{4,3,2,1,0:T(8,128)(2,1)S(1)}, u32[]{:S(2)}, u32[]{:S(2)}) async-start(bf16[8,2,2,16,1280]{4,3,2,1,0:T(8,128)(2,1)} %get-tuple-element.5), calls=%async_computation.2 | async-start | bytes 2621440 | tf_op jit(solution)/shard_map/all_to_all | solution.py:133
  86.4 0.1 fusion.17
  86.6 31.2 %all-to-all-done.2 = bf16[8,2,2,16,1280]{4,3,2,1,0:T(8,128)(2,1)S(1)} async-done(((bf16[8,2,2,16,1280]{4,3,2,1,0:T(8,128)(2,1)}), bf16[8,2,2,16,1280]{4,3,2,1,0:T(8,128)(2,1)S(1)}, u32[]{:S(2)}, u32[]{:S(2)}) %all-to-all-start.2) | async-done | bytes 1310752 | tf_op jit(solution)/shard_map/all_to_all | solution.py:133
  117.8 0.9 fusion
  118.7 0.1 copy.39
  118.8 21.3 %all_to_all.43 = bf16[8,2,16,1280]{3,2,1,0:T(8,128)(2,1)S(1)} all-to-all(bf16[8,2,16,1280]{3,2,1,0:T(8,128)(2,1)S(1)} %copy.39), channel_id=1, replica_groups=mesh['seq'=8,'mp'=4] {'seq'}, dimensions={0} | all-to-all | bytes 1310720 | tf_op jit(solution)/shard_map/all_to_all | solution.py:142
  140.1 0.9 copy.40
  (31 shorter events, 0.7 us)
Async XLA Ops:
  0.6 1.3 copy-start.3
  0.6 9.9 %copy-start.4 = (f32[1280]{0:T(1024)S(1)}, f32[1280]{0:T(1024)}, u32[]{:S(2)}) copy-start(f32[1280]{0:T(1024)} %param.10) | copy-start | bytes 15364
  10.7 6.8 %copy-start.6 = (s32[3]{0:T(128)S(1)}, s32[3]{0:T(128)}, u32[]{:S(2)}) copy-start(s32[3]{0:T(128)} %param.12) | copy-start | bytes 40
  10.7 7.2 %copy-start = (s32[3]{0:T(128)S(1)}, s32[3]{0:T(128)}, u32[]{:S(2)}) copy-start(s32[3]{0:T(128)} %param.13) | copy-start | bytes 40
  11.6 22.0 %all-to-all-start = ((bf16[2,8,16,1280]{3,2,0,1:T(8,128)(2,1)}), bf16[2,8,16,1280]{3,2,0,1:T(8,128)(2,1)S(1)}, u32[]{:S(2)}, u32[]{:S(2)}) async-start(bf16[2,8,16,1280]{3,2,0,1:T(8,128)(2,1)} %copy.32), calls=%async_computation | async-start | bytes 1310720 | tf_op jit(solution)/shard_map/all_to_all | solution.py:115
  35.5 6.0 %copy-start.2 = (bf16[480,1280]{1,0:T(8,128)(2,1)S(1)}, bf16[480,1280]{1,0:T(8,128)(2,1)}, u32[]{:S(2)}) copy-start(bf16[480,1280]{1,0:T(8,128)(2,1)} %param.7) | copy-start | bytes 3686404
  35.5 34.5 %all-to-all-start.1 = ((bf16[8,2,2,16,1280]{4,3,2,1,0:T(8,128)(2,1)}), bf16[8,2,2,16,1280]{4,3,2,1,0:T(8,128)(2,1)S(1)}, u32[]{:S(2)}, u32[]{:S(2)}) async-start(bf16[8,2,2,16,1280]{4,3,2,1,0:T(8,128)(2,1)} %copy.52), calls=%async_computation.1 | async-start | bytes 2621440 | tf_op jit(solution)/shard_map/all_to_all | solution.py:120
  41.5 8.7 %copy-start.5 = (f32[1280]{0:T(1024)S(1)}, f32[1280]{0:T(1024)}, u32[]{:S(2)}) copy-start(f32[1280]{0:T(1024)} %param.8) | copy-start | bytes 15364
  70.0 1.1 copy-start.1
  82.9 34.9 %all-to-all-start.2 = ((bf16[8,2,2,16,1280]{4,3,2,1,0:T(8,128)(2,1)}), bf16[8,2,2,16,1280]{4,3,2,1,0:T(8,128)(2,1)S(1)}, u32[]{:S(2)}, u32[]{:S(2)}) async-start(bf16[8,2,2,16,1280]{4,3,2,1,0:T(8,128)(2,1)} %get-tuple-element.5), calls=%async_computation.2 | async-start | bytes 2621440 | tf_op jit(solution)/shard_map/all_to_all | solution.py:133

commit v13 on v11

--- a/solution.py
+++ b/solution.py
@@ -107,9 +107,10 @@
     clip_of = jnp.sum((position[:, None] >= starts[None, :]).astype(jnp.int32), axis=1) - 1
     device_pos = jnp.arange(seq_count, dtype=jnp.int32) * tok_rows
     device_first = jnp.sum((device_pos[:, None] >= starts[None, :]).astype(jnp.int32), axis=1) - 1
-    own_key = cond[0, 0].astype(jnp.float32)
-    key_scale = lax.rsqrt(lax.psum(jnp.sum(own_key * own_key, axis=1), "mp") / D + EPS)
-    own_key_normed = (own_key * key_scale[:, None] * key_gain).astype(jnp.bfloat16)
+    own_key = cond[0, 0]
+    key_sumsq = jnp.einsum("rf,rf->r", own_key, own_key, preferred_element_type=jnp.float32)
+    key_scale = lax.rsqrt(lax.psum(key_sumsq, "mp") / D + EPS)
+    own_key_normed = (own_key.astype(jnp.float32) * key_scale[:, None] * key_gain).astype(jnp.bfloat16)
     own_slab = jnp.stack([own_key_normed, cond[0, 1]])
     spread = own_slab.reshape(2, seq_count, piece, feat_width)
     gathered = lax.all_to_all(spread, "seq", 1, 0, tiled=True).reshape(seq_count, 2, piece, feat_width)

time: 141 us -> 141 us (level)
  no operation moved by 1% of the time
where the time goes in v13:
time: 141 us
  waiting for transfers between devices  64.8 us (46%)
  blocking collectives  36.4 us (26%)
  starting transfers between devices  13.2 us (9%)
  Pallas kernels  11.8 us (8%)
  local copies, waits for them, and re-layouts  8.67 us (6%)
  other arithmetic  4.18 us (3%)
  between operations  1.44 us (1%)
    all_to_all x1, waiting for transfers between devices, local(): pieces = lax.all_to_all(spread_grads, 'seq', 0, 0, tiled=True)  31 us
    all_to_all x1, blocking collectives, local(): lax.all_to_all(outgoing, 'seq', 0, 2, tiled=True)  21.3 us
    all_to_all x1, waiting for transfers between devices, local(): arrived = lax.all_to_all(wanted, 'seq', 0, 0, tiled=True)  18.8 us
    all_to_all x1, waiting for transfers between devices, local(): lax.all_to_all(spread, 'seq', 1, 0, tiled=True)  15 us
    pallas_call x1, Pallas kernels, attend(): pl.pallas_call(attend_kernel, grid=(feat_width // step_width,), in_specs=...  11.8 us
    psum x1, blocking collectives, local(): key_scale = lax.rsqrt(lax.psum(key_sumsq, 'mp') / D + EPS)  8.34 us
    psum x1, blocking collectives, local(): lax.psum(jnp.sum(query_wide * query_wide, axis=1) + after_first, 'mp')  6.77 us
    all_to_all x1, starting transfers between devices, local(): lax.all_to_all(spread, 'seq', 1, 0, tiled=True)  5.83 us
  transfers between devices with their start and end apart: 3, of which 3 were waited for; matrix products, arithmetic and copies ran while one was open for 4% of the time, Pallas kernels for 0%

profile of v13, /device:TPU:0, one launch (start us, length us, event | category | flops | bytes accessed | tf_op | source)
XLA Modules:
  0.0 140.8 jit_solution(6993647922458168336)
XLA Ops:
  0.6 1.2 fusion.13
  1.9 0.1 fusion.5
  2.1 8.3 %psum.14 = f32[128]{0:T(128)S(1)} all-reduce(f32[128]{0:T(128)S(1)} %fusion.5), channel_id=1, replica_groups=mesh['seq'=8,'mp'=4] {'mp'}, use_global_device_ids=true, to_apply=%region_4.5 | all-reduce | flops 128 | bytes 1024 | tf_op jit(solution)/shard_map/psum | solution.py:112
  10.5 0.2 fusion.4
  10.7 0.9 pad_maximum_fusion
  11.6 5.8 %all-to-all-start = ((bf16[2,8,16,1280]{3,2,0,1:T(8,128)(2,1)}), bf16[2,8,16,1280]{3,2,0,1:T(8,128)(2,1)S(1)}, u32[]{:S(2)}, u32[]{:S(2)}) async-start(bf16[2,8,16,1280]{3,2,0,1:T(8,128)(2,1)} %pad_maximum_fusion), calls=%async_computation | async-start | bytes 1310720 | tf_op jit(solution)/shard_map/all_to_all | solution.py:116
  17.4 0.2 reduce-window.9
  17.6 0.1 convert_reduce_fusion.1
  17.9 0.7 gather_fusion
  18.6 15.0 %all-to-all-done = bf16[2,8,16,1280]{3,2,0,1:T(8,128)(2,1)S(1)} async-done(((bf16[2,8,16,1280]{3,2,0,1:T(8,128)(2,1)}), bf16[2,8,16,1280]{3,2,0,1:T(8,128)(2,1)S(1)}, u32[]{:S(2)}, u32[]{:S(2)}) %all-to-all-start) | async-done | bytes 655392 | tf_op jit(solution)/shard_map/all_to_all | solution.py:116
  33.5 1.7 %gather_fusion.1 = bf16[16,2,16,1280]{3,2,1,0:T(8,128)(2,1)} fusion(bf16[8,2,16,1280]{3,2,1,0:T(8,128)(2,1)S(1)} %bitcast.36, s32[1024]{0:T(1024)S(1)} %pad_clamp_fusion), kind=kCustom, calls=%fused_computation.1 | custom fusion | bytes 2621504 | tf_op jit(solution)/shard_map/jit(_take)/gather | solution.py:118
  35.2 3.8 %all-to-all-start.1 = ((bf16[8,2,2,16,1280]{4,3,2,1,0:T(8,128)(2,1)}), bf16[8,2,2,16,1280]{4,3,2,1,0:T(8,128)(2,1)S(1)}, u32[]{:S(2)}, u32[]{:S(2)}) async-start(bf16[8,2,2,16,1280]{4,3,2,1,0:T(8,128)(2,1)} %bitcast.16), calls=%async_computation.1 | async-start | bytes 2621440 | tf_op jit(solution)/shard_map/all_to_all | solution.py:119
  39.0 0.6 dynamic_slice.3
  39.6 0.1 convert_reduce_fusion
  39.7 0.6 add_subtract_fusion
  40.4 0.8 copy.26.tok_slot_ref
  41.2 0.3 fusion
  41.5 0.5 slice.16
  42.7 6.8 %psum.15 = f32[480]{0:T(512)S(1)} all-reduce(f32[480]{0:T(512)S(1)} %broadcast_add_fusion), channel_id=1, replica_groups=mesh['seq'=8,'mp'=4] {'mp'}, use_global_device_ids=true, to_apply=%region_5.6 | all-reduce | flops 480 | bytes 3840 | tf_op jit(solution)/shard_map/psum | solution.py:122
  49.5 1.4 %fusion.2.q_ref = bf16[480,1280]{1,0:T(8,128)(2,1)} fusion(bf16[480,1280]{1,0:T(8,128)(2,1)S(1)} %copy-done.2, f32[1280]{0:T(1024)S(1)} %copy-done.4, f32[480]{0:T(512)S(1)} %add_rsqrt_fusion), kind=kLoop, calls=%fused_computation.7 | loop fusion | flops 2457600 | bytes 2464640 | tf_op jit(solution)/shard_map/convert_element_type | solution.py:124
  50.9 18.8 %all-to-all-done.1.kv_ref = bf16[8,2,2,16,1280]{4,3,2,1,0:T(8,128)(2,1)S(1)} async-done(((bf16[8,2,2,16,1280]{4,3,2,1,0:T(8,128)(2,1)}), bf16[8,2,2,16,1280]{4,3,2,1,0:T(8,128)(2,1)S(1)}, u32[]{:S(2)}, u32[]{:S(2)}) %all-to-all-start.1) | async-done | bytes 1310752 | tf_op jit(solution)/shard_map/all_to_all | solution.py:119
  69.7 1.1 copy-done.1
  70.8 11.8 %shard_map.86 = (bf16[480,1280]{1,0:T(8,128)(2,1)}, bf16[8,2,2,16,1280]{4,3,2,1,0:T(8,128)(2,1)}) custom-call(s32[480,1]{1,0:T(8,128)} %copy.26.tok_slot_ref, bf16[480,1280]{1,0:T(8,128)(2,1)} %fusion.2.q_ref, bf16[8,2,2,16,1280]{4,3,2,1,0:T(8,128)(2,1)} %copy-done.1, bf16[480,1280]{1,0:T(8,128)(2,1)} %g_ref.1), custom_call_target="tpu_custom_call" | custom-call | tf_op jit(solution)/shard_map/pallas_call | solution.py:80
  82.6 3.6 %all-to-all-start.2 = ((bf16[8,2,2,16,1280]{4,3,2,1,0:T(8,128)(2,1)}), bf16[8,2,2,16,1280]{4,3,2,1,0:T(8,128)(2,1)S(1)}, u32[]{:S(2)}, u32[]{:S(2)}) async-start(bf16[8,2,2,16,1280]{4,3,2,1,0:T(8,128)(2,1)} %get-tuple-element.5), calls=%async_computation.2 | async-start | bytes 2621440 | tf_op jit(solution)/shard_map/all_to_all | solution.py:132
  86.3 0.1 fusion.8
  86.4 0.1 select_reduce_fusion
  86.5 31.0 %all-to-all-done.2 = bf16[8,2,2,16,1280]{4,3,2,1,0:T(8,128)(2,1)S(1)} async-done(((bf16[8,2,2,16,1280]{4,3,2,1,0:T(8,128)(2,1)}), bf16[8,2,2,16,1280]{4,3,2,1,0:T(8,128)(2,1)S(1)}, u32[]{:S(2)}, u32[]{:S(2)}) %all-to-all-start.2) | async-done | bytes 1310752 | tf_op jit(solution)/shard_map/all_to_all | solution.py:132
  117.5 0.6 reshape.170
  118.2 0.4 convolution_convert_fusion
  118.6 0.1 copy.28
  118.7 21.3 %all_to_all.43 = bf16[8,2,16,1280]{3,2,1,0:T(8,128)(2,1)S(1)} all-to-all(bf16[8,2,16,1280]{3,2,1,0:T(8,128)(2,1)S(1)} %copy.28), channel_id=1, replica_groups=mesh['seq'=8,'mp'=4] {'seq'}, dimensions={0} | all-to-all | bytes 1310720 | tf_op jit(solution)/shard_map/all_to_all | solution.py:140
  140.0 0.9 copy.29
  (30 shorter events, 0.6 us)
Async XLA Ops:
  0.6 1.3 copy-start.3
  0.6 9.9 %copy-start.5 = (f32[1280]{0:T(1024)S(1)}, f32[1280]{0:T(1024)}, u32[]{:S(2)}) copy-start(f32[1280]{0:T(1024)} %param.10) | copy-start | bytes 15364
  10.6 6.8 %copy-start.6 = (s32[3]{0:T(128)S(1)}, s32[3]{0:T(128)}, u32[]{:S(2)}) copy-start(s32[3]{0:T(128)} %param.12) | copy-start | bytes 40
  10.7 7.2 %copy-start = (s32[3]{0:T(128)S(1)}, s32[3]{0:T(128)}, u32[]{:S(2)}) copy-start(s32[3]{0:T(128)} %param.13) | copy-start | bytes 40
  11.6 22.0 %all-to-all-start = ((bf16[2,8,16,1280]{3,2,0,1:T(8,128)(2,1)}), bf16[2,8,16,1280]{3,2,0,1:T(8,128)(2,1)S(1)}, u32[]{:S(2)}, u32[]{:S(2)}) async-start(bf16[2,8,16,1280]{3,2,0,1:T(8,128)(2,1)} %pad_maximum_fusion), calls=%async_computation | async-start | bytes 1310720 | tf_op jit(solution)/shard_map/all_to_all | solution.py:116
  35.2 6.0 %copy-start.2 = (bf16[480,1280]{1,0:T(8,128)(2,1)S(1)}, bf16[480,1280]{1,0:T(8,128)(2,1)}, u32[]{:S(2)}) copy-start(bf16[480,1280]{1,0:T(8,128)(2,1)} %param.7) | copy-start | bytes 3686404
  35.2 34.5 %all-to-all-start.1 = ((bf16[8,2,2,16,1280]{4,3,2,1,0:T(8,128)(2,1)}), bf16[8,2,2,16,1280]{4,3,2,1,0:T(8,128)(2,1)S(1)}, u32[]{:S(2)}, u32[]{:S(2)}) async-start(bf16[8,2,2,16,1280]{4,3,2,1,0:T(8,128)(2,1)} %bitcast.16), calls=%async_computation.1 | async-start | bytes 2621440 | tf_op jit(solution)/shard_map/all_to_all | solution.py:119
  39.0 10.5 %copy-start.4 = (f32[1280]{0:T(1024)S(1)}, f32[1280]{0:T(1024)}, u32[]{:S(2)}) copy-start(f32[1280]{0:T(1024)} %param.8) | copy-start | bytes 15364
  69.7 1.1 copy-start.1
  82.6 34.9 %all-to-all-start.2 = ((bf16[8,2,2,16,1280]{4,3,2,1,0:T(8,128)(2,1)}), bf16[8,2,2,16,1280]{4,3,2,1,0:T(8,128)(2,1)S(1)}, u32[]{:S(2)}, u32[]{:S(2)}) async-start(bf16[8,2,2,16,1280]{4,3,2,1,0:T(8,128)(2,1)} %get-tuple-element.5), calls=%async_computation.2 | async-start | bytes 2621440 | tf_op jit(solution)/shard_map/all_to_all | solution.py:132

commit v14 on v11

--- a/solution.py
+++ b/solution.py
@@ -114,7 +114,11 @@
     spread = own_slab.reshape(2, seq_count, piece, feat_width)
     gathered = lax.all_to_all(spread, "seq", 1, 0, tiled=True).reshape(seq_count, 2, piece, feat_width)
     slot_clip = jnp.stack([device_first, device_first + 1], axis=1)
-    wanted = jnp.take(gathered, clip_owner[jnp.minimum(slot_clip, clip_count - 1)], axis=0, mode="clip")
+    owner_rows = jnp.take(gathered, clip_owner, axis=0, mode="clip")
+    slot_of = slot_clip[:, :, None, None, None]
+    wanted = owner_rows[clip_count - 1][None, None]
+    for clip in range(clip_count - 2, -1, -1):
+        wanted = jnp.where(slot_of == clip, owner_rows[clip][None, None], wanted)
     arrived = lax.all_to_all(wanted, "seq", 0, 0, tiled=True)
     query_wide = query.astype(jnp.float32)
     after_first = (gathered[0, 0, 0, 0] * 0).astype(jnp.float32)

time: 141 us -> 141 us (level)
  local copies, waits for them, and re-layouts: 7.47 us -> 5.73 us
    gather x2 -> x1, local copies, waits for them, and re-layouts: 2.35 us -> 0.56 us  [local(): owner_rows = jnp.take(gathered, clip_owner, axis=0, mode='clip')]
where the time goes in v14:
time: 141 us
  waiting for transfers between devices  65.4 us (46%)
  blocking collectives  36.4 us (26%)
  starting transfers between devices  13.2 us (9%)
  Pallas kernels  11.8 us (8%)
  other arithmetic  6.65 us (5%)
  local copies, waits for them, and re-layouts  5.73 us (4%)
  between operations  1.44 us (1%)
    all_to_all x1, waiting for transfers between devices, local(): pieces = lax.all_to_all(spread_grads, 'seq', 0, 0, tiled=True)  31 us
    all_to_all x1, blocking collectives, local(): lax.all_to_all(outgoing, 'seq', 0, 2, tiled=True)  21.3 us
    all_to_all x1, waiting for transfers between devices, local(): arrived = lax.all_to_all(wanted, 'seq', 0, 0, tiled=True)  18.8 us
    all_to_all x1, waiting for transfers between devices, local(): lax.all_to_all(spread, 'seq', 1, 0, tiled=True)  15.6 us
    pallas_call x1, Pallas kernels, attend(): pl.pallas_call(attend_kernel, grid=(feat_width // step_width,), in_specs=...  11.8 us
    psum x1, blocking collectives, local(): lax.psum(jnp.sum(own_key * own_key, axis=1), 'mp') / D + EPS  8.34 us
    psum x1, blocking collectives, local(): lax.psum(jnp.sum(query_wide * query_wide, axis=1) + after_first, 'mp')  6.77 us
    all_to_all x1, starting transfers between devices, local(): lax.all_to_all(spread, 'seq', 1, 0, tiled=True)  5.83 us
  transfers between devices with their start and end apart: 3, of which 3 were waited for; matrix products, arithmetic and copies ran while one was open for 4% of the time, Pallas kernels for 0%

profile of v14, /device:TPU:0, one launch (start us, length us, event | category | flops | bytes accessed | tf_op | source)
XLA Modules:
  0.0 141.0 jit_solution(5763117727873264166)
XLA Ops:
  0.6 1.2 slice_convert_fusion
  1.9 0.1 multiply_reduce_fusion
  2.1 8.3 %psum.14 = f32[128]{0:T(128)S(1)} all-reduce(f32[128]{0:T(128)S(1)} %multiply_reduce_fusion), channel_id=1, replica_groups=mesh['seq'=8,'mp'=4] {'mp'}, use_global_device_ids=true, to_apply=%region_5.6 | all-reduce | flops 128 | bytes 1024 | tf_op jit(solution)/shard_map/psum | solution.py:111
  10.5 0.1 multiply_convert_fusion
  10.7 0.9 pad_maximum_fusion
  11.5 5.8 %all-to-all-start = ((bf16[2,8,16,1280]{3,2,0,1:T(8,128)(2,1)}), bf16[2,8,16,1280]{3,2,0,1:T(8,128)(2,1)S(1)}, u32[]{:S(2)}, u32[]{:S(2)}) async-start(bf16[2,8,16,1280]{3,2,0,1:T(8,128)(2,1)} %pad_maximum_fusion), calls=%async_computation | async-start | bytes 1310720 | tf_op jit(solution)/shard_map/all_to_all | solution.py:115
  17.4 0.2 reduce-window.9
  17.6 0.1 convert_reduce_fusion.1
  17.7 0.1 copy.29
  17.8 0.1 copy.30
  17.9 15.6 %all-to-all-done = bf16[2,8,16,1280]{3,2,0,1:T(8,128)(2,1)S(1)} async-done(((bf16[2,8,16,1280]{3,2,0,1:T(8,128)(2,1)}), bf16[2,8,16,1280]{3,2,0,1:T(8,128)(2,1)S(1)}, u32[]{:S(2)}, u32[]{:S(2)}) %all-to-all-start) | async-done | bytes 655392 | tf_op jit(solution)/shard_map/all_to_all | solution.py:115
  33.5 0.6 gather_fusion
  34.1 1.3 select_select_fusion
  35.4 3.8 %all-to-all-start.1 = ((bf16[8,2,2,16,1280]{4,3,2,1,0:T(8,128)(2,1)}), bf16[8,2,2,16,1280]{4,3,2,1,0:T(8,128)(2,1)S(1)}, u32[]{:S(2)}, u32[]{:S(2)}) async-start(bf16[8,2,2,16,1280]{4,3,2,1,0:T(8,128)(2,1)} %select_select_fusion), calls=%async_computation.1 | async-start | bytes 2621440 | tf_op jit(solution)/shard_map/all_to_all | solution.py:122
  39.2 0.6 dynamic_slice.3
  39.8 0.1 convert_reduce_fusion
  39.9 0.6 add_subtract_fusion
  40.6 0.8 copy.31.tok_slot_ref
  41.4 0.3 fusion
  41.7 0.5 slice.26
  42.9 6.8 %psum.15 = f32[480]{0:T(512)S(1)} all-reduce(f32[480]{0:T(512)S(1)} %broadcast_add_fusion), channel_id=1, replica_groups=mesh['seq'=8,'mp'=4] {'mp'}, use_global_device_ids=true, to_apply=%region_6.7 | all-reduce | flops 480 | bytes 3840 | tf_op jit(solution)/shard_map/psum | solution.py:125
  49.7 1.4 %fusion.2.q_ref = bf16[480,1280]{1,0:T(8,128)(2,1)} fusion(bf16[480,1280]{1,0:T(8,128)(2,1)S(1)} %copy-done.1, f32[1280]{0:T(1024)S(1)} %copy-done.4, f32[480]{0:T(512)S(1)} %add_rsqrt_fusion), kind=kLoop, calls=%fused_computation.6 | loop fusion | flops 2457600 | bytes 2464640 | tf_op jit(solution)/shard_map/convert_element_type | solution.py:127
  51.1 18.8 %all-to-all-done.1.kv_ref = bf16[8,2,2,16,1280]{4,3,2,1,0:T(8,128)(2,1)S(1)} async-done(((bf16[8,2,2,16,1280]{4,3,2,1,0:T(8,128)(2,1)}), bf16[8,2,2,16,1280]{4,3,2,1,0:T(8,128)(2,1)S(1)}, u32[]{:S(2)}, u32[]{:S(2)}) %all-to-all-start.1) | async-done | bytes 1310752 | tf_op jit(solution)/shard_map/all_to_all | solution.py:122
  69.9 1.1 copy-done
  71.0 11.8 %shard_map.86 = (bf16[480,1280]{1,0:T(8,128)(2,1)}, bf16[8,2,2,16,1280]{4,3,2,1,0:T(8,128)(2,1)}) custom-call(s32[480,1]{1,0:T(8,128)} %copy.31.tok_slot_ref, bf16[480,1280]{1,0:T(8,128)(2,1)} %fusion.2.q_ref, bf16[8,2,2,16,1280]{4,3,2,1,0:T(8,128)(2,1)} %copy-done, bf16[480,1280]{1,0:T(8,128)(2,1)} %g_ref.1), custom_call_target="tpu_custom_call" | custom-call | tf_op jit(solution)/shard_map/pallas_call | solution.py:80
  82.8 3.6 %all-to-all-start.2 = ((bf16[8,2,2,16,1280]{4,3,2,1,0:T(8,128)(2,1)}), bf16[8,2,2,16,1280]{4,3,2,1,0:T(8,128)(2,1)S(1)}, u32[]{:S(2)}, u32[]{:S(2)}) async-start(bf16[8,2,2,16,1280]{4,3,2,1,0:T(8,128)(2,1)} %get-tuple-element.5), calls=%async_computation.2 | async-start | bytes 2621440 | tf_op jit(solution)/shard_map/all_to_all | solution.py:135
  86.7 31.0 %all-to-all-done.2 = bf16[8,2,2,16,1280]{4,3,2,1,0:T(8,128)(2,1)S(1)} async-done(((bf16[8,2,2,16,1280]{4,3,2,1,0:T(8,128)(2,1)}), bf16[8,2,2,16,1280]{4,3,2,1,0:T(8,128)(2,1)S(1)}, u32[]{:S(2)}, u32[]{:S(2)}) %all-to-all-start.2) | async-done | bytes 1310752 | tf_op jit(solution)/shard_map/all_to_all | solution.py:135
  117.7 0.6 reshape.166
  118.4 0.4 convolution_convert_fusion
  118.7 0.1 copy.33
  118.9 21.3 %all_to_all.43 = bf16[8,2,16,1280]{3,2,1,0:T(8,128)(2,1)S(1)} all-to-all(bf16[8,2,16,1280]{3,2,1,0:T(8,128)(2,1)S(1)} %copy.33), channel_id=1, replica_groups=mesh['seq'=8,'mp'=4] {'seq'}, dimensions={0} | all-to-all | bytes 1310720 | tf_op jit(solution)/shard_map/all_to_all | solution.py:143
  140.1 0.9 copy.34
  (30 shorter events, 0.6 us)
Async XLA Ops:
  0.6 1.3 copy-start.2
  0.6 9.9 %copy-start.3 = (f32[1280]{0:T(1024)S(1)}, f32[1280]{0:T(1024)}, u32[]{:S(2)}) copy-start(f32[1280]{0:T(1024)} %param.10) | copy-start | bytes 15364
  10.6 6.8 %copy-start.6 = (s32[3]{0:T(128)S(1)}, s32[3]{0:T(128)}, u32[]{:S(2)}) copy-start(s32[3]{0:T(128)} %param.12) | copy-start | bytes 40
  10.6 7.2 %copy-start.5 = (s32[3]{0:T(128)S(1)}, s32[3]{0:T(128)}, u32[]{:S(2)}) copy-start(s32[3]{0:T(128)} %param.13) | copy-start | bytes 40
  11.5 22.0 %all-to-all-start = ((bf16[2,8,16,1280]{3,2,0,1:T(8,128)(2,1)}), bf16[2,8,16,1280]{3,2,0,1:T(8,128)(2,1)S(1)}, u32[]{:S(2)}, u32[]{:S(2)}) async-start(bf16[2,8,16,1280]{3,2,0,1:T(8,128)(2,1)} %pad_maximum_fusion), calls=%async_computation | async-start | bytes 1310720 | tf_op jit(solution)/shard_map/all_to_all | solution.py:115
  35.4 6.0 %copy-start.1 = (bf16[480,1280]{1,0:T(8,128)(2,1)S(1)}, bf16[480,1280]{1,0:T(8,128)(2,1)}, u32[]{:S(2)}) copy-start(bf16[480,1280]{1,0:T(8,128)(2,1)} %param.7) | copy-start | bytes 3686404
  35.4 34.5 %all-to-all-start.1 = ((bf16[8,2,2,16,1280]{4,3,2,1,0:T(8,128)(2,1)}), bf16[8,2,2,16,1280]{4,3,2,1,0:T(8,128)(2,1)S(1)}, u32[]{:S(2)}, u32[]{:S(2)}) async-start(bf16[8,2,2,16,1280]{4,3,2,1,0:T(8,128)(2,1)} %select_select_fusion), calls=%async_computation.1 | async-start | bytes 2621440 | tf_op jit(solution)/shard_map/all_to_all | solution.py:122
  39.2 10.5 %copy-start.4 = (f32[1280]{0:T(1024)S(1)}, f32[1280]{0:T(1024)}, u32[]{:S(2)}) copy-start(f32[1280]{0:T(1024)} %param.8) | copy-start | bytes 15364
  69.9 1.1 copy-start
  82.8 34.9 %all-to-all-start.2 = ((bf16[8,2,2,16,1280]{4,3,2,1,0:T(8,128)(2,1)}), bf16[8,2,2,16,1280]{4,3,2,1,0:T(8,128)(2,1)S(1)}, u32[]{:S(2)}, u32[]{:S(2)}) async-start(bf16[8,2,2,16,1280]{4,3,2,1,0:T(8,128)(2,1)} %get-tuple-element.5), calls=%async_computation.2 | async-start | bytes 2621440 | tf_op jit(solution)/shard_map/all_to_all | solution.py:135

commit v15 on v11

--- a/solution.py
+++ b/solution.py
@@ -15,7 +15,7 @@
 MASKED = -1e30
 
 
-HEADS_PER_STEP = 2
+HEADS_PER_STEP = 5
 
 
 def attend_kernel(tok_slot_ref, q_ref, kv_ref, g_ref, dq_ref, dkv_ref):

time: 141 us -> 141 us (level)
  no operation moved by 1% of the time
where the time goes in v15:
time: 141 us
  waiting for transfers between devices  64.8 us (46%)
  blocking collectives  36.4 us (26%)
  starting transfers between devices  13.2 us (9%)
  Pallas kernels  11.5 us (8%)
  local copies, waits for them, and re-layouts  7.47 us (5%)
  other arithmetic  5.36 us (4%)
  between operations  1.44 us (1%)
    all_to_all x1, waiting for transfers between devices, local(): pieces = lax.all_to_all(spread_grads, 'seq', 0, 0, tiled=True)  31 us
    all_to_all x1, blocking collectives, local(): lax.all_to_all(outgoing, 'seq', 0, 2, tiled=True)  21.3 us
    all_to_all x1, waiting for transfers between devices, local(): arrived = lax.all_to_all(wanted, 'seq', 0, 0, tiled=True)  18.8 us
    all_to_all x1, waiting for transfers between devices, local(): lax.all_to_all(spread, 'seq', 1, 0, tiled=True)  15 us
    pallas_call x1, Pallas kernels, attend(): pl.pallas_call(attend_kernel, grid=(feat_width // step_width,), in_specs=...  11.5 us
    psum x1, blocking collectives, local(): lax.psum(jnp.sum(own_key * own_key, axis=1), 'mp') / D + EPS  8.34 us
    psum x1, blocking collectives, local(): lax.psum(jnp.sum(query_wide * query_wide, axis=1) + after_first, 'mp')  6.77 us
    all_to_all x1, starting transfers between devices, local(): lax.all_to_all(spread, 'seq', 1, 0, tiled=True)  5.83 us
  transfers between devices with their start and end apart: 3, of which 3 were waited for; matrix products, arithmetic and copies ran while one was open for 4% of the time, Pallas kernels for 0%

profile of v15, /device:TPU:0, one launch (start us, length us, event | category | flops | bytes accessed | tf_op | source)
XLA Modules:
  0.0 140.5 jit_solution(13222560181030534333)
XLA Ops:
  0.6 1.2 slice_convert_fusion
  1.9 0.1 multiply_reduce_fusion
  2.1 8.3 %psum.14 = f32[128]{0:T(128)S(1)} all-reduce(f32[128]{0:T(128)S(1)} %multiply_reduce_fusion), channel_id=1, replica_groups=mesh['seq'=8,'mp'=4] {'mp'}, use_global_device_ids=true, to_apply=%region_5.6 | all-reduce | flops 128 | bytes 1024 | tf_op jit(solution)/shard_map/psum | solution.py:111
  10.5 0.1 multiply_convert_fusion
  10.7 0.9 pad_maximum_fusion
  11.5 5.8 %all-to-all-start = ((bf16[2,8,16,1280]{3,2,0,1:T(8,128)(2,1)}), bf16[2,8,16,1280]{3,2,0,1:T(8,128)(2,1)S(1)}, u32[]{:S(2)}, u32[]{:S(2)}) async-start(bf16[2,8,16,1280]{3,2,0,1:T(8,128)(2,1)} %pad_maximum_fusion), calls=%async_computation | async-start | bytes 1310720 | tf_op jit(solution)/shard_map/all_to_all | solution.py:115
  17.4 0.2 reduce-window.9
  17.6 0.1 convert_reduce_fusion.1
  17.9 0.7 gather_fusion
  18.5 15.0 %all-to-all-done = bf16[2,8,16,1280]{3,2,0,1:T(8,128)(2,1)S(1)} async-done(((bf16[2,8,16,1280]{3,2,0,1:T(8,128)(2,1)}), bf16[2,8,16,1280]{3,2,0,1:T(8,128)(2,1)S(1)}, u32[]{:S(2)}, u32[]{:S(2)}) %all-to-all-start) | async-done | bytes 655392 | tf_op jit(solution)/shard_map/all_to_all | solution.py:115
  33.5 1.7 %gather_fusion.1 = bf16[16,2,16,1280]{3,2,1,0:T(8,128)(2,1)} fusion(bf16[8,2,16,1280]{3,2,1,0:T(8,128)(2,1)S(1)} %bitcast.33, s32[1024]{0:T(1024)S(1)} %pad_clamp_fusion), kind=kCustom, calls=%fused_computation.1 | custom fusion | bytes 2621504 | tf_op jit(solution)/shard_map/jit(_take)/gather | solution.py:117
  35.2 3.8 %all-to-all-start.1 = ((bf16[8,2,2,16,1280]{4,3,2,1,0:T(8,128)(2,1)}), bf16[8,2,2,16,1280]{4,3,2,1,0:T(8,128)(2,1)S(1)}, u32[]{:S(2)}, u32[]{:S(2)}) async-start(bf16[8,2,2,16,1280]{4,3,2,1,0:T(8,128)(2,1)} %bitcast.15), calls=%async_computation.1 | async-start | bytes 2621440 | tf_op jit(solution)/shard_map/all_to_all | solution.py:118
  39.0 0.6 dynamic_slice.3
  39.6 0.1 convert_reduce_fusion
  39.7 0.6 add_subtract_fusion
  40.3 0.8 copy.26.tok_slot_ref
  41.2 0.3 fusion
  41.5 0.5 slice.16
  42.7 6.8 %psum.15 = f32[480]{0:T(512)S(1)} all-reduce(f32[480]{0:T(512)S(1)} %broadcast_add_fusion), channel_id=1, replica_groups=mesh['seq'=8,'mp'=4] {'mp'}, use_global_device_ids=true, to_apply=%region_6.7 | all-reduce | flops 480 | bytes 3840 | tf_op jit(solution)/shard_map/psum | solution.py:121
  49.5 1.4 %fusion.2.q_ref = bf16[480,1280]{1,0:T(8,128)(2,1)} fusion(bf16[480,1280]{1,0:T(8,128)(2,1)S(1)} %copy-done.2, f32[1280]{0:T(1024)S(1)} %copy-done.5, f32[480]{0:T(512)S(1)} %add_rsqrt_fusion), kind=kLoop, calls=%fused_computation.7 | loop fusion | flops 2457600 | bytes 2464640 | tf_op jit(solution)/shard_map/convert_element_type | solution.py:123
  50.9 18.8 %all-to-all-done.1.kv_ref = bf16[8,2,2,16,1280]{4,3,2,1,0:T(8,128)(2,1)S(1)} async-done(((bf16[8,2,2,16,1280]{4,3,2,1,0:T(8,128)(2,1)}), bf16[8,2,2,16,1280]{4,3,2,1,0:T(8,128)(2,1)S(1)}, u32[]{:S(2)}, u32[]{:S(2)}) %all-to-all-start.1) | async-done | bytes 1310752 | tf_op jit(solution)/shard_map/all_to_all | solution.py:118
  69.7 1.1 copy-done.1
  70.8 11.5 %shard_map.86 = (bf16[480,1280]{1,0:T(8,128)(2,1)}, bf16[8,2,2,16,1280]{4,3,2,1,0:T(8,128)(2,1)}) custom-call(s32[480,1]{1,0:T(8,128)} %copy.26.tok_slot_ref, bf16[480,1280]{1,0:T(8,128)(2,1)} %fusion.2.q_ref, bf16[8,2,2,16,1280]{4,3,2,1,0:T(8,128)(2,1)} %copy-done.1, bf16[480,1280]{1,0:T(8,128)(2,1)} %g_ref.1), custom_call_target="tpu_custom_call" | custom-call | tf_op jit(solution)/shard_map/pallas_call | solution.py:80
  82.3 3.6 %all-to-all-start.2 = ((bf16[8,2,2,16,1280]{4,3,2,1,0:T(8,128)(2,1)}), bf16[8,2,2,16,1280]{4,3,2,1,0:T(8,128)(2,1)S(1)}, u32[]{:S(2)}, u32[]{:S(2)}) async-start(bf16[8,2,2,16,1280]{4,3,2,1,0:T(8,128)(2,1)} %get-tuple-element.5), calls=%async_computation.2 | async-start | bytes 2621440 | tf_op jit(solution)/shard_map/all_to_all | solution.py:131
  86.1 0.1 fusion.5
  86.1 0.1 select_reduce_fusion
  86.2 31.0 %all-to-all-done.2 = bf16[8,2,2,16,1280]{4,3,2,1,0:T(8,128)(2,1)S(1)} async-done(((bf16[8,2,2,16,1280]{4,3,2,1,0:T(8,128)(2,1)}), bf16[8,2,2,16,1280]{4,3,2,1,0:T(8,128)(2,1)S(1)}, u32[]{:S(2)}, u32[]{:S(2)}) %all-to-all-start.2) | async-done | bytes 1310752 | tf_op jit(solution)/shard_map/all_to_all | solution.py:131
  117.2 0.6 reshape.172
  117.9 0.4 convolution_convert_fusion
  118.2 0.1 copy.28
  118.4 21.3 %all_to_all.43 = bf16[8,2,16,1280]{3,2,1,0:T(8,128)(2,1)S(1)} all-to-all(bf16[8,2,16,1280]{3,2,1,0:T(8,128)(2,1)S(1)} %copy.28), channel_id=1, replica_groups=mesh['seq'=8,'mp'=4] {'seq'}, dimensions={0} | all-to-all | bytes 1310720 | tf_op jit(solution)/shard_map/all_to_all | solution.py:139
  139.6 0.9 copy.29
  (30 shorter events, 0.6 us)
Async XLA Ops:
  0.6 1.3 copy-start.3
  0.6 9.9 %copy-start.4 = (f32[1280]{0:T(1024)S(1)}, f32[1280]{0:T(1024)}, u32[]{:S(2)}) copy-start(f32[1280]{0:T(1024)} %param.10) | copy-start | bytes 15364
  10.6 6.8 %copy-start.6 = (s32[3]{0:T(128)S(1)}, s32[3]{0:T(128)}, u32[]{:S(2)}) copy-start(s32[3]{0:T(128)} %param.12) | copy-start | bytes 40
  10.6 7.2 %copy-start = (s32[3]{0:T(128)S(1)}, s32[3]{0:T(128)}, u32[]{:S(2)}) copy-start(s32[3]{0:T(128)} %param.13) | copy-start | bytes 40
  11.5 22.0 %all-to-all-start = ((bf16[2,8,16,1280]{3,2,0,1:T(8,128)(2,1)}), bf16[2,8,16,1280]{3,2,0,1:T(8,128)(2,1)S(1)}, u32[]{:S(2)}, u32[]{:S(2)}) async-start(bf16[2,8,16,1280]{3,2,0,1:T(8,128)(2,1)} %pad_maximum_fusion), calls=%async_computation | async-start | bytes 1310720 | tf_op jit(solution)/shard_map/all_to_all | solution.py:115
  35.2 6.0 %copy-start.2 = (bf16[480,1280]{1,0:T(8,128)(2,1)S(1)}, bf16[480,1280]{1,0:T(8,128)(2,1)}, u32[]{:S(2)}) copy-start(bf16[480,1280]{1,0:T(8,128)(2,1)} %param.7) | copy-start | bytes 3686404
  35.2 34.5 %all-to-all-start.1 = ((bf16[8,2,2,16,1280]{4,3,2,1,0:T(8,128)(2,1)}), bf16[8,2,2,16,1280]{4,3,2,1,0:T(8,128)(2,1)S(1)}, u32[]{:S(2)}, u32[]{:S(2)}) async-start(bf16[8,2,2,16,1280]{4,3,2,1,0:T(8,128)(2,1)} %bitcast.15), calls=%async_computation.1 | async-start | bytes 2621440 | tf_op jit(solution)/shard_map/all_to_all | solution.py:118
  39.0 10.5 %copy-start.5 = (f32[1280]{0:T(1024)S(1)}, f32[1280]{0:T(1024)}, u32[]{:S(2)}) copy-start(f32[1280]{0:T(1024)} %param.8) | copy-start | bytes 15364
  69.7 1.1 copy-start.1
  82.3 34.9 %all-to-all-start.2 = ((bf16[8,2,2,16,1280]{4,3,2,1,0:T(8,128)(2,1)}), bf16[8,2,2,16,1280]{4,3,2,1,0:T(8,128)(2,1)S(1)}, u32[]{:S(2)}, u32[]{:S(2)}) async-start(bf16[8,2,2,16,1280]{4,3,2,1,0:T(8,128)(2,1)} %get-tuple-element.5), calls=%async_computation.2 | async-start | bytes 2621440 | tf_op jit(solution)/shard_map/all_to_all | solution.py:131
